TPU v7x, 256 devices: a whole 4x4x8 slice. The times are simulated.
256 devices in a mesh: dp: 8 (over z_hi, x), ctx: 32 (over y, z_lo, core).
Axes of the slice: x: 4, y: 4, z: 8 (z_hi: 2, z_lo: 4; z = z_hi * 4 + z_lo), core: 2. Of those that a mesh axis runs over, the one named last changes fastest.
Arguments:
- y_first: bfloat16 [8, 4096, 1024], P('dp', 'ctx'), may hold values from -6 to 6
- x_second: bfloat16 [8, 4096, 1024], P('dp', 'ctx'), may hold values from -40 to 40
- grad_first: bfloat16 [8, 4096, 1024], P('dp', 'ctx'), may hold values from -6 to 6
- grad_second: bfloat16 [8, 4096, 1024], P('dp', 'ctx'), may hold values from -6 to 6
- w_query: bfloat16 [1024, 1024], P('dp'), may hold values from -0.1875 to 0.1875
- w_key: bfloat16 [1024, 1024], P('dp'), may hold values from -0.1875 to 0.1875
- w_value: bfloat16 [1024, 1024], P('dp'), may hold values from -0.1875 to 0.1875
- w_out: bfloat16 [1024, 1024], P('dp'), may hold values from -0.1875 to 0.1875
Outputs:
- x_first: bfloat16 [8, 4096, 1024], P('dp', 'ctx')
- grad_x_second: bfloat16 [8, 4096, 1024], P('dp', 'ctx')
- grad_query: float32 [1024, 1024], P(('dp', 'ctx'))
- grad_out: float32 [1024, 1024], P(('dp', 'ctx'))
All inputs are finite; a program needn't handle non-finite values.
Results may differ from a plain program's by a relative error of at most 0.012.
The roundings to bfloat16 on the way count: a program that leaves them out, or rounds other values in their place, can miss the bound.
Values may be sent and summed in bfloat16 or wider, within the bound.
No kernel may reach another device: no remote copies, remote signals or barrier semaphores. Data moves between devices by JAX's collectives and lax.ppermute only.
A program may use at most 128 MiB of HBM per device.

v0:
```python
import jax
import jax.numpy as jnp
from jax import lax
from jax.sharding import PartitionSpec as P

HEADS = 8
HEAD_DIM = 128


def prefix(shard, axis, combine, identity):
    size, here = (lax.axis_size(axis), lax.axis_index(axis))
    everything = lax.all_gather(shard, axis)
    start = jnp.broadcast_to(jnp.asarray(identity, shard.dtype), shard.shape)

    def turn(k, before):
        reached = k < here
        new = combine(before, everything[k])
        return jnp.where(reached, new, before)

    return lax.fori_loop(0, size, turn, start)


def carried_in(shard, axis, join, neutral):
    count = lax.axis_size(axis)
    place = lax.axis_index(axis)
    ahead = count - 1 - place
    gathered = lax.all_gather(shard.astype(jnp.bfloat16), axis)
    state = jnp.zeros_like(shard) + jnp.asarray(neutral, shard.dtype)

    def one(turn, state):
        source = count - 1 - turn
        return join(state, lax.dynamic_index_in_dim(gathered, source, 0, False).astype(shard.dtype))

    return lax.fori_loop(0, ahead, one, state)


def add_states(earlier, later):
    return earlier + later


def weight_grads(pairs, factor):
    width = pairs[0][0].shape[1]
    blocks = []
    for left, right in pairs:
        made = lax.dot_general(
            left, right, (((0,), (0,)), ((), ())), preferred_element_type=jnp.float32
        )
        blocks.append(factor * made)
    share = lax.psum_scatter(
        jnp.concatenate(blocks, 1), ("dp", "ctx"), scatter_dimension=0, tiled=True
    )
    return tuple((share[:, index * width : (index + 1) * width] for index in range(len(pairs))))


def on_device(y_first, x_second, grad_first, grad_second, w_query, w_key, w_value, w_out):
    batch, tokens_here, width = y_first.shape
    factor = float(batch * tokens_here * lax.axis_size("dp") * lax.axis_size("ctx")) ** (-0.5)
    full_query, full_key, full_value = (
        lax.all_gather(w_query, "dp", axis=0, tiled=True),
        lax.all_gather(w_key, "dp", axis=0, tiled=True),
        lax.all_gather(w_value, "dp", axis=0, tiled=True),
    )
    full_out = lax.all_gather(w_out, "dp", axis=0, tiled=True)
    second_wide = x_second.astype(jnp.float32)
    inv_rms = lax.rsqrt(jnp.mean(second_wide * second_wide, -1, keepdims=True) + 1e-06)
    normed_wide = second_wide * inv_rms
    normed = normed_wide.astype(jnp.bfloat16)

    def project(weight):
        made = jnp.einsum("btd,df->btf", normed, weight, preferred_element_type=jnp.float32)
        return made.astype(jnp.bfloat16).reshape(batch, tokens_here, HEADS, HEAD_DIM)

    queries = project(full_query)
    key_rows = project(full_key)
    values = project(full_value)
    local_state = jnp.einsum(
        "bthe,bthf->bhef", key_rows, values, preferred_element_type=jnp.float32
    )
    zeros_state = jnp.zeros_like(local_state)
    before = prefix(local_state, "ctx", add_states, zeros_state).astype(jnp.bfloat16)
    causal = jnp.tril(jnp.ones((tokens_here, tokens_here), dtype=bool))
    scores = jnp.einsum("bthe,bshe->bhts", queries, key_rows, preferred_element_type=jnp.float32)
    scores = jnp.where(causal[None, None], scores, 0.0).astype(jnp.bfloat16)
    mixed = jnp.einsum("bhts,bshf->bthf", scores, values, preferred_element_type=jnp.float32)
    mixed = mixed + jnp.einsum(
        "bthe,bhef->bthf", queries, before, preferred_element_type=jnp.float32
    )
    inv_head = lax.rsqrt(jnp.mean(mixed * mixed, -1, keepdims=True) + 1e-06)
    unit = mixed * inv_head
    attn_out = unit.astype(jnp.bfloat16).reshape(batch, tokens_here, width)
    attended = jnp.einsum("btf,fd->btd", attn_out, full_out, preferred_element_type=jnp.float32)
    x_first = (y_first.astype(jnp.float32) - attended).astype(jnp.bfloat16)
    grad_unit = jnp.einsum("btd,fd->btf", grad_first, full_out, preferred_element_type=jnp.float32)
    grad_unit = grad_unit.reshape(batch, tokens_here, HEADS, HEAD_DIM)
    grad_mixed = inv_head * (grad_unit - unit * jnp.mean(grad_unit * unit, -1, keepdims=True))
    grad_mixed = grad_mixed.astype(jnp.bfloat16)
    score_grad = jnp.einsum(
        "bthf,bshf->bhts", grad_mixed, values, preferred_element_type=jnp.float32
    )
    score_grad = jnp.where(causal[None, None], score_grad, 0.0).astype(jnp.bfloat16)
    grad_local = jnp.einsum(
        "bthe,bthf->bhef", queries, grad_mixed, preferred_element_type=jnp.float32
    )
    after_state = carried_in(grad_local, "ctx", add_states, zeros_state).astype(jnp.bfloat16)
    query_grad = jnp.einsum(
        "bhts,bshe->bthe", score_grad, key_rows, preferred_element_type=jnp.float32
    )
    query_grad = query_grad + jnp.einsum(
        "bthf,bhef->bthe", grad_mixed, before, preferred_element_type=jnp.float32
    )
    key_grad = jnp.einsum(
        "bhts,bthe->bshe", score_grad, queries, preferred_element_type=jnp.float32
    )
    key_grad = key_grad + jnp.einsum(
        "bshf,bhef->bshe", values, after_state, preferred_element_type=jnp.float32
    )
    value_grad = jnp.einsum(
        "bhts,bthf->bshf", scores, grad_mixed, preferred_element_type=jnp.float32
    )
    value_grad = value_grad + jnp.einsum(
        "bshe,bhef->bshf", key_rows, after_state, preferred_element_type=jnp.float32
    )
    query_grad = query_grad.astype(jnp.bfloat16).reshape(batch, tokens_here, width)
    key_grad = key_grad.astype(jnp.bfloat16).reshape(batch, tokens_here, width)
    value_grad = value_grad.astype(jnp.bfloat16).reshape(batch, tokens_here, width)
    grad_normed = jnp.einsum(
        "btf,df->btd", query_grad, full_query, preferred_element_type=jnp.float32
    )
    grad_normed = grad_normed + jnp.einsum(
        "btf,df->btd", key_grad, full_key, preferred_element_type=jnp.float32
    )
    grad_normed = grad_normed + jnp.einsum(
        "btf,df->btd", value_grad, full_value, preferred_element_type=jnp.float32
    )
    back = inv_rms * (
        grad_normed - normed_wide * jnp.mean(grad_normed * normed_wide, -1, keepdims=True)
    )
    grad_x_second = (grad_second.astype(jnp.float32) + back).astype(jnp.bfloat16)
    pairs = (
        (normed.reshape(-1, width), query_grad.reshape(-1, width)),
        (attn_out.reshape(-1, width), grad_first.reshape(-1, width)),
    )
    grad_query, grad_out = weight_grads(pairs, factor)
    return (x_first, grad_x_second, grad_query, grad_out)


def solution(mesh):
    placed = (
        P("dp", "ctx", None),
        P("dp", "ctx", None),
        P("dp", "ctx", None),
        P("dp", "ctx", None),
        P("dp", None),
        P("dp", None),
        P("dp", None),
        P("dp", None),
    )
    return jax.shard_map(
        on_device,
        mesh=mesh,
        in_specs=placed,
        out_specs=(
            P("dp", "ctx", None),
            P("dp", "ctx", None),
            P(("dp", "ctx"), None),
            P(("dp", "ctx"), None),
        ),
        check_vma=False,
    )
```

profile of v0, /device:TPU:1, one launch (start us, length us, event | category | flops | bytes accessed | tf_op | source)
XLA Modules:
  0.0 815.4 jit_solution(6239691303570350264)
XLA Ops:
  10.6 77.0 %all-gather.13.cloned.1.call-done = bf16[1024,1024]{1,0:T(8,128)(2,1)} async-done(((bf16[128,1024]{1,0:T(8,128)(2,1)}), bf16[1024,1024]{1,0:T(8,128)(2,1)}) %all-gather.13.cloned.1.call-update) | async-done | bytes 2097168 | tf_op jit(solution)/shard_map/all_gather | solution.py:60
  87.5 2.2 convolution_convert_fusion.1
  90.0 71.8 %all-gather.9.cloned.1.call-done = bf16[1024,1024]{1,0:T(8,128)(2,1)} async-done(((bf16[128,1024]{1,0:T(8,128)(2,1)}), bf16[1024,1024]{1,0:T(8,128)(2,1)}) %all-gather.9.cloned.1.call-update) | async-done | bytes 2097168 | tf_op jit(solution)/shard_map/all_gather | solution.py:61
  161.8 2.1 fusion.9
  165.6 70.5 %all-gather.11.cloned.1.call-done = bf16[1024,1024]{1,0:T(8,128)(2,1)} async-done(((bf16[128,1024]{1,0:T(8,128)(2,1)}), bf16[1024,1024]{1,0:T(8,128)(2,1)}) %all-gather.11.cloned.1.call-update) | async-done | bytes 2097168 | tf_op jit(solution)/shard_map/all_gather | solution.py:59
  236.1 2.1 convolution_convert_fusion.2
  239.1 97.4 %all-gather.17.cloned.1.call-done = f32[256,128,128]{2,1,0:T(8,128)} async-done(((f32[8,128,128]{2,1,0:T(8,128)}), f32[256,128,128]{2,1,0:T(8,128)}) %all-gather.17.cloned.1.call-update) | async-done | bytes 16777232 | tf_op jit(solution)/shard_map/all_gather | solution.py:12
  336.5 40.0 %while.27 = (s32[]{:T(128)}, f32[1,8,128,128]{3,2,1,0:T(8,128)S(1)}, s32[]{:T(128)}, f32[32,1,8,128,128]{4,3,2,1,0:T(8,128)}, s32[]{:T(128)}, /*index=5*/s32[]{:T(128)}) while((s32[]{:T(128)}, f32[1,8,128,128]{3,2,1,0:T(8,128)S(1)}, s32[]{:T(128)}, f32[32,1,8,128,128]{4,3,2,1,0:T(8,128)}, s32[]{:T(128)}, /*index=5*/s32[]{:T(128)}) %tuple.88), condition=%wide.region_2.3_spmd.clone, body=%wide.region_1.2_spmd.clone.sunk | while | flops 393220 | bytes 1572965 | solution.py:20
  337.7 1.2 add_select_fusion.2
  339.0 1.2 add_select_fusion.2
  340.2 1.2 add_select_fusion.2
  341.5 1.2 add_select_fusion.2
  342.7 1.2 add_select_fusion.2
  344.0 1.2 add_select_fusion.2
  345.2 1.2 add_select_fusion.2
  346.5 1.2 add_select_fusion.2
  347.7 1.2 add_select_fusion.2
  350.2 1.2 add_select_fusion.2
  351.5 1.2 add_select_fusion.2
  352.8 1.2 add_select_fusion.2
  354.0 1.2 add_select_fusion.2
  361.5 1.2 add_select_fusion.2
  369.0 1.2 add_select_fusion.2
  376.8 35.7 %all-gather.15.cloned.1.call-done = bf16[1024,1024]{1,0:T(8,128)(2,1)} async-done(((bf16[128,1024]{1,0:T(8,128)(2,1)}), bf16[1024,1024]{1,0:T(8,128)(2,1)}) %all-gather.15.cloned.1.call-update) | async-done | bytes 2097168 | tf_op jit(solution)/shard_map/all_gather | solution.py:63
  412.5 2.3 multiply_reduce_fusion
  418.1 4.1 pad_maximum_fusion
  424.4 2.1 fusion.53
  426.5 1.8 fusion.51
  429.5 269.7 %all-reduce.3.cloned.1.call-done = f32[1024,2048]{0,1:T(8,128)} async-done(((f32[1024,2048]{0,1:T(8,128)}), f32[1024,2048]{0,1:T(8,128)}) %all-reduce.3.cloned.1.call-update) | async-done | bytes 8388624
  699.2 1.5 fusion.49
  702.3 68.8 %all-gather.19.cloned.1.call-done = bf16[256,128,128]{2,1,0:T(8,128)(2,1)} async-done(((bf16[8,128,128]{2,1,0:T(8,128)(2,1)}), bf16[256,128,128]{2,1,0:T(8,128)(2,1)}) %all-gather.19.cloned.1.call-update) | async-done | bytes 8388624 | tf_op jit(solution)/shard_map/all_gather | solution.py:27
  771.2 32.9 %while.26 = (s32[]{:T(128)}, f32[1,8,128,128]{3,2,1,0:T(8,128)S(1)}, s32[]{:T(128)}, bf16[32,1,8,128,128]{4,3,2,1,0:T(8,128)(2,1)}, s32[]{:T(128)}, /*index=5*/s32[]{:T(128)}, s32[]{:T(128)}, s32[]{:T(128)}) while((s32[]{:T(128)}, f32[1,8,128,128]{3,2,1,0:T(8,128)S(1)}, s32[]{:T(128)}, bf16[32,1,8,128,128]{4,3,2,1,0:T(8,128)(2,1)}, s32[]{:T(128)}, ...), condition=%wide.region_6.7_spmd, body=%wide.region_5.6_spmd.sunk | while | flops 262150 | bytes 1310863 | solution.py:34
  (130 shorter events, 71.9 us)
Async XLA Ops:
  7.2 405.4 %copy-start = (bf16[1,128,1024]{2,1,0:T(8,128)(2,1)S(1)}, bf16[1,128,1024]{2,1,0:T(8,128)(2,1)}, u32[]{:S(2)}) copy-start(bf16[1,128,1024]{2,1,0:T(8,128)(2,1)} %param.14) | copy-start | bytes 786436
  7.2 80.4 %all-gather.13.cloned.1.call-start = ((), (), s32[]{:S(2)}) async-start(), calls=%async_computation.2 | async-start | bytes 2359296 | tf_op jit(solution)/shard_map/all_gather | solution.py:60
  7.9 153.9 %all-gather.9.cloned.1.call-start = ((), (), s32[]{:S(2)}) async-start(), calls=%async_computation | async-start | bytes 2359296 | tf_op jit(solution)/shard_map/all_gather | solution.py:61
  8.7 153.2 %copy-start.2 = (bf16[1,128,1024]{2,1,0:T(8,128)(2,1)S(1)}, bf16[1,128,1024]{2,1,0:T(8,128)(2,1)}, u32[]{:S(2)}) copy-start(bf16[1,128,1024]{2,1,0:T(8,128)(2,1)} %param.13) | copy-start | bytes 786436
  8.7 227.4 %all-gather.11.cloned.1.call-start = ((), (), s32[]{:S(2)}) async-start(), calls=%async_computation.1 | async-start | bytes 2359296 | tf_op jit(solution)/shard_map/all_gather | solution.py:59
  9.4 327.1 %all-gather.17.cloned.1.call-start = ((), (), s32[]{:S(2)}) async-start(), calls=%async_computation.4 | async-start | bytes 17301504 | tf_op jit(solution)/shard_map/all_gather | solution.py:12
  89.7 148.7 %copy-start.10 = (bf16[128,1024]{1,0:T(8,128)(2,1)}, bf16[128,1024]{1,0:T(8,128)(2,1)S(1)}, u32[]{:S(2)}) copy-start(bf16[128,1024]{1,0:T(8,128)(2,1)S(1)} %convolution_convert_fusion.1) | copy-start | bytes 786436
  165.0 247.6 %all-gather.15.cloned.1.call-start = ((), (), s32[]{:S(2)}) async-start(), calls=%async_computation.3 | async-start | bytes 2359296 | tf_op jit(solution)/shard_map/all_gather | solution.py:63
  165.6 533.6 %all-reduce.3.cloned.1.call-start = ((), (), s32[]{:S(2)}) async-start(), calls=%async_computation.6 | async-start | bytes 16777216
  238.7 97.8 %copy-start.14 = (bf16[8,128,128]{2,1,0:T(8,128)(2,1)}, bf16[8,128,128]{2,1,0:T(8,128)(2,1)S(1)}, u32[]{:S(2)}) copy-start(bf16[8,128,128]{2,1,0:T(8,128)(2,1)S(1)} %fusion.3) | copy-start | bytes 786436
  415.0 2.3 copy-start.7
  415.4 0.7 copy-start.15
  416.6 5.7 copy-start.9
  422.2 1.1 copy-start.16
  422.3 4.3 copy-start.5
  422.3 348.9 %all-gather.19.cloned.1.call-start = ((), (), s32[]{:S(2)}) async-start(), calls=%async_computation.5 | async-start | bytes 8650752 | tf_op jit(solution)/shard_map/all_gather | solution.py:27
  424.4 3.9 copy-start.6
  424.4 3.9 copy-start.8
  424.4 3.9 copy-start.18
  771.2 32.9 %copy-start.12 = (f32[8,128,128]{2,1,0:T(8,128)S(1)}, f32[8,128,128]{2,1,0:T(8,128)}, u32[]{:S(2)}) copy-start(f32[8,128,128]{2,1,0:T(8,128)} %fusion.52) | copy-start | bytes 1572868
  771.2 33.2 %copy-start.11 = (bf16[128,1024]{1,0:T(8,128)(2,1)S(1)}, bf16[128,1024]{1,0:T(8,128)(2,1)}, u32[]{:S(2)}) copy-start(bf16[128,1024]{1,0:T(8,128)(2,1)} %copy-done.10) | copy-start | bytes 786436
  771.2 33.2 %copy-start.13 = (f32[8,128,128]{2,1,0:T(8,128)S(1)}, f32[8,128,128]{2,1,0:T(8,128)}, u32[]{:S(2)}) copy-start(f32[8,128,128]{2,1,0:T(8,128)} %fusion.53) | copy-start | bytes 1572868
  804.1 1.6 copy-start.3
  804.8 1.8 copy-start.4
  806.5 1.0 copy-start.17
  806.6 2.0 copy-start.1
Sparse Core Ops, SparseCore 0:
  10.6 76.8 all-gather.12
  90.2 71.6 all-gather.8
  164.5 71.6 all-gather.10
  237.8 98.6 all-gather.16
  339.0 73.5 all-gather.14
  422.4 276.7 all-reduce.2
  701.1 70.0 all-gather.18
where the time goes:
time: 818 us; the launch traced here: 815 us
  waiting for transfers between devices  694 us (85%)
  other arithmetic  77.8 us (10%)
  matrix products  22.5 us (3%)
  between operations  14.5 us (2%)
    unnamed x8, waiting for transfers between devices  272 us
    all_gather x1, waiting for transfers between devices, prefix(): everything = lax.all_gather(shard, axis)  97.4 us
    all_gather x1, waiting for transfers between devices, on_device(): lax.all_gather(w_key, 'dp', axis=0, tiled=True)  77 us
    all_gather x1, waiting for transfers between devices, on_device(): lax.all_gather(w_value, 'dp', axis=0, tiled=True)  71.8 us
    all_gather x1, waiting for transfers between devices, on_device(): lax.all_gather(w_query, 'dp', axis=0, tiled=True)  70.5 us
    all_gather x1, waiting for transfers between devices, carried_in(): gathered = lax.all_gather(shard.astype(jnp.bfloat16), axis)  68.8 us
    select_n x32, other arithmetic, turn(): return jnp.where(reached, new, before)  39.3 us
    all_gather x1, waiting for transfers between devices, on_device(): full_out = lax.all_gather(w_out, 'dp', axis=0, tiled=True)  35.7 us
  transfers between devices with their start and end apart: 7, of which 7 were waited for; matrix products, arithmetic and copies ran while one was open for 7% of the time, Pallas kernels for 0%

commit v1 on v0

--- a/solution.py
+++ b/solution.py
@@ -7,60 +7,52 @@
 HEAD_DIM = 128
 
 
-def prefix(shard, axis, combine, identity):
-    size, here = (lax.axis_size(axis), lax.axis_index(axis))
-    everything = lax.all_gather(shard, axis)
-    start = jnp.broadcast_to(jnp.asarray(identity, shard.dtype), shard.shape)
-
-    def turn(k, before):
-        reached = k < here
-        new = combine(before, everything[k])
-        return jnp.where(reached, new, before)
-
-    return lax.fori_loop(0, size, turn, start)
+def scan_sum(shard, axis, reverse):
+    count = lax.axis_size(axis)
+    total = shard
+    step = 1
+    while step < count:
+        if reverse:
+            pairs = [(source, source - step) for source in range(step, count)]
+        else:
+            pairs = [(source, source + step) for source in range(count - step)]
+        total = total + lax.ppermute(total, axis, pairs)
+        step *= 2
+    return total
 
 
-def carried_in(shard, axis, join, neutral):
-    count = lax.axis_size(axis)
-    place = lax.axis_index(axis)
-    ahead = count - 1 - place
-    gathered = lax.all_gather(shard.astype(jnp.bfloat16), axis)
-    state = jnp.zeros_like(shard) + jnp.asarray(neutral, shard.dtype)
-
-    def one(turn, state):
-        source = count - 1 - turn
-        return join(state, lax.dynamic_index_in_dim(gathered, source, 0, False).astype(shard.dtype))
-
-    return lax.fori_loop(0, ahead, one, state)
+def gather_rows(weights, piece):
+    place = lax.axis_index("ctx")
+    parts = [lax.dynamic_slice_in_dim(weight, place * piece, piece, 0) for weight in weights]
+    joined = jnp.concatenate(parts, 0)
+    gathered = lax.all_gather(joined, ("dp", "ctx"), axis=0, tiled=True)
+    gathered = gathered.reshape(-1, len(weights), piece, joined.shape[1])
+    return tuple(
+        gathered[:, index].reshape(-1, joined.shape[1]) for index in range(len(weights))
+    )
 
 
-def add_states(earlier, later):
-    return earlier + later
-
-
-def weight_grads(pairs, factor):
+def weight_grads(pairs, factor, owners):
     width = pairs[0][0].shape[1]
     blocks = []
     for left, right in pairs:
         made = lax.dot_general(
             left, right, (((0,), (0,)), ((), ())), preferred_element_type=jnp.float32
         )
-        blocks.append(factor * made)
-    share = lax.psum_scatter(
-        jnp.concatenate(blocks, 1), ("dp", "ctx"), scatter_dimension=0, tiled=True
-    )
-    return tuple((share[:, index * width : (index + 1) * width] for index in range(len(pairs))))
+        blocks.append((factor * made).reshape(owners, -1, width))
+    rows = blocks[0].shape[1]
+    stacked = jnp.concatenate(blocks, 1).reshape(-1, width)
+    share = lax.psum_scatter(stacked, ("dp", "ctx"), scatter_dimension=0, tiled=True)
+    return tuple(share[index * rows : (index + 1) * rows] for index in range(len(pairs)))
 
 
 def on_device(y_first, x_second, grad_first, grad_second, w_query, w_key, w_value, w_out):
     batch, tokens_here, width = y_first.shape
-    factor = float(batch * tokens_here * lax.axis_size("dp") * lax.axis_size("ctx")) ** (-0.5)
-    full_query, full_key, full_value = (
-        lax.all_gather(w_query, "dp", axis=0, tiled=True),
-        lax.all_gather(w_key, "dp", axis=0, tiled=True),
-        lax.all_gather(w_value, "dp", axis=0, tiled=True),
-    )
-    full_out = lax.all_gather(w_out, "dp", axis=0, tiled=True)
+    owners = lax.axis_size("dp") * lax.axis_size("ctx")
+    factor = float(batch * tokens_here * owners) ** (-0.5)
+    piece = w_query.shape[0] // lax.axis_size("ctx")
+    full_query, full_key, full_value = gather_rows((w_query, w_key, w_value), piece)
+    (full_out,) = gather_rows((w_out,), piece)
     second_wide = x_second.astype(jnp.float32)
     inv_rms = lax.rsqrt(jnp.mean(second_wide * second_wide, -1, keepdims=True) + 1e-06)
     normed_wide = second_wide * inv_rms
@@ -76,8 +68,7 @@
     local_state = jnp.einsum(
         "bthe,bthf->bhef", key_rows, values, preferred_element_type=jnp.float32
     )
-    zeros_state = jnp.zeros_like(local_state)
-    before = prefix(local_state, "ctx", add_states, zeros_state).astype(jnp.bfloat16)
+    before = (scan_sum(local_state, "ctx", False) - local_state).astype(jnp.bfloat16)
     causal = jnp.tril(jnp.ones((tokens_here, tokens_here), dtype=bool))
     scores = jnp.einsum("bthe,bshe->bhts", queries, key_rows, preferred_element_type=jnp.float32)
     scores = jnp.where(causal[None, None], scores, 0.0).astype(jnp.bfloat16)
@@ -101,7 +92,7 @@
     grad_local = jnp.einsum(
         "bthe,bthf->bhef", queries, grad_mixed, preferred_element_type=jnp.float32
     )
-    after_state = carried_in(grad_local, "ctx", add_states, zeros_state).astype(jnp.bfloat16)
+    after_state = (scan_sum(grad_local, "ctx", True) - grad_local).astype(jnp.bfloat16)
     query_grad = jnp.einsum(
         "bhts,bshe->bthe", score_grad, key_rows, preferred_element_type=jnp.float32
     )
@@ -140,7 +131,7 @@
         (normed.reshape(-1, width), query_grad.reshape(-1, width)),
         (attn_out.reshape(-1, width), grad_first.reshape(-1, width)),
     )
-    grad_query, grad_out = weight_grads(pairs, factor)
+    grad_query, grad_out = weight_grads(pairs, factor, owners)
     return (x_first, grad_x_second, grad_query, grad_out)
 
 

time: 818 us -> 2220 us (2.71)
  waiting for transfers between devices: 694 us -> 2060 us
  other arithmetic: 77.8 us -> 17.1 us
  local copies, waits for them, and re-layouts: 5.3 us -> 53 us
  starting transfers between devices: 0.27 us -> 44.5 us
    reduce_scatter x0 -> x1, waiting for transfers between devices: none -> 1190 us  [weight_grads(): lax.psum_scatter(stacked, ('dp', 'ctx'), scatter_dimension=0, tiled=True)]
    all_gather x6 -> x2, waiting for transfers between devices: 421 us -> 760 us  [gather_rows(): gathered = lax.all_gather(joined, ('dp', 'ctx'), axis=0, tiled=True)]
    unnamed x8 -> x3, waiting for transfers between devices: 272 us -> 0.05 us
    ppermute x0 -> x10, waiting for transfers between devices: none -> 104 us  [scan_sum(): total = total + lax.ppermute(total, axis, pairs)]
    ppermute x0 -> x10, starting transfers between devices: none -> 44.4 us  [scan_sum(): total = total + lax.ppermute(total, axis, pairs)]
    select_n x32 -> x0, other arithmetic: 39.3 us -> none  [turn(): return jnp.where(reached, new, before)]
    add x30 -> x8, other arithmetic: 32.2 us -> 3.26 us  [scan_sum(): total = total + lax.ppermute(total, axis, pairs)]
  transfers between devices with their start and end apart: 7 -> 13, of which waited for: 7 -> 12; matrix products, arithmetic and copies ran while one was open for 7% -> 3% of each run, Pallas kernels for 0% -> 0%
where the time goes in v1:
time: 2220 us; the launch traced here: 2210 us
  waiting for transfers between devices  2060 us (93%)
  local copies, waits for them, and re-layouts  53 us (2%)
  starting transfers between devices  44.5 us (2%)
  matrix products  24.2 us (1%)
    reduce_scatter x1, waiting for transfers between devices, weight_grads(): lax.psum_scatter(stacked, ('dp', 'ctx'), scatter_dimension=0, tiled=True)  1190 us
    all_gather x2, waiting for transfers between devices, gather_rows(): gathered = lax.all_gather(joined, ('dp', 'ctx'), axis=0, tiled=True)  760 us
    ppermute x10, waiting for transfers between devices, scan_sum(): total = total + lax.ppermute(total, axis, pairs)  104 us
  transfers between devices with their start and end apart: 13, of which 12 were waited for; matrix products, arithmetic and copies ran while one was open for 3% of the time, Pallas kernels for 0%

profile of v1, /device:TPU:1, one launch (start us, length us, event | category | flops | bytes accessed | tf_op | source)
XLA Modules:
  0.0 2213.0 jit_solution(11344175683100216950)
XLA Ops:
  11.9 420.8 %all-gather.5.cloned.1.call-done = bf16[256,12,1024]{2,1,0:T(8,128)(2,1)} async-done(((bf16[1,12,1024]{2,1,0:T(8,128)(2,1)}), bf16[256,12,1024]{2,1,0:T(8,128)(2,1)}) %all-gather.5.cloned.1.call-update) | async-done | bytes 6291472 | tf_op jit(solution)/shard_map/all_gather | solution.py:28
  432.7 6.9 copy.67
  439.6 3.4 fusion.43
  443.0 2.9 copy.68
  446.0 2.5 reshape_squeeze.9
  448.5 4.5 copy.70
  453.0 4.0 reshape_squeeze.11
  460.9 5.3 collective-permute-start
  466.2 6.2 collective-permute-done
  472.5 3.1 collective-permute-start.1
  475.6 10.1 collective-permute-done.1
  485.7 3.5 collective-permute-start.2
  489.3 8.5 collective-permute-done.2
  498.6 19.2 collective-permute-start.3
  517.8 339.7 %all-gather.7.cloned.1.call-done = bf16[256,4,1024]{2,1,0:T(4,128)(2,1)} async-done(((bf16[1,4,1024]{2,1,0:T(4,128)(2,1)}), bf16[256,4,1024]{2,1,0:T(4,128)(2,1)}) %all-gather.7.cloned.1.call-update) | async-done | bytes 2097168 | tf_op jit(solution)/shard_map/all_gather | solution.py:28
  857.5 4.0 reshape.224
  861.5 3.3 fusion.31
  864.8 3.0 copy.69
  867.8 4.0 reshape_squeeze.10
  875.9 2.8 convolution_convert_fusion.1
  888.1 2.8 convolution_multiply_fusion.1
  890.9 5.2 reshape.218
  896.1 3.6 convolution_multiply_fusion
  899.7 5.2 reshape.219
  904.9 8.9 maximum_bitcast_fusion
  914.1 5.7 collective-permute-start.5
  919.8 7.4 collective-permute-done.5
  928.7 14.6 collective-permute-done.6
  944.7 28.7 %collective-permute-done.7 = f32[1,8,128,128]{3,2,1,0:T(8,128)S(1)} collective-permute-done((f32[1,8,128,128]{3,2,1,0:T(8,128)S(1)}, f32[1,8,128,128]{3,2,1,0:T(8,128)S(1)}, u32[]{:S(2)}, u32[]{:S(2)}) %collective-permute-start.7) | collective-permute-done | bytes 524320 | tf_op jit(solution)/shard_map/ppermute | solution.py:19
  975.9 12.0 collective-permute-done.8
  991.0 15.5 collective-permute-done.9
  1010.0 1195.0 %reduce-scatter.2.cloned.1.call-done = f32[8,1024]{1,0:T(8,128)} async-done(((f32[2048,1024]{1,0:T(8,128)}), f32[8,1024]{1,0:T(8,128)}) %reduce-scatter.2.cloned.1.call-update) | async-done | bytes 32784 | tf_op jit(solution)/shard_map/reduce_scatter | solution.py:45
  (102 shorter events, 36.5 us)
Async XLA Ops:
  7.2 854.3 %copy-start = (bf16[1,128,1024]{2,1,0:T(8,128)(2,1)S(1)}, bf16[1,128,1024]{2,1,0:T(8,128)(2,1)}, u32[]{:S(2)}) copy-start(bf16[1,128,1024]{2,1,0:T(8,128)(2,1)} %param.10) | copy-start | bytes 786436
  7.2 425.6 %all-gather.5.cloned.1.call-start = ((), (), s32[]{:S(2)}) async-start(), calls=%async_computation.2 | async-start | bytes 8421376 | tf_op jit(solution)/shard_map/all_gather | solution.py:28
  9.4 848.1 %all-gather.7.cloned.1.call-start = ((), (), s32[]{:S(2)}) async-start(), calls=%async_computation.3 | async-start | bytes 2105344 | tf_op jit(solution)/shard_map/all_gather | solution.py:28
  10.8 2194.2 %reduce-scatter.2.cloned.1.call-start = ((), (), s32[]{:S(2)}) async-start(), calls=%async_computation.1 | async-start | bytes 8421376 | tf_op jit(solution)/shard_map/reduce_scatter | solution.py:45
  453.0 4.0 copy-start.4
  460.1 12.3 copy-start.13
  460.7 25.0 %copy-start.7 = (bf16[16,8,8,128]{3,2,1,0:T(8,128)(2,1)}, bf16[16,8,8,128]{3,2,1,0:T(8,128)(2,1)S(1)}, u32[]{:S(2)}) copy-start(bf16[16,8,8,128]{3,2,1,0:T(8,128)(2,1)S(1)} %fusion.9) | copy-start | bytes 786436
  460.9 11.5 collective-permute-start
  472.5 13.2 collective-permute-start.1
  485.7 12.1 collective-permute-start.2
  498.6 373.1 %collective-permute-start.3 = (f32[1,8,128,128]{3,2,1,0:T(8,128)}, f32[1,8,128,128]{3,2,1,0:T(8,128)}, u32[]{:S(2)}, u32[]{:S(2)}) collective-permute-start(f32[1,8,128,128]{3,2,1,0:T(8,128)} %add.102), channel_id=1, source_target_pairs={{0,8},{1,9},{2,10},{3,11},{4,12},{5,13},{6,14},{7,15},{8,16},{9,17... | collective-permute-start | bytes 1572872 | tf_op jit(solution)/shard_map/ppermute | solution.py:19
  861.5 3.3 copy-start.5
  873.8 10.0 collective-permute-start.4
  881.1 1.4 copy-start.16
  881.1 4.4 copy-start.6
  885.1 1.3 copy-start.8
  885.4 1.3 copy-start.14
  914.1 60.7 %copy-start.19 = (bf16[8,128,128]{2,1,0:T(8,128)(2,1)S(1)}, bf16[8,128,128]{2,1,0:T(8,128)(2,1)}, u32[]{:S(2)}) copy-start(bf16[8,128,128]{2,1,0:T(8,128)(2,1)} %copy-done.18) | copy-start | bytes 786436
  914.1 13.1 collective-permute-start.5
  927.3 47.8 %copy-start.2 = (bf16[1024,1024]{1,0:T(8,128)(2,1)S(1)}, bf16[1024,1024]{1,0:T(8,128)(2,1)}, u32[]{:S(2)}) copy-start(bf16[1024,1024]{1,0:T(8,128)(2,1)} %reshape_squeeze.10) | copy-start | bytes 6291460
  927.3 47.8 %copy-start.10 = (bf16[8,128,128]{2,1,0:T(8,128)(2,1)S(1)}, bf16[8,128,128]{2,1,0:T(8,128)(2,1)}, u32[]{:S(2)}) copy-start(bf16[8,128,128]{2,1,0:T(8,128)(2,1)} %copy-done.9) | copy-start | bytes 786436
  927.3 16.1 collective-permute-start.6
  943.4 30.0 %collective-permute-start.7 = (f32[1,8,128,128]{3,2,1,0:T(8,128)S(1)}, f32[1,8,128,128]{3,2,1,0:T(8,128)S(1)}, u32[]{:S(2)}, u32[]{:S(2)}) collective-permute-start(f32[1,8,128,128]{3,2,1,0:T(8,128)S(1)} %add.112), channel_id=1, source_target_pairs={{4,0},{5,1},{6,2},{7,3},{8,4},{9,5},{10,6},{11,7},{12,8},{13,9},{1... | collective-permute-start | bytes 1572872 | tf_op jit(solution)/shard_map/ppermute | solution.py:19
  973.5 14.5 collective-permute-start.8
  975.1 14.5 copy-start.17
  975.1 14.7 copy-start.1
  975.1 14.7 copy-start.15
  975.1 14.7 copy-start.21
  988.0 18.5 collective-permute-start.9
  989.8 16.8 copy-start.12
  991.0 16.3 copy-start.3
  1008.1 1.0 copy-start.20
  (3 other events, 2.1 us)
Sparse Core Ops, SparseCore 0:
  10.4 422.2 all-gather.4
  435.2 422.2 all-gather.6
  913.9 1291.0 reduce-scatter.1

commit v2 on v1

--- a/solution.py
+++ b/solution.py
@@ -23,26 +23,36 @@
 
 def gather_rows(weights, piece):
     place = lax.axis_index("ctx")
+    width = weights[0].shape[1]
     parts = [lax.dynamic_slice_in_dim(weight, place * piece, piece, 0) for weight in weights]
     joined = jnp.concatenate(parts, 0)
-    gathered = lax.all_gather(joined, ("dp", "ctx"), axis=0, tiled=True)
-    gathered = gathered.reshape(-1, len(weights), piece, joined.shape[1])
+    across = lax.all_gather(joined, "dp", axis=0, tiled=False)
+    return across.reshape(across.shape[0], len(weights), piece, width)
+
+
+def spread_rows(across):
+    blocks, count, piece, width = across.shape
+    gathered = lax.all_gather(across, "ctx", axis=0, tiled=False)
+    gathered = jnp.transpose(gathered, (2, 1, 0, 3, 4))
     return tuple(
-        gathered[:, index].reshape(-1, joined.shape[1]) for index in range(len(weights))
+        gathered[index].reshape(-1, width) for index in range(count)
     )
 
 
-def weight_grads(pairs, factor, owners):
+def weight_grads(pairs, factor):
     width = pairs[0][0].shape[1]
+    outer, inner = lax.axis_size("dp"), lax.axis_size("ctx")
     blocks = []
     for left, right in pairs:
         made = lax.dot_general(
             left, right, (((0,), (0,)), ((), ())), preferred_element_type=jnp.float32
         )
-        blocks.append((factor * made).reshape(owners, -1, width))
-    rows = blocks[0].shape[1]
-    stacked = jnp.concatenate(blocks, 1).reshape(-1, width)
-    share = lax.psum_scatter(stacked, ("dp", "ctx"), scatter_dimension=0, tiled=True)
+        blocks.append((factor * made).reshape(outer, inner, -1, width))
+    rows = blocks[0].shape[2]
+    stacked = jnp.concatenate(blocks, 2)
+    stacked = jnp.transpose(stacked, (1, 0, 2, 3)).reshape(-1, width)
+    share = lax.psum_scatter(stacked, "ctx", scatter_dimension=0, tiled=True)
+    share = lax.psum_scatter(share, "dp", scatter_dimension=0, tiled=True)
     return tuple(share[index * rows : (index + 1) * rows] for index in range(len(pairs)))
 
 
@@ -51,8 +61,9 @@
     owners = lax.axis_size("dp") * lax.axis_size("ctx")
     factor = float(batch * tokens_here * owners) ** (-0.5)
     piece = w_query.shape[0] // lax.axis_size("ctx")
-    full_query, full_key, full_value = gather_rows((w_query, w_key, w_value), piece)
-    (full_out,) = gather_rows((w_out,), piece)
+    across = gather_rows((w_query, w_key, w_value, w_out), piece)
+    full_query, full_key, full_value = spread_rows(across[:, :3])
+    (full_out,) = spread_rows(across[:, 3:])
     second_wide = x_second.astype(jnp.float32)
     inv_rms = lax.rsqrt(jnp.mean(second_wide * second_wide, -1, keepdims=True) + 1e-06)
     normed_wide = second_wide * inv_rms
@@ -131,7 +142,7 @@
         (normed.reshape(-1, width), query_grad.reshape(-1, width)),
         (attn_out.reshape(-1, width), grad_first.reshape(-1, width)),
     )
-    grad_query, grad_out = weight_grads(pairs, factor, owners)
+    grad_query, grad_out = weight_grads(pairs, factor)
     return (x_first, grad_x_second, grad_query, grad_out)
 
 

time: 2220 us -> 542 us (0.24)
  waiting for transfers between devices: 2060 us -> 346 us
  blocking collectives: 0 us -> 40.7 us
    reduce_scatter x1 -> x2, waiting for transfers between devices: 1190 us -> 134 us  [the longest x1 82.2 us: weight_grads(): share = lax.psum_scatter(share, 'dp', scatter_dimension=0, tiled=True)]
    all_gather x2, waiting for transfers between devices: 760 us -> 71 us  [spread_rows(): gathered = lax.all_gather(across, 'ctx', axis=0, tiled=False)]
    all_gather x0 -> x1, blocking collectives: none -> 40.7 us  [gather_rows(): across = lax.all_gather(joined, 'dp', axis=0, tiled=False)]
    ppermute x10, waiting for transfers between devices: 104 us -> 141 us  [scan_sum(): total = total + lax.ppermute(total, axis, pairs)]
  transfers between devices with their start and end apart: 13 -> 14, of which waited for: 12 -> 12; matrix products, arithmetic and copies ran while one was open for 3% -> 11% of each run, Pallas kernels for 0% -> 0%
where the time goes in v2:
time: 542 us; the launch traced here: 540 us
  waiting for transfers between devices  346 us (64%)
  local copies, waits for them, and re-layouts  60 us (11%)
  blocking collectives  40.7 us (8%)
  starting transfers between devices  40.2 us (7%)
  matrix products  24.2 us (4%)
  other arithmetic  14.3 us (3%)
  between operations  14.3 us (3%)
    ppermute x10, waiting for transfers between devices, scan_sum(): total = total + lax.ppermute(total, axis, pairs)  141 us
    reduce_scatter x1, waiting for transfers between devices, weight_grads(): share = lax.psum_scatter(share, 'dp', scatter_dimension=0, tiled=True)  82.2 us
    all_gather x2, waiting for transfers between devices, spread_rows(): gathered = lax.all_gather(across, 'ctx', axis=0, tiled=False)  71 us
    reduce_scatter x1, waiting for transfers between devices, weight_grads(): share = lax.psum_scatter(stacked, 'ctx', scatter_dimension=0, tiled=True)  51.6 us
    all_gather x1, blocking collectives, gather_rows(): across = lax.all_gather(joined, 'dp', axis=0, tiled=False)  40.7 us
    ppermute x10, starting transfers between devices, scan_sum(): total = total + lax.ppermute(total, axis, pairs)  40.1 us
    another operation x4, local copies, waits for them, and re-layouts, spread_rows(): return tuple((gathered[index].reshape(-1, width) for index in range(count)))  14.5 us
    slice x4, local copies, waits for them, and re-layouts, spread_rows(): return tuple((gathered[index].reshape(-1, width) for index in range(count)))  13.3 us
  transfers between devices with their start and end apart: 14, of which 12 were waited for; matrix products, arithmetic and copies ran while one was open for 11% of the time, Pallas kernels for 0%

profile of v2, /device:TPU:1, one launch (start us, length us, event | category | flops | bytes accessed | tf_op | source)
XLA Modules:
  0.0 540.0 jit_solution(4067291238680050435)
XLA Ops:
  8.8 40.7 %all-gather = bf16[128,1024]{1,0:T(8,128)(2,1)S(1)} all-gather(bf16[16,1024]{1,0:T(8,128)(2,1)S(1)} %pad_maximum_fusion), channel_id=2, replica_groups=mesh['dp'=8,'ctx'=32] {'dp'}, dimensions={0}, use_global_device_ids=true | all-gather | bytes 294912 | tf_op jit(solution)/shard_map/all_gather | solution.py:29
  52.2 71.0 %all-gather.6.cloned.1.call-done = bf16[256,3,4,1024]{3,2,1,0:T(4,128)(2,1)} async-done(((bf16[8,3,4,1024]{3,2,1,0:T(4,128)(2,1)}), bf16[256,3,4,1024]{3,2,1,0:T(4,128)(2,1)}) %all-gather.6.cloned.1.call-update) | async-done | bytes 6291472 | tf_op jit(solution)/shard_map/all_gather | solution.py:35
  123.2 5.0 copy.153
  130.9 3.0 copy.95
  136.4 4.6 copy.97
  141.0 4.1 reshape_squeeze.14
  148.9 3.2 collective-permute-start
  152.1 7.7 %collective-permute-done = f32[1,8,128,128]{3,2,1,0:T(8,128)S(1)} collective-permute-done((f32[1,8,128,128]{3,2,1,0:T(8,128)S(1)}, f32[1,8,128,128]{3,2,1,0:T(8,128)S(1)}, u32[]{:S(2)}, u32[]{:S(2)}) %collective-permute-start) | collective-permute-done | bytes 524320 | tf_op jit(solution)/shard_map/ppermute | solution.py:19
  162.5 11.5 %collective-permute-done.1 = f32[1,8,128,128]{3,2,1,0:T(8,128)S(1)} collective-permute-done((f32[1,8,128,128]{3,2,1,0:T(8,128)S(1)}, f32[1,8,128,128]{3,2,1,0:T(8,128)S(1)}, u32[]{:S(2)}, u32[]{:S(2)}) %collective-permute-start.1) | collective-permute-done | bytes 524320 | tf_op jit(solution)/shard_map/ppermute | solution.py:19
  174.1 6.8 %collective-permute-start.2 = (f32[1,8,128,128]{3,2,1,0:T(8,128)S(1)}, f32[1,8,128,128]{3,2,1,0:T(8,128)S(1)}, u32[]{:S(2)}, u32[]{:S(2)}) collective-permute-start(f32[1,8,128,128]{3,2,1,0:T(8,128)S(1)} %add.103), channel_id=1, source_target_pairs={{0,4},{1,5},{2,6},{3,7},{4,8},{5,9},{6,10},{7,11},{8,12},{9,13},{1... | collective-permute-start | bytes 1572872 | tf_op jit(solution)/shard_map/ppermute | solution.py:19
  180.9 11.7 %collective-permute-done.2 = f32[1,8,128,128]{3,2,1,0:T(8,128)S(1)} collective-permute-done((f32[1,8,128,128]{3,2,1,0:T(8,128)S(1)}, f32[1,8,128,128]{3,2,1,0:T(8,128)S(1)}, u32[]{:S(2)}, u32[]{:S(2)}) %collective-permute-start.2) | collective-permute-done | bytes 524320 | tf_op jit(solution)/shard_map/ppermute | solution.py:19
  193.5 14.2 %collective-permute-start.3 = (f32[1,8,128,128]{3,2,1,0:T(8,128)}, f32[1,8,128,128]{3,2,1,0:T(8,128)}, u32[]{:S(2)}, u32[]{:S(2)}) collective-permute-start(f32[1,8,128,128]{3,2,1,0:T(8,128)} %add.104), channel_id=1, source_target_pairs={{0,8},{1,9},{2,10},{3,11},{4,12},{5,13},{6,14},{7,15},{8,16},{9,17... | collective-permute-start | bytes 1572872 | tf_op jit(solution)/shard_map/ppermute | solution.py:19
  210.0 2.9 copy.106
  212.9 4.0 reshape_squeeze.15
  216.9 3.3 fusion.31
  220.1 3.0 copy.96
  223.1 3.9 reshape_squeeze.13
  229.1 4.8 collective-permute-start.4
  240.6 3.9 collective-permute-done.4
  251.6 5.2 reshape.218
  256.7 3.6 convolution_multiply_fusion
  260.4 5.3 reshape.219
  265.7 5.6 %maximum_bitcast_fusion = f32[32,8,8,1024]{3,2,0,1:T(8,128)S(1)} fusion(f32[8,32,4,1024]{3,2,1,0:T(4,128)} %reshape.219, f32[8,32,4,1024]{3,2,1,0:T(4,128)} %reshape.218), kind=kLoop, calls=%fused_computation | loop fusion | flops 2097152 | bytes 16777216 | tf_op jit(solution)/shard_map/transpose | solution.py:53
  271.3 4.1 copy.117
  275.8 3.2 collective-permute-start.5
  279.0 7.4 %collective-permute-done.5 = f32[1,8,128,128]{3,2,1,0:T(8,128)S(1)} collective-permute-done((f32[1,8,128,128]{3,2,1,0:T(8,128)S(1)}, f32[1,8,128,128]{3,2,1,0:T(8,128)S(1)}, u32[]{:S(2)}, u32[]{:S(2)}) %collective-permute-start.5) | collective-permute-done | bytes 524320 | tf_op jit(solution)/shard_map/ppermute | solution.py:19
  287.9 24.1 %collective-permute-done.6 = f32[1,8,128,128]{3,2,1,0:T(8,128)S(1)} collective-permute-done((f32[1,8,128,128]{3,2,1,0:T(8,128)S(1)}, f32[1,8,128,128]{3,2,1,0:T(8,128)S(1)}, u32[]{:S(2)}, u32[]{:S(2)}) %collective-permute-start.6) | collective-permute-done | bytes 524320 | tf_op jit(solution)/shard_map/ppermute | solution.py:19
  313.4 41.2 %collective-permute-done.7 = f32[1,8,128,128]{3,2,1,0:T(8,128)S(1)} collective-permute-done((f32[1,8,128,128]{3,2,1,0:T(8,128)S(1)}, f32[1,8,128,128]{3,2,1,0:T(8,128)S(1)}, u32[]{:S(2)}, u32[]{:S(2)}) %collective-permute-start.7) | collective-permute-done | bytes 524320 | tf_op jit(solution)/shard_map/ppermute | solution.py:19
  357.1 12.3 %collective-permute-done.8 = f32[1,8,128,128]{3,2,1,0:T(8,128)S(1)} collective-permute-done((f32[1,8,128,128]{3,2,1,0:T(8,128)S(1)}, f32[1,8,128,128]{3,2,1,0:T(8,128)S(1)}, u32[]{:S(2)}, u32[]{:S(2)}) %collective-permute-start.8) | collective-permute-done | bytes 524320 | tf_op jit(solution)/shard_map/ppermute | solution.py:19
  372.2 21.6 %collective-permute-done.9 = f32[1,8,128,128]{3,2,1,0:T(8,128)S(1)} collective-permute-done((f32[1,8,128,128]{3,2,1,0:T(8,128)S(1)}, f32[1,8,128,128]{3,2,1,0:T(8,128)S(1)}, u32[]{:S(2)}, u32[]{:S(2)}) %collective-permute-start.9) | collective-permute-done | bytes 524320 | tf_op jit(solution)/shard_map/ppermute | solution.py:19
  395.4 51.6 %reduce-scatter.3.cloned.1.call-done = f32[64,1024]{1,0:T(8,128)} async-done(((f32[2048,1024]{1,0:T(8,128)}), f32[64,1024]{1,0:T(8,128)}) %reduce-scatter.3.cloned.1.call-update) | async-done | bytes 262160 | tf_op jit(solution)/shard_map/reduce_scatter | solution.py:54
  449.9 82.2 %reduce-scatter.5.cloned.1.call-done = f32[8,1024]{1,0:T(8,128)} async-done(((f32[64,1024]{1,0:T(8,128)}), f32[8,1024]{1,0:T(8,128)}) %reduce-scatter.5.cloned.1.call-update) | async-done | bytes 32784 | tf_op jit(solution)/shard_map/reduce_scatter | solution.py:55
  (111 shorter events, 49.2 us)
Async XLA Ops:
  7.2 209.7 %copy-start = (bf16[1,128,1024]{2,1,0:T(8,128)(2,1)S(1)}, bf16[1,128,1024]{2,1,0:T(8,128)(2,1)}, u32[]{:S(2)}) copy-start(bf16[1,128,1024]{2,1,0:T(8,128)(2,1)} %param.10) | copy-start | bytes 786436
  7.2 116.0 %all-gather.6.cloned.1.call-start = ((), (), s32[]{:S(2)}) async-start(), calls=%async_computation.4 | async-start | bytes 6488064 | tf_op jit(solution)/shard_map/all_gather | solution.py:35
  50.3 157.4 %all-gather.8.cloned.1.call-start = ((), (), s32[]{:S(2)}) async-start(), calls=%async_computation.5 | async-start | bytes 2162688 | tf_op jit(solution)/shard_map/all_gather | solution.py:35
  51.1 395.9 %reduce-scatter.3.cloned.1.call-start = ((), (), s32[]{:S(2)}) async-start(), calls=%async_computation.2 | async-start | bytes 8650752 | tf_op jit(solution)/shard_map/reduce_scatter | solution.py:54
  141.0 4.1 copy-start.5
  148.2 11.7 %copy-start.14 = (bf16[128,8,128]{0,2,1:T(8,128)(2,1)}, bf16[128,8,128]{0,2,1:T(8,128)(2,1)S(1)}, u32[]{:S(2)}) copy-start(bf16[128,8,128]{0,2,1:T(8,128)(2,1)S(1)} %copy.101) | copy-start | bytes 786436
  148.7 25.3 %copy-start.8 = (bf16[16,8,8,128]{3,2,1,0:T(8,128)(2,1)}, bf16[16,8,8,128]{3,2,1,0:T(8,128)(2,1)S(1)}, u32[]{:S(2)}) copy-start(bf16[16,8,8,128]{3,2,1,0:T(8,128)(2,1)S(1)} %fusion.9) | copy-start | bytes 786436
  148.9 10.9 %collective-permute-start = (f32[1,8,128,128]{3,2,1,0:T(8,128)S(1)}, f32[1,8,128,128]{3,2,1,0:T(8,128)S(1)}, u32[]{:S(2)}, u32[]{:S(2)}) collective-permute-start(f32[1,8,128,128]{3,2,1,0:T(8,128)S(1)} %convolution_bitcast_fusion.2), channel_id=1, source_target_pairs={{0,1},{1,2},{2,3},{3,4},{4,5},{5,6},{6,7},{7,8},{8,9},{9,10},{10,1... | collective-permute-start | bytes 1572872 | tf_op jit(solution)/shard_map/ppermute | solution.py:19
  159.9 14.1 %collective-permute-start.1 = (f32[1,8,128,128]{3,2,1,0:T(8,128)S(1)}, f32[1,8,128,128]{3,2,1,0:T(8,128)S(1)}, u32[]{:S(2)}, u32[]{:S(2)}) collective-permute-start(f32[1,8,128,128]{3,2,1,0:T(8,128)S(1)} %add.102), channel_id=1, source_target_pairs={{0,2},{1,3},{2,4},{3,5},{4,6},{5,7},{6,8},{7,9},{8,10},{9,11},{10,... | collective-permute-start | bytes 1572872 | tf_op jit(solution)/shard_map/ppermute | solution.py:19
  174.1 18.6 %collective-permute-start.2 = (f32[1,8,128,128]{3,2,1,0:T(8,128)S(1)}, f32[1,8,128,128]{3,2,1,0:T(8,128)S(1)}, u32[]{:S(2)}, u32[]{:S(2)}) collective-permute-start(f32[1,8,128,128]{3,2,1,0:T(8,128)S(1)} %add.103), channel_id=1, source_target_pairs={{0,4},{1,5},{2,6},{3,7},{4,8},{5,9},{6,10},{7,11},{8,12},{9,13},{1... | collective-permute-start | bytes 1572872 | tf_op jit(solution)/shard_map/ppermute | solution.py:19
  193.5 33.6 %collective-permute-start.3 = (f32[1,8,128,128]{3,2,1,0:T(8,128)}, f32[1,8,128,128]{3,2,1,0:T(8,128)}, u32[]{:S(2)}, u32[]{:S(2)}) collective-permute-start(f32[1,8,128,128]{3,2,1,0:T(8,128)} %add.104), channel_id=1, source_target_pairs={{0,8},{1,9},{2,10},{3,11},{4,12},{5,13},{6,14},{7,15},{8,16},{9,17... | collective-permute-start | bytes 1572872 | tf_op jit(solution)/shard_map/ppermute | solution.py:19
  216.9 3.3 copy-start.6
  229.1 15.3 %collective-permute-start.4 = (f32[1,8,128,128]{3,2,1,0:T(8,128)}, f32[1,8,128,128]{3,2,1,0:T(8,128)}, u32[]{:S(2)}, u32[]{:S(2)}) collective-permute-start(f32[1,8,128,128]{3,2,1,0:T(8,128)} %add.105), channel_id=1, source_target_pairs={{0,16},{1,17},{2,18},{3,19},{4,20},{5,21},{6,22},{7,23},{8,24},{9,... | collective-permute-start | bytes 1572872 | tf_op jit(solution)/shard_map/ppermute | solution.py:19
  239.1 1.4 copy-start.17
  239.1 6.9 %copy-start.7 = (f32[1024,128]{1,0:T(8,128)S(1)}, f32[1024,128]{1,0:T(8,128)}, u32[]{:S(2)}) copy-start(f32[1024,128]{1,0:T(8,128)} %fusion.31) | copy-start | bytes 1572868
  246.0 1.3 copy-start.15
  275.4 256.6 %reduce-scatter.5.cloned.1.call-start = ((), (), s32[]{:S(2)}) async-start(), calls=%async_computation.3 | async-start | bytes 294912 | tf_op jit(solution)/shard_map/reduce_scatter | solution.py:55
  275.8 80.2 %copy-start.20 = (bf16[8,128,128]{2,1,0:T(8,128)(2,1)S(1)}, bf16[8,128,128]{2,1,0:T(8,128)(2,1)}, u32[]{:S(2)}) copy-start(bf16[8,128,128]{2,1,0:T(8,128)(2,1)} %copy-done.19) | copy-start | bytes 786436
  275.8 10.6 %collective-permute-start.5 = (f32[1,8,128,128]{3,2,1,0:T(8,128)S(1)}, f32[1,8,128,128]{3,2,1,0:T(8,128)S(1)}, u32[]{:S(2)}, u32[]{:S(2)}) collective-permute-start(f32[1,8,128,128]{3,2,1,0:T(8,128)S(1)} %convolution_bitcast_fusion), channel_id=1, source_target_pairs={{1,0},{2,1},{3,2},{4,3},{5,4},{6,5},{7,6},{8,7},{9,8},{10,9},{11,1... | collective-permute-start | bytes 1572872 | tf_op jit(solution)/shard_map/ppermute | solution.py:19
  286.5 69.7 %copy-start.3 = (bf16[1024,1024]{1,0:T(8,128)(2,1)S(1)}, bf16[1024,1024]{1,0:T(8,128)(2,1)}, u32[]{:S(2)}) copy-start(bf16[1024,1024]{1,0:T(8,128)(2,1)} %reshape_squeeze.13) | copy-start | bytes 6291460
  286.5 69.7 %copy-start.11 = (bf16[8,128,128]{2,1,0:T(8,128)(2,1)S(1)}, bf16[8,128,128]{2,1,0:T(8,128)(2,1)}, u32[]{:S(2)}) copy-start(bf16[8,128,128]{2,1,0:T(8,128)(2,1)} %copy-done.10) | copy-start | bytes 786436
  286.5 25.5 %collective-permute-start.6 = (f32[1,8,128,128]{3,2,1,0:T(8,128)S(1)}, f32[1,8,128,128]{3,2,1,0:T(8,128)S(1)}, u32[]{:S(2)}, u32[]{:S(2)}) collective-permute-start(f32[1,8,128,128]{3,2,1,0:T(8,128)S(1)} %add.113), channel_id=1, source_target_pairs={{2,0},{3,1},{4,2},{5,3},{6,4},{7,5},{8,6},{9,7},{10,8},{11,9},{12,... | collective-permute-start | bytes 1572872 | tf_op jit(solution)/shard_map/ppermute | solution.py:19
  312.1 42.5 %collective-permute-start.7 = (f32[1,8,128,128]{3,2,1,0:T(8,128)S(1)}, f32[1,8,128,128]{3,2,1,0:T(8,128)S(1)}, u32[]{:S(2)}, u32[]{:S(2)}) collective-permute-start(f32[1,8,128,128]{3,2,1,0:T(8,128)S(1)} %add.114), channel_id=1, source_target_pairs={{4,0},{5,1},{6,2},{7,3},{8,4},{9,5},{10,6},{11,7},{12,8},{13,9},{1... | collective-permute-start | bytes 1572872 | tf_op jit(solution)/shard_map/ppermute | solution.py:19
  354.6 14.7 %collective-permute-start.8 = (f32[1,8,128,128]{3,2,1,0:T(8,128)S(1)}, f32[1,8,128,128]{3,2,1,0:T(8,128)S(1)}, u32[]{:S(2)}, u32[]{:S(2)}) collective-permute-start(f32[1,8,128,128]{3,2,1,0:T(8,128)S(1)} %add.115), channel_id=1, source_target_pairs={{8,0},{9,1},{10,2},{11,3},{12,4},{13,5},{14,6},{15,7},{16,8},{17,9... | collective-permute-start | bytes 1572872 | tf_op jit(solution)/shard_map/ppermute | solution.py:19
  356.2 14.6 %copy-start.18 = (bf16[8,128,128]{2,1,0:T(8,128)(2,1)S(1)}, bf16[8,128,128]{2,1,0:T(8,128)(2,1)}, u32[]{:S(2)}) copy-start(bf16[8,128,128]{2,1,0:T(8,128)(2,1)} %copy-done.17) | copy-start | bytes 786436
  356.2 14.8 %copy-start.2 = (bf16[1024,1024]{1,0:T(8,128)(2,1)S(1)}, bf16[1024,1024]{1,0:T(8,128)(2,1)}, u32[]{:S(2)}) copy-start(bf16[1024,1024]{1,0:T(8,128)(2,1)} %reshape_squeeze.15) | copy-start | bytes 6291460
  356.2 14.8 %copy-start.16 = (bf16[1,128,8,128]{1,3,2,0:T(8,128)(2,1)S(1)}, bf16[1,128,8,128]{1,3,2,0:T(8,128)(2,1)}, u32[]{:S(2)}) copy-start(bf16[1,128,8,128]{1,3,2,0:T(8,128)(2,1)} %get-tuple-element.8) | copy-start | bytes 786436
  356.2 14.8 %copy-start.21 = (bf16[1,128,1024]{2,1,0:T(8,128)(2,1)S(1)}, bf16[1,128,1024]{2,1,0:T(8,128)(2,1)}, u32[]{:S(2)}) copy-start(bf16[1,128,1024]{2,1,0:T(8,128)(2,1)} %param.8) | copy-start | bytes 786436
  369.4 24.3 %collective-permute-start.9 = (f32[1,8,128,128]{3,2,1,0:T(8,128)S(1)}, f32[1,8,128,128]{3,2,1,0:T(8,128)S(1)}, u32[]{:S(2)}, u32[]{:S(2)}) collective-permute-start(f32[1,8,128,128]{3,2,1,0:T(8,128)S(1)} %add.116), channel_id=1, source_target_pairs={{16,0},{17,1},{18,2},{19,3},{20,4},{21,5},{22,6},{23,7},{24,8},{25... | collective-permute-start | bytes 1572872 | tf_op jit(solution)/shard_map/ppermute | solution.py:19
  371.0 22.9 %copy-start.13 = (bf16[128,1024]{1,0:T(8,128)(2,1)S(1)}, bf16[128,1024]{1,0:T(8,128)(2,1)}, u32[]{:S(2)}) copy-start(bf16[128,1024]{1,0:T(8,128)(2,1)} %copy-done.12) | copy-start | bytes 786436
  372.2 22.3 %copy-start.4 = (bf16[1024,1024]{1,0:T(8,128)(2,1)S(1)}, bf16[1024,1024]{1,0:T(8,128)(2,1)}, u32[]{:S(2)}) copy-start(bf16[1024,1024]{1,0:T(8,128)(2,1)} %reshape_squeeze.14) | copy-start | bytes 6291460
  447.0 86.5 %copy-start.1 = (bf16[1,128,1024]{2,1,0:T(8,128)(2,1)S(1)}, bf16[1,128,1024]{2,1,0:T(8,128)(2,1)}, u32[]{:S(2)}) copy-start(bf16[1,128,1024]{2,1,0:T(8,128)(2,1)} %param.10) | copy-start | bytes 786436
  (4 other events, 3.4 us)
Sparse Core Ops, SparseCore 0:
  50.5 72.6 all-gather.5
  125.1 82.0 all-gather.7
  275.6 171.3 reduce-scatter.2
  450.7 81.3 reduce-scatter.4

commit v3 on v2

--- a/solution.py
+++ b/solution.py
@@ -1,10 +1,11 @@
 import jax
 import jax.numpy as jnp
 from jax import lax
-from jax.sharding import PartitionSpec as P
+from jax.sharding import Mesh, PartitionSpec as P
 
 HEADS = 8
 HEAD_DIM = 128
+CTX = ("cy", "core")
 
 
 def scan_sum(shard, axis, reverse):
@@ -22,7 +23,7 @@
 
 
 def gather_rows(weights, piece):
-    place = lax.axis_index("ctx")
+    place = lax.axis_index(CTX)
     width = weights[0].shape[1]
     parts = [lax.dynamic_slice_in_dim(weight, place * piece, piece, 0) for weight in weights]
     joined = jnp.concatenate(parts, 0)
@@ -32,7 +33,7 @@
 
 def spread_rows(across):
     blocks, count, piece, width = across.shape
-    gathered = lax.all_gather(across, "ctx", axis=0, tiled=False)
+    gathered = lax.all_gather(across, CTX, axis=0, tiled=False)
     gathered = jnp.transpose(gathered, (2, 1, 0, 3, 4))
     return tuple(
         gathered[index].reshape(-1, width) for index in range(count)
@@ -41,26 +42,34 @@
 
 def weight_grads(pairs, factor):
     width = pairs[0][0].shape[1]
-    outer, inner = lax.axis_size("dp"), lax.axis_size("ctx")
+    outer, chips, cores = lax.axis_size("dp"), lax.axis_size("cy"), lax.axis_size("core")
+    mine = lax.axis_index("core")
+    swap = [(0, 1), (1, 0)]
     blocks = []
     for left, right in pairs:
+        other_left, other_right = lax.ppermute((left, right), "core", swap)
+        both_left = jnp.concatenate([left, other_left], 0)
+        both_right = jnp.concatenate([right, other_right], 0)
+        tokens = both_left.shape[0]
+        picked = both_left.reshape(tokens, outer * chips, cores, -1)
+        picked = lax.dynamic_index_in_dim(picked, mine, 2, False).reshape(tokens, -1)
         made = lax.dot_general(
-            left, right, (((0,), (0,)), ((), ())), preferred_element_type=jnp.float32
+            picked, both_right, (((0,), (0,)), ((), ())), preferred_element_type=jnp.float32
         )
-        blocks.append((factor * made).reshape(outer, inner, -1, width))
+        blocks.append((factor * made).reshape(outer, chips, -1, width))
     rows = blocks[0].shape[2]
     stacked = jnp.concatenate(blocks, 2)
     stacked = jnp.transpose(stacked, (1, 0, 2, 3)).reshape(-1, width)
-    share = lax.psum_scatter(stacked, "ctx", scatter_dimension=0, tiled=True)
+    share = lax.psum_scatter(stacked, "cy", scatter_dimension=0, tiled=True)
     share = lax.psum_scatter(share, "dp", scatter_dimension=0, tiled=True)
     return tuple(share[index * rows : (index + 1) * rows] for index in range(len(pairs)))
 
 
 def on_device(y_first, x_second, grad_first, grad_second, w_query, w_key, w_value, w_out):
     batch, tokens_here, width = y_first.shape
-    owners = lax.axis_size("dp") * lax.axis_size("ctx")
+    owners = lax.axis_size("dp") * lax.axis_size(CTX)
     factor = float(batch * tokens_here * owners) ** (-0.5)
-    piece = w_query.shape[0] // lax.axis_size("ctx")
+    piece = w_query.shape[0] // lax.axis_size(CTX)
     across = gather_rows((w_query, w_key, w_value, w_out), piece)
     full_query, full_key, full_value = spread_rows(across[:, :3])
     (full_out,) = spread_rows(across[:, 3:])
@@ -79,7 +88,7 @@
     local_state = jnp.einsum(
         "bthe,bthf->bhef", key_rows, values, preferred_element_type=jnp.float32
     )
-    before = (scan_sum(local_state, "ctx", False) - local_state).astype(jnp.bfloat16)
+    before = (scan_sum(local_state, CTX, False) - local_state).astype(jnp.bfloat16)
     causal = jnp.tril(jnp.ones((tokens_here, tokens_here), dtype=bool))
     scores = jnp.einsum("bthe,bshe->bhts", queries, key_rows, preferred_element_type=jnp.float32)
     scores = jnp.where(causal[None, None], scores, 0.0).astype(jnp.bfloat16)
@@ -103,7 +112,7 @@
     grad_local = jnp.einsum(
         "bthe,bthf->bhef", queries, grad_mixed, preferred_element_type=jnp.float32
     )
-    after_state = (scan_sum(grad_local, "ctx", True) - grad_local).astype(jnp.bfloat16)
+    after_state = (scan_sum(grad_local, CTX, True) - grad_local).astype(jnp.bfloat16)
     query_grad = jnp.einsum(
         "bhts,bshe->bthe", score_grad, key_rows, preferred_element_type=jnp.float32
     )
@@ -147,25 +156,15 @@
 
 
 def solution(mesh):
-    placed = (
-        P("dp", "ctx", None),
-        P("dp", "ctx", None),
-        P("dp", "ctx", None),
-        P("dp", "ctx", None),
-        P("dp", None),
-        P("dp", None),
-        P("dp", None),
-        P("dp", None),
-    )
+    dp, ctx = mesh.devices.shape
+    fine = Mesh(mesh.devices.reshape(dp, ctx // 2, 2), ("dp", "cy", "core"))
+    ctx_axes = ("cy", "core")
+    rows = P("dp", ctx_axes, None)
+    placed = (rows, rows, rows, rows, P("dp", None), P("dp", None), P("dp", None), P("dp", None))
     return jax.shard_map(
         on_device,
-        mesh=mesh,
+        mesh=fine,
         in_specs=placed,
-        out_specs=(
-            P("dp", "ctx", None),
-            P("dp", "ctx", None),
-            P(("dp", "ctx"), None),
-            P(("dp", "ctx"), None),
-        ),
+        out_specs=(rows, rows, P(("dp",) + ctx_axes, None), P(("dp",) + ctx_axes, None)),
         check_vma=False,
     )

time: 542 us -> 510 us (0.941)
  waiting for transfers between devices: 346 us -> 313 us
    reduce_scatter x1, waiting for transfers between devices: 51.6 us -> 0.02 us  [weight_grads(): share = lax.psum_scatter(stacked, 'cy', scatter_dimension=0, tiled=True)]
    ppermute x10, waiting for transfers between devices: 141 us -> 160 us  [scan_sum(): total = total + lax.ppermute(total, axis, pairs)]
  transfers between devices with their start and end apart: 14 -> 18, of which waited for: 12 -> 11; matrix products, arithmetic and copies ran while one was open for 11% -> 16% of each run, Pallas kernels for 0% -> 0%
where the time goes in v3:
time: 510 us; the launch traced here: 507 us
  waiting for transfers between devices  313 us (61%)
  local copies, waits for them, and re-layouts  59.8 us (12%)
  starting transfers between devices  41.4 us (8%)
  blocking collectives  40.7 us (8%)
  matrix products  24.2 us (5%)
  between operations  14.3 us (3%)
  other arithmetic  13.9 us (3%)
    ppermute x10, waiting for transfers between devices, scan_sum(): total = total + lax.ppermute(total, axis, pairs)  160 us
    reduce_scatter x1, waiting for transfers between devices, weight_grads(): share = lax.psum_scatter(share, 'dp', scatter_dimension=0, tiled=True)  81.8 us
    all_gather x2, waiting for transfers between devices, spread_rows(): gathered = lax.all_gather(across, CTX, axis=0, tiled=False)  70.9 us
    all_gather x1, blocking collectives, gather_rows(): across = lax.all_gather(joined, 'dp', axis=0, tiled=False)  40.7 us
    ppermute x10, starting transfers between devices, scan_sum(): total = total + lax.ppermute(total, axis, pairs)  37.3 us
    another operation x4, local copies, waits for them, and re-layouts, spread_rows(): return tuple((gathered[index].reshape(-1, width) for index in range(count)))  14.5 us
    slice x4, local copies, waits for them, and re-layouts, spread_rows(): return tuple((gathered[index].reshape(-1, width) for index in range(count)))  13.2 us
  transfers between devices with their start and end apart: 18, of which 11 were waited for; matrix products, arithmetic and copies ran while one was open for 16% of the time, Pallas kernels for 0%

profile of v3, /device:TPU:1, one launch (start us, length us, event | category | flops | bytes accessed | tf_op | source)
XLA Modules:
  0.0 507.2 jit_solution(15313963412199255969)
XLA Ops:
  8.8 40.7 %all-gather = bf16[128,1024]{1,0:T(8,128)(2,1)S(1)} all-gather(bf16[16,1024]{1,0:T(8,128)(2,1)S(1)} %pad_maximum_fusion), channel_id=2, replica_groups=mesh['dp'=8,'cy'=16,'core'=2] {'dp'}, dimensions={0}, use_global_device_ids=true | all-gather | bytes 294912 | tf_op jit(solution)/shard_map/all_gather | solution.py:30
  52.4 70.8 %all-gather.6.cloned.1.call-done = bf16[256,3,4,1024]{3,2,1,0:T(4,128)(2,1)} async-done(((bf16[8,3,4,1024]{3,2,1,0:T(4,128)(2,1)}), bf16[256,3,4,1024]{3,2,1,0:T(4,128)(2,1)}) %all-gather.6.cloned.1.call-update) | async-done | bytes 6291472 | tf_op jit(solution)/shard_map/all_gather | solution.py:36
  123.2 5.0 copy.161
  128.2 2.7 fusion.50
  130.9 3.0 copy.101
  136.4 4.6 copy.103
  141.0 4.0 reshape_squeeze.14
  149.9 3.2 collective-permute-start
  153.1 7.9 %collective-permute-done = f32[1,8,128,128]{3,2,1,0:T(8,128)S(1)} collective-permute-done((f32[1,8,128,128]{3,2,1,0:T(8,128)S(1)}, f32[1,8,128,128]{3,2,1,0:T(8,128)S(1)}, u32[]{:S(2)}, u32[]{:S(2)}) %collective-permute-start) | collective-permute-done | bytes 524320 | tf_op jit(solution)/shard_map/ppermute | solution.py:20
  163.4 11.1 %collective-permute-done.1 = f32[1,8,128,128]{3,2,1,0:T(8,128)S(1)} collective-permute-done((f32[1,8,128,128]{3,2,1,0:T(8,128)S(1)}, f32[1,8,128,128]{3,2,1,0:T(8,128)S(1)}, u32[]{:S(2)}, u32[]{:S(2)}) %collective-permute-start.1) | collective-permute-done | bytes 524320 | tf_op jit(solution)/shard_map/ppermute | solution.py:20
  174.6 6.6 %collective-permute-start.2 = (f32[1,8,128,128]{3,2,1,0:T(8,128)S(1)}, f32[1,8,128,128]{3,2,1,0:T(8,128)S(1)}, u32[]{:S(2)}, u32[]{:S(2)}) collective-permute-start(f32[1,8,128,128]{3,2,1,0:T(8,128)S(1)} %add.112), channel_id=1, source_target_pairs={{0,4},{1,5},{2,6},{3,7},{4,8},{5,9},{6,10},{7,11},{8,12},{9,13},{1... | collective-permute-start | bytes 1572872 | tf_op jit(solution)/shard_map/ppermute | solution.py:20
  181.2 10.5 %collective-permute-done.2 = f32[1,8,128,128]{3,2,1,0:T(8,128)S(1)} collective-permute-done((f32[1,8,128,128]{3,2,1,0:T(8,128)S(1)}, f32[1,8,128,128]{3,2,1,0:T(8,128)S(1)}, u32[]{:S(2)}, u32[]{:S(2)}) %collective-permute-start.2) | collective-permute-done | bytes 524320 | tf_op jit(solution)/shard_map/ppermute | solution.py:20
  192.6 15.8 %collective-permute-start.3 = (f32[1,8,128,128]{3,2,1,0:T(8,128)}, f32[1,8,128,128]{3,2,1,0:T(8,128)}, u32[]{:S(2)}, u32[]{:S(2)}) collective-permute-start(f32[1,8,128,128]{3,2,1,0:T(8,128)} %add.113), channel_id=1, source_target_pairs={{0,8},{1,9},{2,10},{3,11},{4,12},{5,13},{6,14},{7,15},{8,16},{9,17... | collective-permute-start | bytes 1572872 | tf_op jit(solution)/shard_map/ppermute | solution.py:20
  209.2 2.7 collective-permute-start.10
  214.2 2.9 copy.112
  217.1 4.0 reshape_squeeze.15
  221.1 3.3 fusion.45
  224.4 3.0 copy.102
  227.4 4.0 reshape_squeeze.13
  235.5 2.7 convolution_convert_fusion.1
  242.1 4.4 collective-permute-done.4
  258.0 2.9 convolution_multiply_fusion.1
  261.0 2.9 reshape.235
  263.8 2.8 convolution_multiply_fusion
  266.6 2.9 reshape.237
  269.5 3.3 maximum_bitcast_fusion
  278.4 8.6 %collective-permute-done.5 = f32[1,8,128,128]{3,2,1,0:T(8,128)S(1)} collective-permute-done((f32[1,8,128,128]{3,2,1,0:T(8,128)S(1)}, f32[1,8,128,128]{3,2,1,0:T(8,128)S(1)}, u32[]{:S(2)}, u32[]{:S(2)}) %collective-permute-start.5) | collective-permute-done | bytes 524320 | tf_op jit(solution)/shard_map/ppermute | solution.py:20
  288.5 33.7 %collective-permute-done.6 = f32[1,8,128,128]{3,2,1,0:T(8,128)S(1)} collective-permute-done((f32[1,8,128,128]{3,2,1,0:T(8,128)S(1)}, f32[1,8,128,128]{3,2,1,0:T(8,128)S(1)}, u32[]{:S(2)}, u32[]{:S(2)}) %collective-permute-start.6) | collective-permute-done | bytes 524320 | tf_op jit(solution)/shard_map/ppermute | solution.py:20
  323.6 51.6 %collective-permute-done.7 = f32[1,8,128,128]{3,2,1,0:T(8,128)S(1)} collective-permute-done((f32[1,8,128,128]{3,2,1,0:T(8,128)S(1)}, f32[1,8,128,128]{3,2,1,0:T(8,128)S(1)}, u32[]{:S(2)}, u32[]{:S(2)}) %collective-permute-start.7) | collective-permute-done | bytes 524320 | tf_op jit(solution)/shard_map/ppermute | solution.py:20
  378.8 11.7 %collective-permute-done.8 = f32[1,8,128,128]{3,2,1,0:T(8,128)S(1)} collective-permute-done((f32[1,8,128,128]{3,2,1,0:T(8,128)S(1)}, f32[1,8,128,128]{3,2,1,0:T(8,128)S(1)}, u32[]{:S(2)}, u32[]{:S(2)}) %collective-permute-start.8) | collective-permute-done | bytes 524320 | tf_op jit(solution)/shard_map/ppermute | solution.py:20
  393.3 20.5 %collective-permute-done.9 = f32[1,8,128,128]{3,2,1,0:T(8,128)S(1)} collective-permute-done((f32[1,8,128,128]{3,2,1,0:T(8,128)S(1)}, f32[1,8,128,128]{3,2,1,0:T(8,128)S(1)}, u32[]{:S(2)}, u32[]{:S(2)}) %collective-permute-start.9) | collective-permute-done | bytes 524320 | tf_op jit(solution)/shard_map/ppermute | solution.py:20
  417.4 81.8 %reduce-scatter.5.cloned.1.call-done = f32[8,1024]{1,0:T(8,128)} async-done(((f32[64,1024]{1,0:T(8,128)}), f32[8,1024]{1,0:T(8,128)}) %reduce-scatter.5.cloned.1.call-update) | async-done | bytes 32784 | tf_op jit(solution)/shard_map/reduce_scatter | solution.py:64
  (123 shorter events, 57.2 us)
Async XLA Ops:
  7.2 45.1 %copy-start.4 = (bf16[1,128,1024]{2,1,0:T(8,128)(2,1)S(1)}, bf16[1,128,1024]{2,1,0:T(8,128)(2,1)}, u32[]{:S(2)}) copy-start(bf16[1,128,1024]{2,1,0:T(8,128)(2,1)} %param.9) | copy-start | bytes 786436
  7.2 116.0 %all-gather.6.cloned.1.call-start = ((), (), s32[]{:S(2)}) async-start(), calls=%async_computation.4 | async-start | bytes 6488064 | tf_op jit(solution)/shard_map/all_gather | solution.py:36
  50.3 161.6 %all-gather.8.cloned.1.call-start = ((), (), s32[]{:S(2)}) async-start(), calls=%async_computation.5 | async-start | bytes 2162688 | tf_op jit(solution)/shard_map/all_gather | solution.py:36
  51.1 364.4 %reduce-scatter.3.cloned.1.call-start = ((), (), s32[]{:S(2)}) async-start(), calls=%async_computation.2 | async-start | bytes 4456448 | tf_op jit(solution)/shard_map/reduce_scatter | solution.py:63
  149.9 11.2 %collective-permute-start = (f32[1,8,128,128]{3,2,1,0:T(8,128)S(1)}, f32[1,8,128,128]{3,2,1,0:T(8,128)S(1)}, u32[]{:S(2)}, u32[]{:S(2)}) collective-permute-start(f32[1,8,128,128]{3,2,1,0:T(8,128)S(1)} %convolution_bitcast_fusion.2), channel_id=1, source_target_pairs={{0,1},{1,2},{2,3},{3,4},{4,5},{5,6},{6,7},{7,8},{8,9},{9,10},{10,1... | collective-permute-start | bytes 1572872 | tf_op jit(solution)/shard_map/ppermute | solution.py:20
  161.1 13.4 %collective-permute-start.1 = (f32[1,8,128,128]{3,2,1,0:T(8,128)S(1)}, f32[1,8,128,128]{3,2,1,0:T(8,128)S(1)}, u32[]{:S(2)}, u32[]{:S(2)}) collective-permute-start(f32[1,8,128,128]{3,2,1,0:T(8,128)S(1)} %add.111), channel_id=1, source_target_pairs={{0,2},{1,3},{2,4},{3,5},{4,6},{5,7},{6,8},{7,9},{8,10},{9,11},{10,... | collective-permute-start | bytes 1572872 | tf_op jit(solution)/shard_map/ppermute | solution.py:20
  174.6 17.1 %collective-permute-start.2 = (f32[1,8,128,128]{3,2,1,0:T(8,128)S(1)}, f32[1,8,128,128]{3,2,1,0:T(8,128)S(1)}, u32[]{:S(2)}, u32[]{:S(2)}) collective-permute-start(f32[1,8,128,128]{3,2,1,0:T(8,128)S(1)} %add.112), channel_id=1, source_target_pairs={{0,4},{1,5},{2,6},{3,7},{4,8},{5,9},{6,10},{7,11},{8,12},{9,13},{1... | collective-permute-start | bytes 1572872 | tf_op jit(solution)/shard_map/ppermute | solution.py:20
  192.6 38.8 %collective-permute-start.3 = (f32[1,8,128,128]{3,2,1,0:T(8,128)}, f32[1,8,128,128]{3,2,1,0:T(8,128)}, u32[]{:S(2)}, u32[]{:S(2)}) collective-permute-start(f32[1,8,128,128]{3,2,1,0:T(8,128)} %add.113), channel_id=1, source_target_pairs={{0,8},{1,9},{2,10},{3,11},{4,12},{5,13},{6,14},{7,15},{8,16},{9,17... | collective-permute-start | bytes 1572872 | tf_op jit(solution)/shard_map/ppermute | solution.py:20
  209.2 43.2 %collective-permute-start.10 = (bf16[128,1024]{1,0:T(8,128)(2,1)}, bf16[128,1024]{1,0:T(8,128)(2,1)}, u32[]{:S(2)}, u32[]{:S(2)}) collective-permute-start(bf16[128,1024]{1,0:T(8,128)(2,1)} %fusion.88), channel_id=1, source_target_pairs={{0,1},{1,0},{2,3},{3,2},{4,5},{5,4},{6,7},{7,6},{8,9},{9,8},{10,11... | collective-permute-start | bytes 786440 | tf_op jit(solution)/shard_map/ppermute | solution.py:50
  221.1 3.3 copy-start.3
  233.4 13.1 %collective-permute-start.4 = (f32[1,8,128,128]{3,2,1,0:T(8,128)}, f32[1,8,128,128]{3,2,1,0:T(8,128)}, u32[]{:S(2)}, u32[]{:S(2)}) collective-permute-start(f32[1,8,128,128]{3,2,1,0:T(8,128)} %add.114), channel_id=1, source_target_pairs={{0,16},{1,17},{2,18},{3,19},{4,20},{5,21},{6,22},{7,23},{8,24},{9,... | collective-permute-start | bytes 1572872 | tf_op jit(solution)/shard_map/ppermute | solution.py:20
  240.0 7.8 %copy-start.6 = (bf16[128,1024]{0,1:T(8,128)(2,1)S(1)}, bf16[128,1024]{0,1:T(8,128)(2,1)}, u32[]{:S(2)}) copy-start(bf16[128,1024]{0,1:T(8,128)(2,1)} %copy.131) | copy-start | bytes 786436
  241.4 6.7 %copy-start.5 = (f32[1024,128]{1,0:T(8,128)S(1)}, f32[1024,128]{1,0:T(8,128)}, u32[]{:S(2)}) copy-start(f32[1024,128]{1,0:T(8,128)} %fusion.45) | copy-start | bytes 1572868
  248.4 8.5 %copy-start.12 = (bf16[1,128,8,128]{1,3,2,0:T(8,128)(2,1)}, bf16[1,128,8,128]{1,3,2,0:T(8,128)(2,1)S(1)}, u32[]{:S(2)}) copy-start(bf16[1,128,8,128]{1,3,2,0:T(8,128)(2,1)S(1)} %get-tuple-element.8) | copy-start | bytes 786436
  249.1 1.9 copy-start.16
  249.4 7.5 %collective-permute-start.12 = (bf16[128,1024]{0,1:T(8,128)(2,1)S(1)}, bf16[128,1024]{0,1:T(8,128)(2,1)}, u32[]{:S(2)}, u32[]{:S(2)}) collective-permute-start(bf16[128,1024]{0,1:T(8,128)(2,1)S(1)} %bitcast.141), channel_id=1, source_target_pairs={{0,1},{1,0},{2,3},{3,2},{4,5},{5,4},{6,7},{7,6},{8,9},{9,8},{10,11... | collective-permute-start | bytes 786440 | tf_op jit(solution)/shard_map/ppermute | solution.py:50
  251.0 7.0 %collective-permute-start.11 = (bf16[128,1024]{0,1:T(8,128)(2,1)}, bf16[128,1024]{0,1:T(8,128)(2,1)}, u32[]{:S(2)}, u32[]{:S(2)}) collective-permute-start(bf16[128,1024]{0,1:T(8,128)(2,1)} %bitcast.20), channel_id=1, source_target_pairs={{0,1},{1,0},{2,3},{3,2},{4,5},{5,4},{6,7},{7,6},{8,9},{9,8},{10,11... | collective-permute-start | bytes 786440 | tf_op jit(solution)/shard_map/ppermute | solution.py:50
  251.0 12.8 %collective-permute-start.13 = (bf16[128,1024]{1,0:T(8,128)(2,1)}, bf16[128,1024]{1,0:T(8,128)(2,1)}, u32[]{:S(2)}, u32[]{:S(2)}) collective-permute-start(bf16[128,1024]{1,0:T(8,128)(2,1)} %bitcast.13), channel_id=1, source_target_pairs={{0,1},{1,0},{2,3},{3,2},{4,5},{5,4},{6,7},{7,6},{8,9},{9,8},{10,11... | collective-permute-start | bytes 786440 | tf_op jit(solution)/shard_map/ppermute | solution.py:50
  275.1 224.1 %reduce-scatter.5.cloned.1.call-start = ((), (), s32[]{:S(2)}) async-start(), calls=%async_computation.3 | async-start | bytes 294912 | tf_op jit(solution)/shard_map/reduce_scatter | solution.py:64
  276.4 100.2 %copy-start.17 = (bf16[8,128,128]{2,1,0:T(8,128)(2,1)S(1)}, bf16[8,128,128]{2,1,0:T(8,128)(2,1)}, u32[]{:S(2)}) copy-start(bf16[8,128,128]{2,1,0:T(8,128)(2,1)} %copy-done.16) | copy-start | bytes 786436
  276.4 10.6 %collective-permute-start.5 = (f32[1,8,128,128]{3,2,1,0:T(8,128)S(1)}, f32[1,8,128,128]{3,2,1,0:T(8,128)S(1)}, u32[]{:S(2)}, u32[]{:S(2)}) collective-permute-start(f32[1,8,128,128]{3,2,1,0:T(8,128)S(1)} %convolution_bitcast_fusion), channel_id=1, source_target_pairs={{1,0},{2,1},{3,2},{4,3},{5,4},{6,5},{7,6},{8,7},{9,8},{10,9},{11,1... | collective-permute-start | bytes 1572872 | tf_op jit(solution)/shard_map/ppermute | solution.py:20
  287.1 89.7 %copy-start = (bf16[1024,1024]{1,0:T(8,128)(2,1)S(1)}, bf16[1024,1024]{1,0:T(8,128)(2,1)}, u32[]{:S(2)}) copy-start(bf16[1024,1024]{1,0:T(8,128)(2,1)} %reshape_squeeze.13) | copy-start | bytes 6291460
  287.1 35.2 %collective-permute-start.6 = (f32[1,8,128,128]{3,2,1,0:T(8,128)S(1)}, f32[1,8,128,128]{3,2,1,0:T(8,128)S(1)}, u32[]{:S(2)}, u32[]{:S(2)}) collective-permute-start(f32[1,8,128,128]{3,2,1,0:T(8,128)S(1)} %add.122), channel_id=1, source_target_pairs={{2,0},{3,1},{4,2},{5,3},{6,4},{7,5},{8,6},{9,7},{10,8},{11,9},{12,... | collective-permute-start | bytes 1572872 | tf_op jit(solution)/shard_map/ppermute | solution.py:20
  322.3 52.9 %collective-permute-start.7 = (f32[1,8,128,128]{3,2,1,0:T(8,128)S(1)}, f32[1,8,128,128]{3,2,1,0:T(8,128)S(1)}, u32[]{:S(2)}, u32[]{:S(2)}) collective-permute-start(f32[1,8,128,128]{3,2,1,0:T(8,128)S(1)} %add.123), channel_id=1, source_target_pairs={{4,0},{5,1},{6,2},{7,3},{8,4},{9,5},{10,6},{11,7},{12,8},{13,9},{1... | collective-permute-start | bytes 1572872 | tf_op jit(solution)/shard_map/ppermute | solution.py:20
  375.3 15.3 %collective-permute-start.8 = (f32[1,8,128,128]{3,2,1,0:T(8,128)S(1)}, f32[1,8,128,128]{3,2,1,0:T(8,128)S(1)}, u32[]{:S(2)}, u32[]{:S(2)}) collective-permute-start(f32[1,8,128,128]{3,2,1,0:T(8,128)S(1)} %add.124), channel_id=1, source_target_pairs={{8,0},{9,1},{10,2},{11,3},{12,4},{13,5},{14,6},{15,7},{16,8},{17,9... | collective-permute-start | bytes 1572872 | tf_op jit(solution)/shard_map/ppermute | solution.py:20
  376.8 15.1 %copy-start.15 = (bf16[8,128,128]{2,1,0:T(8,128)(2,1)S(1)}, bf16[8,128,128]{2,1,0:T(8,128)(2,1)}, u32[]{:S(2)}) copy-start(bf16[8,128,128]{2,1,0:T(8,128)(2,1)} %copy-done.14) | copy-start | bytes 786436
  376.8 15.3 %copy-start.2 = (bf16[1024,1024]{1,0:T(8,128)(2,1)S(1)}, bf16[1024,1024]{1,0:T(8,128)(2,1)}, u32[]{:S(2)}) copy-start(bf16[1024,1024]{1,0:T(8,128)(2,1)} %reshape_squeeze.15) | copy-start | bytes 6291460
  376.8 15.3 %copy-start.13 = (bf16[1,128,8,128]{1,3,2,0:T(8,128)(2,1)S(1)}, bf16[1,128,8,128]{1,3,2,0:T(8,128)(2,1)}, u32[]{:S(2)}) copy-start(bf16[1,128,8,128]{1,3,2,0:T(8,128)(2,1)} %copy-done.12) | copy-start | bytes 786436
  376.8 15.3 %copy-start.19 = (bf16[1,128,1024]{2,1,0:T(8,128)(2,1)S(1)}, bf16[1,128,1024]{2,1,0:T(8,128)(2,1)}, u32[]{:S(2)}) copy-start(bf16[1,128,1024]{2,1,0:T(8,128)(2,1)} %param.8) | copy-start | bytes 786436
  390.6 23.2 %collective-permute-start.9 = (f32[1,8,128,128]{3,2,1,0:T(8,128)S(1)}, f32[1,8,128,128]{3,2,1,0:T(8,128)S(1)}, u32[]{:S(2)}, u32[]{:S(2)}) collective-permute-start(f32[1,8,128,128]{3,2,1,0:T(8,128)S(1)} %add.125), channel_id=1, source_target_pairs={{16,0},{17,1},{18,2},{19,3},{20,4},{21,5},{22,6},{23,7},{24,8},{25... | collective-permute-start | bytes 1572872 | tf_op jit(solution)/shard_map/ppermute | solution.py:20
  392.1 21.8 %copy-start.9 = (bf16[128,1024]{1,0:T(8,128)(2,1)S(1)}, bf16[128,1024]{1,0:T(8,128)(2,1)}, u32[]{:S(2)}) copy-start(bf16[128,1024]{1,0:T(8,128)(2,1)} %copy-done.8) | copy-start | bytes 786436
  393.3 21.2 %copy-start.1 = (bf16[1024,1024]{1,0:T(8,128)(2,1)S(1)}, bf16[1024,1024]{1,0:T(8,128)(2,1)}, u32[]{:S(2)}) copy-start(bf16[1024,1024]{1,0:T(8,128)(2,1)} %reshape_squeeze.14) | copy-start | bytes 6291460
  (6 other events, 5.3 us)
Sparse Core Ops, SparseCore 0:
  50.5 72.6 all-gather.5
  125.6 82.5 all-gather.7
  275.3 133.5 reduce-scatter.2
  415.6 83.5 reduce-scatter.4

commit v4 on v3

--- a/solution.py
+++ b/solution.py
@@ -11,14 +11,21 @@
 def scan_sum(shard, axis, reverse):
     count = lax.axis_size(axis)
     total = shard
-    step = 1
-    while step < count:
-        if reverse:
-            pairs = [(source, source - step) for source in range(step, count)]
-        else:
-            pairs = [(source, source + step) for source in range(count - step)]
-        total = total + lax.ppermute(total, axis, pairs)
-        step *= 2
+    span = 1
+    while span < count:
+        moved = []
+        for hop in range(1, 4):
+            step = hop * span
+            if step >= count:
+                break
+            if reverse:
+                pairs = [(source, source - step) for source in range(step, count)]
+            else:
+                pairs = [(source, source + step) for source in range(count - step)]
+            moved.append(lax.ppermute(total, axis, pairs))
+        for part in moved:
+            total = total + part
+        span *= 4
     return total
 
 
@@ -61,7 +68,9 @@
     stacked = jnp.concatenate(blocks, 2)
     stacked = jnp.transpose(stacked, (1, 0, 2, 3)).reshape(-1, width)
     share = lax.psum_scatter(stacked, "cy", scatter_dimension=0, tiled=True)
-    share = lax.psum_scatter(share, "dp", scatter_dimension=0, tiled=True)
+    share = lax.all_to_all(
+        share.reshape(outer, -1, width), "dp", 0, 0, tiled=False
+    ).sum(0)
     return tuple(share[index * rows : (index + 1) * rows] for index in range(len(pairs)))
 
 
@@ -71,8 +80,7 @@
     factor = float(batch * tokens_here * owners) ** (-0.5)
     piece = w_query.shape[0] // lax.axis_size(CTX)
     across = gather_rows((w_query, w_key, w_value, w_out), piece)
-    full_query, full_key, full_value = spread_rows(across[:, :3])
-    (full_out,) = spread_rows(across[:, 3:])
+    full_query, full_key, full_value, full_out = spread_rows(across)
     second_wide = x_second.astype(jnp.float32)
     inv_rms = lax.rsqrt(jnp.mean(second_wide * second_wide, -1, keepdims=True) + 1e-06)
     normed_wide = second_wide * inv_rms

time: 510 us -> 481 us (0.943)
  the two profiles are of different devices: /device:TPU:1 before, /device:TPU:105 now
where the time goes in v4:
time: 481 us; the launch traced here: 479 us
  waiting for transfers between devices  282 us (59%)
  starting transfers between devices  71.7 us (15%)
  local copies, waits for them, and re-layouts  40 us (8%)
  blocking collectives  38 us (8%)
  matrix products  19.3 us (4%)
  between operations  14.6 us (3%)
  other arithmetic  13.5 us (3%)
    ppermute x14, waiting for transfers between devices, scan_sum(): moved.append(lax.ppermute(total, axis, pairs))  199 us
    all_gather x1, waiting for transfers between devices, spread_rows(): gathered = lax.all_gather(across, CTX, axis=0, tiled=False)  73.4 us
    ppermute x14, starting transfers between devices, scan_sum(): moved.append(lax.ppermute(total, axis, pairs))  63.4 us
    all_gather x1, blocking collectives, gather_rows(): across = lax.all_gather(joined, 'dp', axis=0, tiled=False)  38 us
    another operation x4, local copies, waits for them, and re-layouts, spread_rows(): return tuple((gathered[index].reshape(-1, width) for index in range(count)))  12.7 us
  transfers between devices with their start and end apart: 21, of which 15 were waited for; matrix products, arithmetic and copies ran while one was open for 9% of the time, Pallas kernels for 0%

profile of v4, /device:TPU:105, one launch (start us, length us, event | category | flops | bytes accessed | tf_op | source)
XLA Modules:
  0.0 479.5 jit_solution(560830048675181561)
XLA Ops:
  8.8 38.0 %all-gather = bf16[128,1024]{1,0:T(8,128)(2,1)S(1)} all-gather(bf16[16,1024]{1,0:T(8,128)(2,1)S(1)} %pad_maximum_fusion.1), channel_id=2, replica_groups=mesh['dp'=8,'cy'=16,'core'=2] {'dp'}, dimensions={0}, use_global_device_ids=true | all-gather | bytes 294912 | tf_op jit(solution)/shard_map/all_gather | solution.py:37
  49.0 73.4 %all-gather.3.cloned.1.call-done = bf16[32,8,4,4,1024]{4,3,0,1,2:T(4,128)(2,1)} async-done(((bf16[1,8,4,4,1024]{4,3,0,1,2:T(4,128)(2,1)}), bf16[32,8,4,4,1024]{4,3,0,1,2:T(4,128)(2,1)}) %all-gather.3.cloned.1.call-update) | async-done | bytes 8388624 | tf_op jit(solution)/shard_map/all_gather | solution.py:43
  122.4 6.9 %fusion.50 = (bf16[1,8,32,4,1024]{4,3,2,1,0:T(4,128)(2,1)}, bf16[1,8,32,4,1024]{4,3,2,1,0:T(4,128)(2,1)S(1)}, bf16[1,8,32,4,1024]{4,3,2,1,0:T(4,128)(2,1)}, bf16[1,8,32,4,1024]{4,3,2,1,0:T(4,128)(2,1)}) fusion(bf16[4,8,32,4,1024]{4,3,2,1,0:T(4,128)(2,1)} %bitcast.125), kind=kLoop, calls=%fused_computation.93 | loop fusion | bytes 16777216 | tf_op jit(solution)/shard_map/slice | solution.py:46
  131.4 2.5 reshape_squeeze.12
  138.8 3.8 collective-permute-start.2
  142.6 3.6 collective-permute-start.1
  146.2 2.6 collective-permute-start
  156.8 4.0 reshape_squeeze.13
  160.8 3.9 collective-permute-done.1
  164.7 6.5 %collective-permute-done = f32[1,8,128,128]{3,2,1,0:T(8,128)} collective-permute-done((f32[1,8,128,128]{3,2,1,0:T(8,128)S(1)}, f32[1,8,128,128]{3,2,1,0:T(8,128)}, u32[]{:S(2)}, u32[]{:S(2)}) %collective-permute-start) | collective-permute-done | bytes 524320 | tf_op jit(solution)/shard_map/ppermute | solution.py:25
  173.5 9.0 %collective-permute-start.5 = (f32[1,8,128,128]{3,2,1,0:T(8,128)}, f32[1,8,128,128]{3,2,1,0:T(8,128)}, u32[]{:S(2)}, u32[]{:S(2)}) collective-permute-start(f32[1,8,128,128]{3,2,1,0:T(8,128)} %add_add_fusion.3), channel_id=1, source_target_pairs={{0,12},{1,13},{2,14},{3,15},{4,16},{5,17},{6,18},{7,19},{8,20},{9,... | collective-permute-start | bytes 1572872 | tf_op jit(solution)/shard_map/ppermute | solution.py:25
  188.6 4.1 reshape_squeeze.15
  194.1 22.4 %collective-permute-done.5 = f32[1,8,128,128]{3,2,1,0:T(8,128)} collective-permute-done((f32[1,8,128,128]{3,2,1,0:T(8,128)}, f32[1,8,128,128]{3,2,1,0:T(8,128)}, u32[]{:S(2)}, u32[]{:S(2)}) %collective-permute-start.5) | collective-permute-done | bytes 524320 | tf_op jit(solution)/shard_map/ppermute | solution.py:25
  216.5 9.7 %collective-permute-done.3 = f32[1,8,128,128]{3,2,1,0:T(8,128)} collective-permute-done((f32[1,8,128,128]{3,2,1,0:T(8,128)}, f32[1,8,128,128]{3,2,1,0:T(8,128)}, u32[]{:S(2)}, u32[]{:S(2)}) %collective-permute-start.3) | collective-permute-done | bytes 524320 | tf_op jit(solution)/shard_map/ppermute | solution.py:25
  230.3 10.6 %collective-permute-done.6 = f32[1,8,128,128]{3,2,1,0:T(8,128)S(1)} collective-permute-done((f32[1,8,128,128]{3,2,1,0:T(8,128)S(1)}, f32[1,8,128,128]{3,2,1,0:T(8,128)S(1)}, u32[]{:S(2)}, u32[]{:S(2)}) %collective-permute-start.6) | collective-permute-done | bytes 524320 | tf_op jit(solution)/shard_map/ppermute | solution.py:25
  246.1 2.9 convolution_multiply_fusion
  249.0 2.9 reshape.236
  251.9 2.8 convolution_multiply_fusion.1
  254.7 2.9 reshape.234
  257.6 3.3 pad_maximum_fusion
  260.9 2.3 copy.56
  264.4 3.2 collective-permute-start.9
  269.5 5.4 %collective-permute-start.7 = (f32[1,8,128,128]{3,2,1,0:T(8,128)S(1)}, f32[1,8,128,128]{3,2,1,0:T(8,128)S(1)}, u32[]{:S(2)}, u32[]{:S(2)}) collective-permute-start(f32[1,8,128,128]{3,2,1,0:T(8,128)S(1)} %convolution_bitcast_fusion), channel_id=1, source_target_pairs={{1,0},{2,1},{3,2},{4,3},{5,4},{6,5},{7,6},{8,7},{9,8},{10,9},{11,1... | collective-permute-start | bytes 1572872 | tf_op jit(solution)/shard_map/ppermute | solution.py:25
  274.9 20.3 %collective-permute-done.9 = f32[1,8,128,128]{3,2,1,0:T(8,128)S(1)} collective-permute-done((f32[1,8,128,128]{3,2,1,0:T(8,128)S(1)}, f32[1,8,128,128]{3,2,1,0:T(8,128)S(1)}, u32[]{:S(2)}, u32[]{:S(2)}) %collective-permute-start.9) | collective-permute-done | bytes 524320 | tf_op jit(solution)/shard_map/ppermute | solution.py:25
  295.2 18.5 %collective-permute-done.8 = f32[1,8,128,128]{3,2,1,0:T(8,128)S(1)} collective-permute-done((f32[1,8,128,128]{3,2,1,0:T(8,128)S(1)}, f32[1,8,128,128]{3,2,1,0:T(8,128)S(1)}, u32[]{:S(2)}, u32[]{:S(2)}) %collective-permute-start.8) | collective-permute-done | bytes 524320 | tf_op jit(solution)/shard_map/ppermute | solution.py:25
  313.7 15.3 %collective-permute-done.7 = f32[1,8,128,128]{3,2,1,0:T(8,128)S(1)} collective-permute-done((f32[1,8,128,128]{3,2,1,0:T(8,128)S(1)}, f32[1,8,128,128]{3,2,1,0:T(8,128)S(1)}, u32[]{:S(2)}, u32[]{:S(2)}) %collective-permute-start.7) | collective-permute-done | bytes 524320 | tf_op jit(solution)/shard_map/ppermute | solution.py:25
  329.1 23.7 %collective-permute-start.12 = (f32[1,8,128,128]{3,2,1,0:T(8,128)S(1)}, f32[1,8,128,128]{3,2,1,0:T(8,128)S(1)}, u32[]{:S(2)}, u32[]{:S(2)}) collective-permute-start(f32[1,8,128,128]{3,2,1,0:T(8,128)S(1)} %add_add_fusion.1), channel_id=1, source_target_pairs={{12,0},{13,1},{14,2},{15,3},{16,4},{17,5},{18,6},{19,7},{20,8},{21... | collective-permute-start | bytes 1572872 | tf_op jit(solution)/shard_map/ppermute | solution.py:25
  357.8 21.4 %collective-permute-done.12 = f32[1,8,128,128]{3,2,1,0:T(8,128)S(1)} collective-permute-done((f32[1,8,128,128]{3,2,1,0:T(8,128)S(1)}, f32[1,8,128,128]{3,2,1,0:T(8,128)S(1)}, u32[]{:S(2)}, u32[]{:S(2)}) %collective-permute-start.12) | collective-permute-done | bytes 524320 | tf_op jit(solution)/shard_map/ppermute | solution.py:25
  379.2 57.3 %collective-permute-done.10 = f32[1,8,128,128]{3,2,1,0:T(8,128)S(1)} collective-permute-done((f32[1,8,128,128]{3,2,1,0:T(8,128)S(1)}, f32[1,8,128,128]{3,2,1,0:T(8,128)S(1)}, u32[]{:S(2)}, u32[]{:S(2)}) %collective-permute-start.10) | collective-permute-done | bytes 524320 | tf_op jit(solution)/shard_map/ppermute | solution.py:25
  439.4 12.9 %collective-permute-done.13 = f32[1,8,128,128]{3,2,1,0:T(8,128)S(1)} collective-permute-done((f32[1,8,128,128]{3,2,1,0:T(8,128)S(1)}, f32[1,8,128,128]{3,2,1,0:T(8,128)S(1)}, u32[]{:S(2)}, u32[]{:S(2)}) %collective-permute-start.13) | collective-permute-done | bytes 524320 | tf_op jit(solution)/shard_map/ppermute | solution.py:25
  454.8 6.7 %all-to-all-start = ((f32[8,8,1024]{2,1,0:T(8,128)}), f32[8,8,1024]{2,1,0:T(8,128)S(1)}, u32[]{:S(2)}, u32[]{:S(2)}) async-start(f32[8,8,1024]{2,1,0:T(8,128)} %bitcast.145), calls=%async_computation.1 | async-start | bytes 524288 | tf_op jit(solution)/shard_map/all_to_all | solution.py:71
  462.5 9.5 %all-to-all-done = f32[8,8,1024]{2,1,0:T(8,128)S(1)} async-done(((f32[8,8,1024]{2,1,0:T(8,128)}), f32[8,8,1024]{2,1,0:T(8,128)S(1)}, u32[]{:S(2)}, u32[]{:S(2)}) %all-to-all-start) | async-done | bytes 262176 | tf_op jit(solution)/shard_map/all_to_all | solution.py:71
  (117 shorter events, 52.7 us)
Async XLA Ops:
  7.2 41.8 %copy-start.5 = (bf16[1,128,1024]{2,1,0:T(8,128)(2,1)S(1)}, bf16[1,128,1024]{2,1,0:T(8,128)(2,1)}, u32[]{:S(2)}) copy-start(bf16[1,128,1024]{2,1,0:T(8,128)(2,1)} %param.9) | copy-start | bytes 786436
  7.2 115.2 %all-gather.3.cloned.1.call-start = ((), (), s32[]{:S(2)}) async-start(), calls=%async_computation.2 | async-start | bytes 8650752 | tf_op jit(solution)/shard_map/all_gather | solution.py:43
  47.8 407.0 %reduce-scatter.2.cloned.1.call-start = ((), (), s32[]{:S(2)}) async-start(), calls=%async_computation.3 | async-start | bytes 4456448 | tf_op jit(solution)/shard_map/reduce_scatter | solution.py:70
  138.8 22.1 %collective-permute-start.2 = (f32[1,8,128,128]{3,2,1,0:T(8,128)S(1)}, f32[1,8,128,128]{3,2,1,0:T(8,128)}, u32[]{:S(2)}, u32[]{:S(2)}) collective-permute-start(f32[1,8,128,128]{3,2,1,0:T(8,128)S(1)} %convolution_bitcast_fusion.2), channel_id=1, source_target_pairs={{0,3},{1,4},{2,5},{3,6},{4,7},{5,8},{6,9},{7,10},{8,11},{9,12},{10... | collective-permute-start | bytes 1572872 | tf_op jit(solution)/shard_map/ppermute | solution.py:25
  142.6 22.1 %collective-permute-start.1 = (f32[1,8,128,128]{3,2,1,0:T(8,128)S(1)}, f32[1,8,128,128]{3,2,1,0:T(8,128)}, u32[]{:S(2)}, u32[]{:S(2)}) collective-permute-start(f32[1,8,128,128]{3,2,1,0:T(8,128)S(1)} %convolution_bitcast_fusion.2), channel_id=1, source_target_pairs={{0,2},{1,3},{2,4},{3,5},{4,6},{5,7},{6,8},{7,9},{8,10},{9,11},{10,... | collective-permute-start | bytes 1572872 | tf_op jit(solution)/shard_map/ppermute | solution.py:25
  146.2 25.0 %collective-permute-start = (f32[1,8,128,128]{3,2,1,0:T(8,128)S(1)}, f32[1,8,128,128]{3,2,1,0:T(8,128)}, u32[]{:S(2)}, u32[]{:S(2)}) collective-permute-start(f32[1,8,128,128]{3,2,1,0:T(8,128)S(1)} %convolution_bitcast_fusion.2), channel_id=1, source_target_pairs={{0,1},{1,2},{2,3},{3,4},{4,5},{5,6},{6,7},{7,8},{8,9},{9,10},{10,1... | collective-permute-start | bytes 1572872 | tf_op jit(solution)/shard_map/ppermute | solution.py:25
  149.6 1.9 collective-permute-start.14
  149.6 96.4 %collective-permute-start.17 = (bf16[128,1024]{1,0:T(8,128)(2,1)}, bf16[128,1024]{1,0:T(8,128)(2,1)}, u32[]{:S(2)}, u32[]{:S(2)}) collective-permute-start(bf16[128,1024]{1,0:T(8,128)(2,1)} %bitcast.143), channel_id=1, source_target_pairs={{0,1},{1,0},{2,3},{3,2},{4,5},{5,4},{6,7},{7,6},{8,9},{9,8},{10,11... | collective-permute-start | bytes 786440 | tf_op jit(solution)/shard_map/ppermute | solution.py:57
  173.5 43.0 %collective-permute-start.5 = (f32[1,8,128,128]{3,2,1,0:T(8,128)}, f32[1,8,128,128]{3,2,1,0:T(8,128)}, u32[]{:S(2)}, u32[]{:S(2)}) collective-permute-start(f32[1,8,128,128]{3,2,1,0:T(8,128)} %add_add_fusion.3), channel_id=1, source_target_pairs={{0,12},{1,13},{2,14},{3,15},{4,16},{5,17},{6,18},{7,19},{8,20},{9,... | collective-permute-start | bytes 1572872 | tf_op jit(solution)/shard_map/ppermute | solution.py:25
  182.5 34.1 %collective-permute-start.4 = (f32[1,8,128,128]{3,2,1,0:T(8,128)}, f32[1,8,128,128]{3,2,1,0:T(8,128)}, u32[]{:S(2)}, u32[]{:S(2)}) collective-permute-start(f32[1,8,128,128]{3,2,1,0:T(8,128)} %add_add_fusion.3), channel_id=1, source_target_pairs={{0,8},{1,9},{2,10},{3,11},{4,12},{5,13},{6,14},{7,15},{8,16},{9,17... | collective-permute-start | bytes 1572872 | tf_op jit(solution)/shard_map/ppermute | solution.py:25
  184.4 41.9 %collective-permute-start.3 = (f32[1,8,128,128]{3,2,1,0:T(8,128)}, f32[1,8,128,128]{3,2,1,0:T(8,128)}, u32[]{:S(2)}, u32[]{:S(2)}) collective-permute-start(f32[1,8,128,128]{3,2,1,0:T(8,128)} %add_add_fusion.3), channel_id=1, source_target_pairs={{0,4},{1,5},{2,6},{3,7},{4,8},{5,9},{6,10},{7,11},{8,12},{9,13},{1... | collective-permute-start | bytes 1572872 | tf_op jit(solution)/shard_map/ppermute | solution.py:25
  188.6 52.4 %copy-start.6 = (bf16[128,1024]{0,1:T(8,128)(2,1)}, bf16[128,1024]{0,1:T(8,128)(2,1)S(1)}, u32[]{:S(2)}) copy-start(bf16[128,1024]{0,1:T(8,128)(2,1)S(1)} %copy.57) | copy-start | bytes 786436
  192.7 36.8 %copy-start.3 = (bf16[1024,1024]{1,0:T(8,128)(2,1)S(1)}, bf16[1024,1024]{1,0:T(8,128)(2,1)}, u32[]{:S(2)}) copy-start(bf16[1024,1024]{1,0:T(8,128)(2,1)} %reshape_squeeze.15) | copy-start | bytes 6291460
  192.7 36.8 %copy-start.17 = (bf16[1,128,1024]{2,1,0:T(8,128)(2,1)S(1)}, bf16[1,128,1024]{2,1,0:T(8,128)(2,1)}, u32[]{:S(2)}) copy-start(bf16[1,128,1024]{2,1,0:T(8,128)(2,1)} %param.10) | copy-start | bytes 786436
  194.1 36.1 %copy-start.13 = (bf16[8,128,128]{2,1,0:T(8,128)(2,1)}, bf16[8,128,128]{2,1,0:T(8,128)(2,1)S(1)}, u32[]{:S(2)}) copy-start(bf16[8,128,128]{2,1,0:T(8,128)(2,1)S(1)} %fusion.3) | copy-start | bytes 786436
  227.9 13.0 %collective-permute-start.6 = (f32[1,8,128,128]{3,2,1,0:T(8,128)S(1)}, f32[1,8,128,128]{3,2,1,0:T(8,128)S(1)}, u32[]{:S(2)}, u32[]{:S(2)}) collective-permute-start(f32[1,8,128,128]{3,2,1,0:T(8,128)S(1)} %add_add_fusion.2), channel_id=1, source_target_pairs={{0,16},{1,17},{2,18},{3,19},{4,20},{5,21},{6,22},{7,23},{8,24},{9,... | collective-permute-start | bytes 1572872 | tf_op jit(solution)/shard_map/ppermute | solution.py:25
  241.9 1.6 collective-permute-start.16
  242.8 9.0 %collective-permute-start.15 = (bf16[128,1024]{0,1:T(8,128)(2,1)S(1)}, bf16[128,1024]{0,1:T(8,128)(2,1)}, u32[]{:S(2)}, u32[]{:S(2)}) collective-permute-start(bf16[128,1024]{0,1:T(8,128)(2,1)S(1)} %bitcast.135), channel_id=1, source_target_pairs={{0,1},{1,0},{2,3},{3,2},{4,5},{5,4},{6,7},{7,6},{8,9},{9,8},{10,11... | collective-permute-start | bytes 786440 | tf_op jit(solution)/shard_map/ppermute | solution.py:57
  264.1 92.6 %copy-start.16 = (bf16[8,128,128]{2,1,0:T(8,128)(2,1)S(1)}, bf16[8,128,128]{2,1,0:T(8,128)(2,1)}, u32[]{:S(2)}) copy-start(bf16[8,128,128]{2,1,0:T(8,128)(2,1)} %copy-done.15) | copy-start | bytes 786436
  264.4 92.5 %copy-start.1 = (bf16[1024,1024]{1,0:T(8,128)(2,1)S(1)}, bf16[1024,1024]{1,0:T(8,128)(2,1)}, u32[]{:S(2)}) copy-start(bf16[1024,1024]{1,0:T(8,128)(2,1)} %reshape_squeeze.13) | copy-start | bytes 6291460
  264.4 92.5 %copy-start.12 = (bf16[8,128,128]{2,1,0:T(8,128)(2,1)S(1)}, bf16[8,128,128]{2,1,0:T(8,128)(2,1)}, u32[]{:S(2)}) copy-start(bf16[8,128,128]{2,1,0:T(8,128)(2,1)} %copy-done.11) | copy-start | bytes 786436
  264.4 30.8 %collective-permute-start.9 = (f32[1,8,128,128]{3,2,1,0:T(8,128)S(1)}, f32[1,8,128,128]{3,2,1,0:T(8,128)S(1)}, u32[]{:S(2)}, u32[]{:S(2)}) collective-permute-start(f32[1,8,128,128]{3,2,1,0:T(8,128)S(1)} %convolution_bitcast_fusion), channel_id=1, source_target_pairs={{3,0},{4,1},{5,2},{6,3},{7,4},{8,5},{9,6},{10,7},{11,8},{12,9},{13... | collective-permute-start | bytes 1572872 | tf_op jit(solution)/shard_map/ppermute | solution.py:25
  267.6 46.1 %collective-permute-start.8 = (f32[1,8,128,128]{3,2,1,0:T(8,128)S(1)}, f32[1,8,128,128]{3,2,1,0:T(8,128)S(1)}, u32[]{:S(2)}, u32[]{:S(2)}) collective-permute-start(f32[1,8,128,128]{3,2,1,0:T(8,128)S(1)} %convolution_bitcast_fusion), channel_id=1, source_target_pairs={{2,0},{3,1},{4,2},{5,3},{6,4},{7,5},{8,6},{9,7},{10,8},{11,9},{12,... | collective-permute-start | bytes 1572872 | tf_op jit(solution)/shard_map/ppermute | solution.py:25
  269.5 59.5 %collective-permute-start.7 = (f32[1,8,128,128]{3,2,1,0:T(8,128)S(1)}, f32[1,8,128,128]{3,2,1,0:T(8,128)S(1)}, u32[]{:S(2)}, u32[]{:S(2)}) collective-permute-start(f32[1,8,128,128]{3,2,1,0:T(8,128)S(1)} %convolution_bitcast_fusion), channel_id=1, source_target_pairs={{1,0},{2,1},{3,2},{4,3},{5,4},{6,5},{7,6},{8,7},{9,8},{10,9},{11,1... | collective-permute-start | bytes 1572872 | tf_op jit(solution)/shard_map/ppermute | solution.py:25
  329.1 50.1 %collective-permute-start.12 = (f32[1,8,128,128]{3,2,1,0:T(8,128)S(1)}, f32[1,8,128,128]{3,2,1,0:T(8,128)S(1)}, u32[]{:S(2)}, u32[]{:S(2)}) collective-permute-start(f32[1,8,128,128]{3,2,1,0:T(8,128)S(1)} %add_add_fusion.1), channel_id=1, source_target_pairs={{12,0},{13,1},{14,2},{15,3},{16,4},{17,5},{18,6},{19,7},{20,8},{21... | collective-permute-start | bytes 1572872 | tf_op jit(solution)/shard_map/ppermute | solution.py:25
  352.8 26.4 %collective-permute-start.11 = (f32[1,8,128,128]{3,2,1,0:T(8,128)S(1)}, f32[1,8,128,128]{3,2,1,0:T(8,128)S(1)}, u32[]{:S(2)}, u32[]{:S(2)}) collective-permute-start(f32[1,8,128,128]{3,2,1,0:T(8,128)S(1)} %add_add_fusion.1), channel_id=1, source_target_pairs={{8,0},{9,1},{10,2},{11,3},{12,4},{13,5},{14,6},{15,7},{16,8},{17,9... | collective-permute-start | bytes 1572872 | tf_op jit(solution)/shard_map/ppermute | solution.py:25
  354.7 81.8 %collective-permute-start.10 = (f32[1,8,128,128]{3,2,1,0:T(8,128)S(1)}, f32[1,8,128,128]{3,2,1,0:T(8,128)S(1)}, u32[]{:S(2)}, u32[]{:S(2)}) collective-permute-start(f32[1,8,128,128]{3,2,1,0:T(8,128)S(1)} %add_add_fusion.1), channel_id=1, source_target_pairs={{4,0},{5,1},{6,2},{7,3},{8,4},{9,5},{10,6},{11,7},{12,8},{13,9},{1... | collective-permute-start | bytes 1572872 | tf_op jit(solution)/shard_map/ppermute | solution.py:25
  356.9 81.0 %copy-start.14 = (bf16[8,128,128]{2,1,0:T(8,128)(2,1)S(1)}, bf16[8,128,128]{2,1,0:T(8,128)(2,1)}, u32[]{:S(2)}) copy-start(bf16[8,128,128]{2,1,0:T(8,128)(2,1)} %copy-done.13) | copy-start | bytes 786436
  357.8 80.4 %copy-start.4 = (bf16[1024,1024]{1,0:T(8,128)(2,1)S(1)}, bf16[1024,1024]{1,0:T(8,128)(2,1)}, u32[]{:S(2)}) copy-start(bf16[1024,1024]{1,0:T(8,128)(2,1)} %reshape_squeeze.15) | copy-start | bytes 6291460
  357.8 80.4 %copy-start.19 = (bf16[1,128,1024]{2,1,0:T(8,128)(2,1)S(1)}, bf16[1,128,1024]{2,1,0:T(8,128)(2,1)}, u32[]{:S(2)}) copy-start(bf16[1,128,1024]{2,1,0:T(8,128)(2,1)} %param.8) | copy-start | bytes 786436
  436.6 15.6 %collective-permute-start.13 = (f32[1,8,128,128]{3,2,1,0:T(8,128)S(1)}, f32[1,8,128,128]{3,2,1,0:T(8,128)S(1)}, u32[]{:S(2)}, u32[]{:S(2)}) collective-permute-start(f32[1,8,128,128]{3,2,1,0:T(8,128)S(1)} %add_add_fusion), channel_id=1, source_target_pairs={{16,0},{17,1},{18,2},{19,3},{20,4},{21,5},{22,6},{23,7},{24,8},{25... | collective-permute-start | bytes 1572872 | tf_op jit(solution)/shard_map/ppermute | solution.py:25
  454.8 17.2 %all-to-all-start = ((f32[8,8,1024]{2,1,0:T(8,128)}), f32[8,8,1024]{2,1,0:T(8,128)S(1)}, u32[]{:S(2)}, u32[]{:S(2)}) async-start(f32[8,8,1024]{2,1,0:T(8,128)} %bitcast.145), calls=%async_computation.1 | async-start | bytes 524288 | tf_op jit(solution)/shard_map/all_to_all | solution.py:71
  (9 other events, 73.5 us)
Sparse Core Ops, SparseCore 0:
  47.9 74.4 all-gather.2
  263.3 169.7 reduce-scatter.1

commit v5 on v4

--- a/solution.py
+++ b/solution.py
@@ -8,25 +8,13 @@
 CTX = ("cy", "core")
 
 
-def scan_sum(shard, axis, reverse):
+def state_sum(shard, axis, later):
     count = lax.axis_size(axis)
-    total = shard
-    span = 1
-    while span < count:
-        moved = []
-        for hop in range(1, 4):
-            step = hop * span
-            if step >= count:
-                break
-            if reverse:
-                pairs = [(source, source - step) for source in range(step, count)]
-            else:
-                pairs = [(source, source + step) for source in range(count - step)]
-            moved.append(lax.ppermute(total, axis, pairs))
-        for part in moved:
-            total = total + part
-        span *= 4
-    return total
+    place = lax.axis_index(axis)
+    gathered = lax.all_gather(shard, axis, axis=0, tiled=False)
+    blocks = lax.broadcasted_iota(jnp.int32, (count,) + (1,) * shard.ndim, 0)
+    chosen = blocks > place if later else blocks < place
+    return jnp.sum(jnp.where(chosen, gathered, 0.0), axis=0)
 
 
 def gather_rows(weights, piece):
@@ -67,7 +55,9 @@
     rows = blocks[0].shape[2]
     stacked = jnp.concatenate(blocks, 2)
     stacked = jnp.transpose(stacked, (1, 0, 2, 3)).reshape(-1, width)
-    share = lax.psum_scatter(stacked, "cy", scatter_dimension=0, tiled=True)
+    share = lax.all_to_all(
+        stacked.reshape(chips, -1, width), "cy", 0, 0, tiled=False
+    ).sum(0)
     share = lax.all_to_all(
         share.reshape(outer, -1, width), "dp", 0, 0, tiled=False
     ).sum(0)
@@ -96,7 +86,7 @@
     local_state = jnp.einsum(
         "bthe,bthf->bhef", key_rows, values, preferred_element_type=jnp.float32
     )
-    before = (scan_sum(local_state, CTX, False) - local_state).astype(jnp.bfloat16)
+    before = state_sum(local_state, CTX, False).astype(jnp.bfloat16)
     causal = jnp.tril(jnp.ones((tokens_here, tokens_here), dtype=bool))
     scores = jnp.einsum("bthe,bshe->bhts", queries, key_rows, preferred_element_type=jnp.float32)
     scores = jnp.where(causal[None, None], scores, 0.0).astype(jnp.bfloat16)
@@ -120,7 +110,7 @@
     grad_local = jnp.einsum(
         "bthe,bthf->bhef", queries, grad_mixed, preferred_element_type=jnp.float32
     )
-    after_state = (scan_sum(grad_local, CTX, True) - grad_local).astype(jnp.bfloat16)
+    after_state = state_sum(grad_local, CTX, True).astype(jnp.bfloat16)
     query_grad = jnp.einsum(
         "bhts,bshe->bthe", score_grad, key_rows, preferred_element_type=jnp.float32
     )

time: 481 us -> 472 us (0.981)
  the two profiles are of different devices: /device:TPU:105 before, /device:TPU:1 now
where the time goes in v5:
time: 472 us; the launch traced here: 467 us
  waiting for transfers between devices  292 us (62%)
  blocking collectives  40.7 us (9%)
  local copies, waits for them, and re-layouts  39.6 us (8%)
  matrix products  30.4 us (6%)
  other arithmetic  30.1 us (6%)
  starting transfers between devices  19.7 us (4%)
  between operations  14.1 us (3%)
    all_gather x2, waiting for transfers between devices, state_sum(): gathered = lax.all_gather(shard, axis, axis=0, tiled=False)  116 us
    all_to_all x1, waiting for transfers between devices, weight_grads(): lax.all_to_all(stacked.reshape(chips, -1, width), 'cy', 0, 0, tiled=False)  93.3 us
    all_gather x1, waiting for transfers between devices, spread_rows(): gathered = lax.all_gather(across, CTX, axis=0, tiled=False)  74.8 us
    all_gather x1, blocking collectives, gather_rows(): across = lax.all_gather(joined, 'dp', axis=0, tiled=False)  40.7 us
    reduce_sum x2, other arithmetic, state_sum(): return jnp.sum(jnp.where(chosen, gathered, 0.0), axis=0)  15.7 us
    another operation x4, local copies, waits for them, and re-layouts, spread_rows(): return tuple((gathered[index].reshape(-1, width) for index in range(count)))  12.8 us
    all_to_all x1, starting transfers between devices, weight_grads(): lax.all_to_all(share.reshape(outer, -1, width), 'dp', 0, 0, tiled=False)  11.4 us
  transfers between devices with their start and end apart: 9, of which 7 were waited for; matrix products, arithmetic and copies ran while one was open for 12% of the time, Pallas kernels for 0%

profile of v5, /device:TPU:1, one launch (start us, length us, event | category | flops | bytes accessed | tf_op | source)
XLA Modules:
  0.0 466.7 jit_solution(9594058674873507127)
XLA Ops:
  8.8 40.7 %all-gather = bf16[128,1024]{1,0:T(8,128)(2,1)S(1)} all-gather(bf16[16,1024]{1,0:T(8,128)(2,1)S(1)} %pad_maximum_fusion.1), channel_id=2, replica_groups=mesh['dp'=8,'cy'=16,'core'=2] {'dp'}, dimensions={0}, use_global_device_ids=true | all-gather | bytes 294912 | tf_op jit(solution)/shard_map/all_gather | solution.py:25
  51.7 74.8 %all-gather.7.cloned.1.call-done = bf16[32,8,4,4,1024]{4,3,0,1,2:T(4,128)(2,1)} async-done(((bf16[1,8,4,4,1024]{4,3,0,1,2:T(4,128)(2,1)}), bf16[32,8,4,4,1024]{4,3,0,1,2:T(4,128)(2,1)}) %all-gather.7.cloned.1.call-update) | async-done | bytes 8388624 | tf_op jit(solution)/shard_map/all_gather | solution.py:31
  126.5 7.2 %fusion.53 = (bf16[1,8,32,4,1024]{4,3,2,1,0:T(4,128)(2,1)}, bf16[1,8,32,4,1024]{4,3,2,1,0:T(4,128)(2,1)S(1)}, bf16[1,8,32,4,1024]{4,3,2,1,0:T(4,128)(2,1)}, bf16[1,8,32,4,1024]{4,3,2,1,0:T(4,128)(2,1)}) fusion(bf16[4,8,32,4,1024]{4,3,2,1,0:T(4,128)(2,1)} %bitcast.121), kind=kLoop, calls=%fused_computation.93 | loop fusion | bytes 16777216 | tf_op jit(solution)/shard_map/slice | solution.py:34
  133.7 2.1 reshape_squeeze.14
  135.8 2.5 reshape_squeeze.12
  138.4 2.0 convolution_convert_fusion
  141.6 1.1 copy.77
  143.9 4.0 reshape_squeeze.13
  148.0 2.7 convolution_convert_fusion.1
  151.8 4.1 reshape_squeeze.15
  158.1 2.3 fusion.48
  160.5 82.0 %all-gather.9.cloned.1.call-done = f32[256,128,128]{2,1,0:T(8,128)} async-done(((f32[8,128,128]{2,1,0:T(8,128)}), f32[256,128,128]{2,1,0:T(8,128)}) %all-gather.9.cloned.1.call-update) | async-done | bytes 16777232 | tf_op jit(solution)/shard_map/all_gather | solution.py:14
  242.5 7.8 %select_reduce_fusion.1 = bf16[8,128,128]{2,1,0:T(8,128)(2,1)S(1)} fusion(f32[32,1,8,128,128]{4,3,2,0,1:T(8,128)} %bitcast.120, pred[32]{0:T(512)(128)(4,1)S(1)} %iota_compare_fusion.2), kind=kLoop, calls=%fused_computation.1 | loop fusion | flops 8257536 | bytes 17039392 | tf_op jit(solution)/shard_map/reduce_sum | solution.py:17
  256.1 1.8 copy.92
  257.8 1.8 fusion.27
  259.6 1.7 reshape.251
  264.0 2.9 convolution_multiply_fusion
  267.0 2.9 reshape.254
  269.9 2.8 convolution_multiply_fusion.1
  272.7 2.9 reshape.252
  275.6 5.3 %copy_bitcast_fusion = f32[16,64,1024]{2,1,0:T(8,128)} fusion(f32[8,16,4,1024]{3,2,1,0:T(4,128)} %reshape.254, f32[8,16,4,1024]{3,2,1,0:T(4,128)} %reshape.252), kind=kLoop, calls=%fused_computation.3 | loop fusion | flops 1048576 | bytes 8388608 | tf_op jit(solution)/shard_map/reshape;reshape | solution.py:59
  280.9 6.9 %all-to-all-start = ((f32[16,64,1024]{2,1,0:T(8,128)}), f32[16,64,1024]{2,1,0:T(8,128)}, u32[]{:S(2)}, u32[]{:S(2)}) async-start(f32[16,64,1024]{2,1,0:T(8,128)} %copy_bitcast_fusion), calls=%async_computation | async-start | bytes 8388608 | tf_op jit(solution)/shard_map/all_to_all | solution.py:58
  287.8 2.0 fusion.57
  289.8 3.3 fusion.56
  293.1 93.3 %all-to-all-done = f32[16,64,1024]{2,1,0:T(8,128)} async-done(((f32[16,64,1024]{2,1,0:T(8,128)}), f32[16,64,1024]{2,1,0:T(8,128)}, u32[]{:S(2)}, u32[]{:S(2)}) %all-to-all-start) | async-done | bytes 4194336 | tf_op jit(solution)/shard_map/all_to_all | solution.py:58
  386.4 3.2 reduce_sum.78
  389.6 11.4 %all-to-all-start.1 = ((f32[8,8,1024]{2,1,0:T(8,128)}), f32[8,8,1024]{2,1,0:T(8,128)S(1)}, u32[]{:S(2)}, u32[]{:S(2)}) async-start(f32[8,8,1024]{2,1,0:T(8,128)} %bitcast.32), calls=%async_computation.1 | async-start | bytes 524288 | tf_op jit(solution)/shard_map/all_to_all | solution.py:61
  401.0 2.0 fusion.59
  403.1 2.8 fusion.5
  405.8 7.1 %all-to-all-done.1 = f32[8,8,1024]{2,1,0:T(8,128)S(1)} async-done(((f32[8,8,1024]{2,1,0:T(8,128)}), f32[8,8,1024]{2,1,0:T(8,128)S(1)}, u32[]{:S(2)}, u32[]{:S(2)}) %all-to-all-start.1) | async-done | bytes 262176 | tf_op jit(solution)/shard_map/all_to_all | solution.py:61
  413.6 34.3 %all-gather.11.cloned.1.call-done = f32[256,128,128]{2,1,0:T(8,128)} async-done(((f32[8,128,128]{2,1,0:T(8,128)}), f32[256,128,128]{2,1,0:T(8,128)}) %all-gather.11.cloned.1.call-update) | async-done | bytes 16777232 | tf_op jit(solution)/shard_map/all_gather | solution.py:14
  447.9 7.8 %select_reduce_fusion = bf16[8,128,128]{2,1,0:T(8,128)(2,1)S(1)} fusion(f32[32,1,8,128,128]{4,3,2,0,1:T(8,128)} %bitcast.119, pred[32]{0:T(512)(128)(4,1)S(1)} %iota_compare_fusion.1), kind=kLoop, calls=%fused_computation | loop fusion | flops 8257536 | bytes 17039392 | tf_op jit(solution)/shard_map/reduce_sum | solution.py:17
  (102 shorter events, 22.8 us)
Async XLA Ops:
  7.2 44.4 %copy-start.1 = (bf16[1,128,1024]{2,1,0:T(8,128)(2,1)S(1)}, bf16[1,128,1024]{2,1,0:T(8,128)(2,1)}, u32[]{:S(2)}) copy-start(bf16[1,128,1024]{2,1,0:T(8,128)(2,1)} %param.9) | copy-start | bytes 786436
  7.2 119.3 %all-gather.7.cloned.1.call-start = ((), (), s32[]{:S(2)}) async-start(), calls=%async_computation.2 | async-start | bytes 8650752 | tf_op jit(solution)/shard_map/all_gather | solution.py:31
  50.4 192.1 %all-gather.9.cloned.1.call-start = ((), (), s32[]{:S(2)}) async-start(), calls=%async_computation.3 | async-start | bytes 17301504 | tf_op jit(solution)/shard_map/all_gather | solution.py:14
  140.4 15.5 %copy-start.9 = (bf16[128,1024]{1,0:T(8,128)(2,1)}, bf16[128,1024]{1,0:T(8,128)(2,1)S(1)}, u32[]{:S(2)}) copy-start(bf16[128,1024]{1,0:T(8,128)(2,1)S(1)} %convolution_convert_fusion) | copy-start | bytes 786436
  142.8 5.2 %copy-start.11 = (bf16[128,8,128]{0,2,1:T(8,128)(2,1)}, bf16[128,8,128]{0,2,1:T(8,128)(2,1)S(1)}, u32[]{:S(2)}) copy-start(bf16[128,8,128]{0,2,1:T(8,128)(2,1)S(1)} %copy.77) | copy-start | bytes 786436
  143.8 304.0 %all-gather.11.cloned.1.call-start = ((), (), s32[]{:S(2)}) async-start(), calls=%async_computation.4 | async-start | bytes 17301504 | tf_op jit(solution)/shard_map/all_gather | solution.py:14
  151.8 4.1 copy-start.4
  242.5 7.8 %copy-start.5 = (bf16[128,1024]{0,1:T(8,128)(2,1)S(1)}, bf16[128,1024]{0,1:T(8,128)(2,1)}, u32[]{:S(2)}) copy-start(bf16[128,1024]{0,1:T(8,128)(2,1)} %copy-done.4) | copy-start | bytes 786436
  242.5 7.8 %copy-start.17 = (f32[8,128,128]{2,1,0:T(8,128)S(1)}, f32[8,128,128]{2,1,0:T(8,128)}, u32[]{:S(2)}) copy-start(f32[8,128,128]{2,1,0:T(8,128)} %fusion.30) | copy-start | bytes 1572868
  250.3 1.3 copy-start.7
  253.4 8.3 %copy-start.3 = (bf16[128,8,128]{0,2,1:T(8,128)(2,1)S(1)}, bf16[128,8,128]{0,2,1:T(8,128)(2,1)}, u32[]{:S(2)}) copy-start(bf16[128,8,128]{0,2,1:T(8,128)(2,1)} %copy-done.2) | copy-start | bytes 786436
  254.2 1.9 collective-permute-start
  254.5 9.6 %collective-permute-start.3 = (bf16[128,1024]{1,0:T(8,128)(2,1)}, bf16[128,1024]{1,0:T(8,128)(2,1)}, u32[]{:S(2)}, u32[]{:S(2)}) collective-permute-start(bf16[128,1024]{1,0:T(8,128)(2,1)} %bitcast.139), channel_id=1, source_target_pairs={{0,1},{1,0},{2,3},{3,2},{4,5},{5,4},{6,7},{7,6},{8,9},{9,8},{10,11... | collective-permute-start | bytes 786440 | tf_op jit(solution)/shard_map/ppermute | solution.py:45
  254.7 7.6 %copy-start.8 = (bf16[8,128,128]{2,1,0:T(8,128)(2,1)S(1)}, bf16[8,128,128]{2,1,0:T(8,128)(2,1)}, u32[]{:S(2)}) copy-start(bf16[8,128,128]{2,1,0:T(8,128)(2,1)} %copy-done.7) | copy-start | bytes 786436
  255.6 6.4 %copy-start.12 = (bf16[128,8,128]{0,2,1:T(8,128)(2,1)S(1)}, bf16[128,8,128]{0,2,1:T(8,128)(2,1)}, u32[]{:S(2)}) copy-start(bf16[128,8,128]{0,2,1:T(8,128)(2,1)} %copy-done.11) | copy-start | bytes 786436
  261.4 1.8 copy-start.13
  261.4 1.7 collective-permute-start.2
  262.0 1.1 copy-start.22
  262.6 7.3 %copy-start.15 = (bf16[8,128,128]{2,1,0:T(8,128)(2,1)}, bf16[8,128,128]{2,1,0:T(8,128)(2,1)S(1)}, u32[]{:S(2)}) copy-start(bf16[8,128,128]{2,1,0:T(8,128)(2,1)S(1)} %fusion.6) | copy-start | bytes 786436
  262.6 7.3 %collective-permute-start.1 = (bf16[128,1024]{0,1:T(8,128)(2,1)S(1)}, bf16[128,1024]{0,1:T(8,128)(2,1)}, u32[]{:S(2)}, u32[]{:S(2)}) collective-permute-start(bf16[128,1024]{0,1:T(8,128)(2,1)S(1)} %bitcast.131), channel_id=1, source_target_pairs={{0,1},{1,0},{2,3},{3,2},{4,5},{5,4},{6,7},{7,6},{8,9},{9,8},{10,11... | collective-permute-start | bytes 786440 | tf_op jit(solution)/shard_map/ppermute | solution.py:45
  267.0 2.9 copy-start.23
  280.9 6.9 %copy-start.6 = (bf16[128,1024]{0,1:T(8,128)(2,1)S(1)}, bf16[128,1024]{0,1:T(8,128)(2,1)}, u32[]{:S(2)}) copy-start(bf16[128,1024]{0,1:T(8,128)(2,1)} %copy-done.4) | copy-start | bytes 786436
  280.9 8.9 %copy-start.16 = (bf16[8,128,128]{2,1,0:T(8,128)(2,1)S(1)}, bf16[8,128,128]{2,1,0:T(8,128)(2,1)}, u32[]{:S(2)}) copy-start(bf16[8,128,128]{2,1,0:T(8,128)(2,1)} %copy-done.15) | copy-start | bytes 786436
  280.9 105.5 %all-to-all-start = ((f32[16,64,1024]{2,1,0:T(8,128)}), f32[16,64,1024]{2,1,0:T(8,128)}, u32[]{:S(2)}, u32[]{:S(2)}) async-start(f32[16,64,1024]{2,1,0:T(8,128)} %copy_bitcast_fusion), calls=%async_computation | async-start | bytes 8388608 | tf_op jit(solution)/shard_map/all_to_all | solution.py:58
  293.1 109.9 %copy-start.14 = (bf16[1,128,8,128]{1,3,2,0:T(8,128)(2,1)S(1)}, bf16[1,128,8,128]{1,3,2,0:T(8,128)(2,1)}, u32[]{:S(2)}) copy-start(bf16[1,128,8,128]{1,3,2,0:T(8,128)(2,1)} %get-tuple-element.9) | copy-start | bytes 786436
  389.6 23.3 %all-to-all-start.1 = ((f32[8,8,1024]{2,1,0:T(8,128)}), f32[8,8,1024]{2,1,0:T(8,128)S(1)}, u32[]{:S(2)}, u32[]{:S(2)}) async-start(f32[8,8,1024]{2,1,0:T(8,128)} %bitcast.32), calls=%async_computation.1 | async-start | bytes 524288 | tf_op jit(solution)/shard_map/all_to_all | solution.py:61
  447.9 7.9 %copy-start.18 = (f32[8,128,128]{2,1,0:T(8,128)S(1)}, f32[8,128,128]{2,1,0:T(8,128)}, u32[]{:S(2)}) copy-start(f32[8,128,128]{2,1,0:T(8,128)} %fusion.57) | copy-start | bytes 1572868
  447.9 8.2 %copy-start.10 = (bf16[128,1024]{1,0:T(8,128)(2,1)S(1)}, bf16[128,1024]{1,0:T(8,128)(2,1)}, u32[]{:S(2)}) copy-start(bf16[128,1024]{1,0:T(8,128)(2,1)} %copy-done.9) | copy-start | bytes 786436
  447.9 8.2 %copy-start.19 = (f32[8,128,128]{2,1,0:T(8,128)S(1)}, f32[8,128,128]{2,1,0:T(8,128)}, u32[]{:S(2)}) copy-start(f32[8,128,128]{2,1,0:T(8,128)} %fusion.59) | copy-start | bytes 1572868
  455.7 1.6 copy-start
  455.7 1.7 copy-start.20
  458.3 1.0 copy-start.24
  (2 other events, 1.4 us)
Sparse Core Ops, SparseCore 0:
  50.5 75.9 all-gather.6
  144.0 98.4 all-gather.8
  253.5 194.3 all-gather.10

commit v6 on v5

--- a/solution.py
+++ b/solution.py
@@ -8,13 +8,25 @@
 CTX = ("cy", "core")
 
 
-def state_sum(shard, axis, later):
-    count = lax.axis_size(axis)
-    place = lax.axis_index(axis)
-    gathered = lax.all_gather(shard, axis, axis=0, tiled=False)
-    blocks = lax.broadcasted_iota(jnp.int32, (count,) + (1,) * shard.ndim, 0)
-    chosen = blocks > place if later else blocks < place
-    return jnp.sum(jnp.where(chosen, gathered, 0.0), axis=0)
+def state_sum(shard, later):
+    chips = lax.axis_size("cy")
+    chip = lax.axis_index("cy")
+    core = lax.axis_index("core")
+    swap = [(0, 1), (1, 0)]
+    partner = lax.ppermute(shard, "core", swap)
+    both = shard + partner
+    half = shard.shape[1] // 2
+    mine = lax.dynamic_slice_in_dim(both, core * half, half, 1)
+    gathered = lax.all_gather(mine, "cy", axis=0, tiled=False)
+    blocks = lax.broadcasted_iota(jnp.int32, (chips,) + (1,) * mine.ndim, 0)
+    chosen = blocks > chip if later else blocks < chip
+    summed = jnp.sum(jnp.where(chosen, gathered, 0.0), axis=0)
+    other = lax.ppermute(summed, "core", swap)
+    first = jnp.where(core == 0, summed, other)
+    second = jnp.where(core == 0, other, summed)
+    across = jnp.concatenate([first, second], 1)
+    inside = (core == 0) if later else (core == 1)
+    return across + jnp.where(inside, partner, 0.0)
 
 
 def gather_rows(weights, piece):
@@ -86,7 +98,7 @@
     local_state = jnp.einsum(
         "bthe,bthf->bhef", key_rows, values, preferred_element_type=jnp.float32
     )
-    before = state_sum(local_state, CTX, False).astype(jnp.bfloat16)
+    before = state_sum(local_state, False).astype(jnp.bfloat16)
     causal = jnp.tril(jnp.ones((tokens_here, tokens_here), dtype=bool))
     scores = jnp.einsum("bthe,bshe->bhts", queries, key_rows, preferred_element_type=jnp.float32)
     scores = jnp.where(causal[None, None], scores, 0.0).astype(jnp.bfloat16)
@@ -110,7 +122,7 @@
     grad_local = jnp.einsum(
         "bthe,bthf->bhef", queries, grad_mixed, preferred_element_type=jnp.float32
     )
-    after_state = state_sum(grad_local, CTX, True).astype(jnp.bfloat16)
+    after_state = state_sum(grad_local, True).astype(jnp.bfloat16)
     query_grad = jnp.einsum(
         "bhts,bshe->bthe", score_grad, key_rows, preferred_element_type=jnp.float32
     )

time: 472 us -> 496 us (1.051)
  waiting for transfers between devices: 292 us -> 329 us
    all_to_all x1, waiting for transfers between devices: 93.3 us -> 169 us  [weight_grads(): lax.all_to_all(stacked.reshape(chips, -1, width), 'cy', 0, 0, tiled=False)]
    all_gather x2, waiting for transfers between devices: 116 us -> 79.3 us  [state_sum(): gathered = lax.all_gather(mine, 'cy', axis=0, tiled=False)]
    reduce_sum x2, other arithmetic: 15.7 us -> 5.41 us  [state_sum(): summed = jnp.sum(jnp.where(chosen, gathered, 0.0), axis=0)]
    ppermute x0 -> x4, starting transfers between devices: none -> 6.42 us  [the longest x2 5.65 us: state_sum(): other = lax.ppermute(summed, 'core', swap)]
    all_to_all x1, starting transfers between devices: 11.4 us -> 5.37 us  [weight_grads(): lax.all_to_all(share.reshape(outer, -1, width), 'dp', 0, 0, tiled=False)]
  transfers between devices with their start and end apart: 9 -> 13, of which waited for: 7 -> 7; matrix products, arithmetic and copies ran while one was open for 12% -> 13% of each run, Pallas kernels for 0% -> 0%
where the time goes in v6:
time: 496 us; the launch traced here: 491 us
  waiting for transfers between devices  329 us (66%)
  blocking collectives  40.7 us (8%)
  local copies, waits for them, and re-layouts  35.7 us (7%)
  matrix products  27.7 us (6%)
  other arithmetic  25.7 us (5%)
  starting transfers between devices  17.5 us (4%)
  between operations  14.2 us (3%)
    all_to_all x1, waiting for transfers between devices, weight_grads(): lax.all_to_all(stacked.reshape(chips, -1, width), 'cy', 0, 0, tiled=False)  169 us
    all_gather x2, waiting for transfers between devices, state_sum(): gathered = lax.all_gather(mine, 'cy', axis=0, tiled=False)  79.3 us
    all_gather x1, waiting for transfers between devices, spread_rows(): gathered = lax.all_gather(across, CTX, axis=0, tiled=False)  74.8 us
    all_gather x1, blocking collectives, gather_rows(): across = lax.all_gather(joined, 'dp', axis=0, tiled=False)  40.7 us
    another operation x4, local copies, waits for them, and re-layouts, spread_rows(): return tuple((gathered[index].reshape(-1, width) for index in range(count)))  12.6 us
  transfers between devices with their start and end apart: 13, of which 7 were waited for; matrix products, arithmetic and copies ran while one was open for 13% of the time, Pallas kernels for 0%

profile of v6, /device:TPU:1, one launch (start us, length us, event | category | flops | bytes accessed | tf_op | source)
XLA Modules:
  0.0 490.9 jit_solution(15921133639333494569)
XLA Ops:
  8.8 40.7 %all-gather = bf16[128,1024]{1,0:T(8,128)(2,1)S(1)} all-gather(bf16[16,1024]{1,0:T(8,128)(2,1)S(1)} %pad_maximum_fusion.1), channel_id=2, replica_groups=mesh['dp'=8,'cy'=16,'core'=2] {'dp'}, dimensions={0}, use_global_device_ids=true | all-gather | bytes 294912 | tf_op jit(solution)/shard_map/all_gather | solution.py:37
  51.7 74.8 %all-gather.7.cloned.1.call-done = bf16[32,8,4,4,1024]{4,3,0,1,2:T(4,128)(2,1)} async-done(((bf16[1,8,4,4,1024]{4,3,0,1,2:T(4,128)(2,1)}), bf16[32,8,4,4,1024]{4,3,0,1,2:T(4,128)(2,1)}) %all-gather.7.cloned.1.call-update) | async-done | bytes 8388624 | tf_op jit(solution)/shard_map/all_gather | solution.py:43
  126.5 7.2 %fusion.54 = (bf16[1,8,32,4,1024]{4,3,2,1,0:T(4,128)(2,1)}, bf16[1,8,32,4,1024]{4,3,2,1,0:T(4,128)(2,1)S(1)}, bf16[1,8,32,4,1024]{4,3,2,1,0:T(4,128)(2,1)}, bf16[1,8,32,4,1024]{4,3,2,1,0:T(4,128)(2,1)}) fusion(bf16[4,8,32,4,1024]{4,3,2,1,0:T(4,128)(2,1)} %bitcast.139), kind=kLoop, calls=%fused_computation.104 | loop fusion | bytes 16777216 | tf_op jit(solution)/shard_map/slice | solution.py:46
  133.7 2.1 reshape_squeeze.14
  135.7 2.5 reshape_squeeze.12
  138.3 2.0 convolution_convert_fusion
  144.0 2.0 collective-permute-done
  146.0 1.8 dynamic-slice_add_fusion.1
  150.5 1.8 copy.92
  152.3 1.7 fusion.31
  154.0 1.7 reshape.246
  155.8 4.0 reshape_squeeze.13
  159.7 2.0 convolution_convert_fusion.1
  162.0 4.0 reshape_squeeze.15
  166.0 2.3 fusion.49
  168.3 79.3 %all-gather.9.cloned.1.call-done = f32[16,4,128,128]{3,2,1,0:T(8,128)} async-done(((f32[1,4,128,128]{3,2,1,0:T(8,128)}), f32[16,4,128,128]{3,2,1,0:T(8,128)}) %all-gather.9.cloned.1.call-update) | async-done | bytes 4194320 | tf_op jit(solution)/shard_map/all_gather | solution.py:20
  247.6 2.7 fusion.1
  259.0 2.9 convolution_multiply_fusion
  261.9 2.9 reshape.249
  264.8 2.8 convolution_multiply_fusion.1
  267.6 2.9 reshape.247
  270.5 5.2 %copy_bitcast_fusion = f32[16,64,1024]{2,1,0:T(8,128)} fusion(f32[8,16,4,1024]{3,2,1,0:T(4,128)} %reshape.249, f32[8,16,4,1024]{3,2,1,0:T(4,128)} %reshape.247), kind=kLoop, calls=%fused_computation.1 | loop fusion | flops 1048576 | bytes 8388608 | tf_op jit(solution)/shard_map/reshape;reshape | solution.py:71
  275.8 4.7 all-to-all-start
  280.5 1.8 dynamic-slice_add_fusion
  282.3 2.1 fusion.58
  284.5 3.3 fusion.57
  289.0 169.4 %all-to-all-done = f32[16,64,1024]{2,1,0:T(8,128)} async-done(((f32[16,64,1024]{2,1,0:T(8,128)}), f32[16,64,1024]{2,1,0:T(8,128)}, u32[]{:S(2)}, u32[]{:S(2)}) %all-to-all-start) | async-done | bytes 4194336 | tf_op jit(solution)/shard_map/all_to_all | solution.py:70
  458.4 3.2 reduce_sum.84
  461.5 5.4 %all-to-all-start.1 = ((f32[8,8,1024]{2,1,0:T(8,128)}), f32[8,8,1024]{2,1,0:T(8,128)}, u32[]{:S(2)}, u32[]{:S(2)}) async-start(f32[8,8,1024]{2,1,0:T(8,128)} %bitcast.38), calls=%async_computation.1 | async-start | bytes 524288 | tf_op jit(solution)/shard_map/all_to_all | solution.py:73
  466.9 2.7 fusion
  469.6 4.1 collective-permute-start.3
  474.8 2.2 all-to-all-done.1
  (110 shorter events, 28.4 us)
Async XLA Ops:
  7.2 44.4 %copy-start.2 = (bf16[1,128,1024]{2,1,0:T(8,128)(2,1)S(1)}, bf16[1,128,1024]{2,1,0:T(8,128)(2,1)}, u32[]{:S(2)}) copy-start(bf16[1,128,1024]{2,1,0:T(8,128)(2,1)} %param.9) | copy-start | bytes 786436
  7.2 119.3 %all-gather.7.cloned.1.call-start = ((), (), s32[]{:S(2)}) async-start(), calls=%async_computation.2 | async-start | bytes 8650752 | tf_op jit(solution)/shard_map/all_gather | solution.py:43
  50.4 197.2 %all-gather.9.cloned.1.call-start = ((), (), s32[]{:S(2)}) async-start(), calls=%async_computation.3 | async-start | bytes 4456448 | tf_op jit(solution)/shard_map/all_gather | solution.py:20
  140.3 3.4 copy-start.6
  142.7 11.3 %copy-start.9 = (bf16[128,8,128]{0,2,1:T(8,128)(2,1)}, bf16[128,8,128]{0,2,1:T(8,128)(2,1)S(1)}, u32[]{:S(2)}) copy-start(bf16[128,8,128]{0,2,1:T(8,128)(2,1)S(1)} %copy.77) | copy-start | bytes 786436
  143.7 2.3 collective-permute-start
  148.6 1.9 collective-permute-start.4
  148.9 110.1 %collective-permute-start.7 = (bf16[128,1024]{1,0:T(8,128)(2,1)}, bf16[128,1024]{1,0:T(8,128)(2,1)}, u32[]{:S(2)}, u32[]{:S(2)}) collective-permute-start(bf16[128,1024]{1,0:T(8,128)(2,1)} %bitcast.159), channel_id=1, source_target_pairs={{0,1},{1,0},{2,3},{3,2},{4,5},{5,4},{6,7},{7,6},{8,9},{9,8},{10,11... | collective-permute-start | bytes 786440 | tf_op jit(solution)/shard_map/ppermute | solution.py:57
  162.0 92.2 %copy-start.3 = (bf16[128,1024]{0,1:T(8,128)(2,1)}, bf16[128,1024]{0,1:T(8,128)(2,1)S(1)}, u32[]{:S(2)}) copy-start(bf16[128,1024]{0,1:T(8,128)(2,1)S(1)} %copy.101) | copy-start | bytes 786436
  247.6 4.3 copy-start.7
  250.3 2.7 collective-permute-start.1
  254.5 1.3 copy-start.4
  254.8 3.3 copy-start.11
  255.4 1.6 copy-start.18
  255.7 2.3 collective-permute-start.6
  257.0 23.5 %collective-permute-start.2 = (f32[1,8,128,128]{3,2,1,0:T(8,128)}, f32[1,8,128,128]{3,2,1,0:T(8,128)}, u32[]{:S(2)}, u32[]{:S(2)}) collective-permute-start(f32[1,8,128,128]{3,2,1,0:T(8,128)} %convolution_bitcast_fusion), channel_id=1, source_target_pairs={{0,1},{1,0},{2,3},{3,2},{4,5},{5,4},{6,7},{7,6},{8,9},{9,8},{10,11... | collective-permute-start | bytes 1572872 | tf_op jit(solution)/shard_map/ppermute | solution.py:16
  257.7 7.1 %copy-start.13 = (bf16[8,128,128]{2,1,0:T(8,128)(2,1)}, bf16[8,128,128]{2,1,0:T(8,128)(2,1)S(1)}, u32[]{:S(2)}) copy-start(bf16[8,128,128]{2,1,0:T(8,128)(2,1)S(1)} %fusion.8) | copy-start | bytes 786436
  257.8 7.1 %collective-permute-start.5 = (bf16[128,1024]{0,1:T(8,128)(2,1)S(1)}, bf16[128,1024]{0,1:T(8,128)(2,1)}, u32[]{:S(2)}, u32[]{:S(2)}) collective-permute-start(bf16[128,1024]{0,1:T(8,128)(2,1)S(1)} %bitcast.149), channel_id=1, source_target_pairs={{0,1},{1,0},{2,3},{3,2},{4,5},{5,4},{6,7},{7,6},{8,9},{9,8},{10,11... | collective-permute-start | bytes 786440 | tf_op jit(solution)/shard_map/ppermute | solution.py:57
  261.9 2.9 copy-start.19
  275.8 6.6 %copy-start.5 = (bf16[128,1024]{0,1:T(8,128)(2,1)S(1)}, bf16[128,1024]{0,1:T(8,128)(2,1)}, u32[]{:S(2)}) copy-start(bf16[128,1024]{0,1:T(8,128)(2,1)} %copy-done.3) | copy-start | bytes 786436
  275.8 182.6 %all-to-all-start = ((f32[16,64,1024]{2,1,0:T(8,128)}), f32[16,64,1024]{2,1,0:T(8,128)}, u32[]{:S(2)}, u32[]{:S(2)}) async-start(f32[16,64,1024]{2,1,0:T(8,128)} %copy_bitcast_fusion), calls=%async_computation | async-start | bytes 8388608 | tf_op jit(solution)/shard_map/all_to_all | solution.py:70
  280.4 186.5 %all-gather.11.cloned.1.call-start = ((), (), s32[]{:S(2)}) async-start(), calls=%async_computation.4 | async-start | bytes 4456448 | tf_op jit(solution)/shard_map/all_gather | solution.py:20
  282.3 5.5 %copy-start.12 = (bf16[1,128,8,128]{1,3,2,0:T(8,128)(2,1)S(1)}, bf16[1,128,8,128]{1,3,2,0:T(8,128)(2,1)}, u32[]{:S(2)}) copy-start(bf16[1,128,8,128]{1,3,2,0:T(8,128)(2,1)} %copy-done.11) | copy-start | bytes 786436
  282.3 5.5 %copy-start.1 = (bf16[1024,1024]{1,0:T(8,128)(2,1)S(1)}, bf16[1024,1024]{1,0:T(8,128)(2,1)}, u32[]{:S(2)}) copy-start(bf16[1024,1024]{1,0:T(8,128)(2,1)} %reshape_squeeze.15) | copy-start | bytes 6291460
  282.3 5.5 %copy-start.21 = (bf16[1,128,1024]{2,1,0:T(8,128)(2,1)S(1)}, bf16[1,128,1024]{2,1,0:T(8,128)(2,1)}, u32[]{:S(2)}) copy-start(bf16[1,128,1024]{2,1,0:T(8,128)(2,1)} %param.8) | copy-start | bytes 786436
  461.5 15.5 %all-to-all-start.1 = ((f32[8,8,1024]{2,1,0:T(8,128)}), f32[8,8,1024]{2,1,0:T(8,128)}, u32[]{:S(2)}, u32[]{:S(2)}) async-start(f32[8,8,1024]{2,1,0:T(8,128)} %bitcast.38), calls=%async_computation.1 | async-start | bytes 524288 | tf_op jit(solution)/shard_map/all_to_all | solution.py:73
  466.9 6.8 %copy-start.17 = (bf16[8,128,128]{2,1,0:T(8,128)(2,1)S(1)}, bf16[8,128,128]{2,1,0:T(8,128)(2,1)}, u32[]{:S(2)}) copy-start(bf16[8,128,128]{2,1,0:T(8,128)(2,1)} %copy-done.16) | copy-start | bytes 786436
  469.6 9.0 %collective-permute-start.3 = (f32[1,4,128,128]{3,2,1,0:T(8,128)S(1)}, f32[1,4,128,128]{3,2,1,0:T(8,128)}, u32[]{:S(2)}, u32[]{:S(2)}) collective-permute-start(f32[1,4,128,128]{3,2,1,0:T(8,128)S(1)} %bitcast.152), channel_id=1, source_target_pairs={{0,1},{1,0},{2,3},{3,2},{4,5},{5,4},{6,7},{7,6},{8,9},{9,8},{10,11... | collective-permute-start | bytes 786440 | tf_op jit(solution)/shard_map/ppermute | solution.py:24
  474.8 6.4 %copy-start.8 = (bf16[128,1024]{1,0:T(8,128)(2,1)S(1)}, bf16[128,1024]{1,0:T(8,128)(2,1)}, u32[]{:S(2)}) copy-start(bf16[128,1024]{1,0:T(8,128)(2,1)} %copy-done.6) | copy-start | bytes 786436
  478.0 3.2 copy-start.14
  479.6 2.0 copy-start
  479.6 1.9 copy-start.15
  (3 other events, 2.8 us)
Sparse Core Ops, SparseCore 0:
  50.5 75.9 all-gather.6
  147.9 99.6 all-gather.8
  283.0 174.8 all-gather.10

commit v7 on v6

--- a/solution.py
+++ b/solution.py
@@ -34,7 +34,8 @@
     width = weights[0].shape[1]
     parts = [lax.dynamic_slice_in_dim(weight, place * piece, piece, 0) for weight in weights]
     joined = jnp.concatenate(parts, 0)
-    across = lax.all_gather(joined, "dp", axis=0, tiled=False)
+    copies = jnp.broadcast_to(joined[None], (lax.axis_size("dp"),) + joined.shape)
+    across = lax.all_to_all(copies, "dp", 0, 0, tiled=False)
     return across.reshape(across.shape[0], len(weights), piece, width)
 
 
@@ -47,7 +48,7 @@
     )
 
 
-def weight_grads(pairs, factor):
+def weight_grads(pairs, factor, wait_for):
     width = pairs[0][0].shape[1]
     outer, chips, cores = lax.axis_size("dp"), lax.axis_size("cy"), lax.axis_size("core")
     mine = lax.axis_index("core")
@@ -67,6 +68,7 @@
     rows = blocks[0].shape[2]
     stacked = jnp.concatenate(blocks, 2)
     stacked = jnp.transpose(stacked, (1, 0, 2, 3)).reshape(-1, width)
+    stacked, _ = lax.optimization_barrier((stacked, wait_for))
     share = lax.all_to_all(
         stacked.reshape(chips, -1, width), "cy", 0, 0, tiled=False
     ).sum(0)
@@ -161,7 +163,7 @@
         (normed.reshape(-1, width), query_grad.reshape(-1, width)),
         (attn_out.reshape(-1, width), grad_first.reshape(-1, width)),
     )
-    grad_query, grad_out = weight_grads(pairs, factor)
+    grad_query, grad_out = weight_grads(pairs, factor, after_state)
     return (x_first, grad_x_second, grad_query, grad_out)
 
 

time: 496 us -> 487 us (0.982)
  blocking collectives: 40.7 us -> 21.3 us
  local copies, waits for them, and re-layouts: 35.7 us -> 54.8 us
    all_gather x2, waiting for transfers between devices: 79.3 us -> 161 us  [state_sum(): gathered = lax.all_gather(mine, 'cy', axis=0, tiled=False)]
    all_to_all x1, waiting for transfers between devices: 169 us -> 88.2 us  [weight_grads(): lax.all_to_all(stacked.reshape(chips, -1, width), 'cy', 0, 0, tiled=False)]
    all_gather x1 -> x0, blocking collectives: 40.7 us -> none  [gather_rows(): across = lax.all_gather(joined, 'dp', axis=0, tiled=False)]
    all_to_all x0 -> x1, blocking collectives: none -> 21.3 us  [gather_rows(): across = lax.all_to_all(copies, 'dp', 0, 0, tiled=False)]
    slice x1 -> x5, local copies, waits for them, and re-layouts: 7.17 us -> 21.2 us  [spread_rows(): return tuple((gathered[index].reshape(-1, width) for index in range(count)))]
    all_gather x1, waiting for transfers between devices: 74.8 us -> 67.6 us  [spread_rows(): gathered = lax.all_gather(across, CTX, axis=0, tiled=False)]
    all_to_all x1, waiting for transfers between devices: 2.24 us -> 9.11 us  [weight_grads(): lax.all_to_all(share.reshape(outer, -1, width), 'dp', 0, 0, tiled=False)]
  transfers between devices with their start and end apart: 13 -> 13, of which waited for: 7 -> 10; matrix products, arithmetic and copies ran while one was open for 13% -> 13% of each run, Pallas kernels for 0% -> 0%
where the time goes in v7:
time: 487 us; the launch traced here: 485 us
  waiting for transfers between devices  331 us (68%)
  local copies, waits for them, and re-layouts  54.8 us (11%)
  matrix products  24.3 us (5%)
  other arithmetic  22.6 us (5%)
  blocking collectives  21.3 us (4%)
  starting transfers between devices  16.3 us (3%)
  between operations  14.2 us (3%)
    all_gather x2, waiting for transfers between devices, state_sum(): gathered = lax.all_gather(mine, 'cy', axis=0, tiled=False)  161 us
    all_to_all x1, waiting for transfers between devices, weight_grads(): lax.all_to_all(stacked.reshape(chips, -1, width), 'cy', 0, 0, tiled=False)  88.2 us
    all_gather x1, waiting for transfers between devices, spread_rows(): gathered = lax.all_gather(across, CTX, axis=0, tiled=False)  67.6 us
    all_to_all x1, blocking collectives, gather_rows(): across = lax.all_to_all(copies, 'dp', 0, 0, tiled=False)  21.3 us
    slice x5, local copies, waits for them, and re-layouts, spread_rows(): return tuple((gathered[index].reshape(-1, width) for index in range(count)))  21.2 us
    another operation x4, local copies, waits for them, and re-layouts, spread_rows(): return tuple((gathered[index].reshape(-1, width) for index in range(count)))  12.7 us
  transfers between devices with their start and end apart: 13, of which 10 were waited for; matrix products, arithmetic and copies ran while one was open for 13% of the time, Pallas kernels for 0%

profile of v7, /device:TPU:1, one launch (start us, length us, event | category | flops | bytes accessed | tf_op | source)
XLA Modules:
  0.0 484.8 jit_solution(12482957371104660671)
XLA Ops:
  8.8 21.3 %all_to_all.15 = bf16[8,16,1024]{2,1,0:T(8,128)(2,1)S(1)} all-to-all(bf16[8,16,1024]{2,1,0:T(8,128)(2,1)S(1)} %broadcast_in_dim.56), channel_id=1, replica_groups=mesh['dp'=8,'cy'=16,'core'=2] {'dp'}, dimensions={0} | all-to-all | bytes 524288 | tf_op jit(solution)/shard_map/all_to_all | solution.py:38
  32.3 67.6 %all-gather.6.cloned.1.call-done = bf16[32,8,4,4,1024]{4,1,3,2,0:T(8,128)(2,1)} async-done(((bf16[1,8,4,4,1024]{4,1,3,2,0:T(8,128)(2,1)}), bf16[32,8,4,4,1024]{4,1,3,2,0:T(8,128)(2,1)}) %all-gather.6.cloned.1.call-update) | async-done | bytes 8388624 | tf_op jit(solution)/shard_map/all_gather | solution.py:44
  99.9 5.9 %fusion.55 = (bf16[1,8,32,4,1024]{4,1,3,0,2:T(8,128)(2,1)}, bf16[1,8,32,4,1024]{4,1,3,0,2:T(8,128)(2,1)S(1)}, bf16[1,8,32,4,1024]{4,1,3,0,2:T(8,128)(2,1)}, bf16[1,8,32,4,1024]{4,1,3,0,2:T(8,128)(2,1)}) fusion(bf16[4,8,32,4,1024]{4,1,3,0,2:T(8,128)(2,1)} %bitcast.142), kind=kLoop, calls=%fused_computation.104 | loop fusion | bytes 16777216 | tf_op jit(solution)/shard_map/slice | solution.py:47
  107.5 2.1 reshape_squeeze.14
  109.6 4.6 copy.102
  114.1 2.5 reshape_squeeze.12
  116.7 2.0 convolution_convert_fusion
  122.4 2.0 collective-permute-done
  126.4 4.6 copy.103
  131.0 4.0 reshape_squeeze.13
  135.0 2.1 convolution_convert_fusion.1
  138.0 4.6 copy.112
  142.6 4.0 reshape_squeeze.15
  146.6 2.3 fusion.50
  148.9 76.9 %all-gather.8.cloned.1.call-done = f32[16,4,128,128]{3,2,1,0:T(8,128)} async-done(((f32[1,4,128,128]{3,2,1,0:T(8,128)}), f32[16,4,128,128]{3,2,1,0:T(8,128)}) %all-gather.8.cloned.1.call-update) | async-done | bytes 4194320 | tf_op jit(solution)/shard_map/all_gather | solution.py:20
  225.8 2.7 fusion.1
  235.1 1.9 collective-permute-done.2
  243.1 1.8 fusion.31
  249.3 2.9 convolution_multiply_fusion
  252.2 84.4 %all-gather.10.cloned.1.call-done = f32[16,4,128,128]{3,2,1,0:T(8,128)} async-done(((f32[1,4,128,128]{3,2,1,0:T(8,128)}), f32[16,4,128,128]{3,2,1,0:T(8,128)}) %all-gather.10.cloned.1.call-update) | async-done | bytes 4194320 | tf_op jit(solution)/shard_map/all_gather | solution.py:20
  336.6 2.7 fusion
  341.1 2.8 convolution_multiply_fusion.1
  343.9 2.9 reshape.256
  346.8 2.8 reshape.254
  349.6 3.3 pad_maximum_fusion
  352.9 2.3 copy.132
  356.3 4.7 all-to-all-start.1
  363.6 2.4 fusion.58
  369.7 88.2 %all-to-all-done.1 = f32[16,64,1024]{2,1,0:T(8,128)} async-done(((f32[16,64,1024]{2,1,0:T(8,128)}), f32[16,64,1024]{2,1,0:T(8,128)}, u32[]{:S(2)}, u32[]{:S(2)}) %all-to-all-start.1) | async-done | bytes 4194336 | tf_op jit(solution)/shard_map/all_to_all | solution.py:72
  457.9 3.2 reduce_sum.84
  461.1 6.5 %all-to-all-start.2 = ((f32[8,8,1024]{2,1,0:T(8,128)}), f32[8,8,1024]{2,1,0:T(8,128)S(1)}, u32[]{:S(2)}, u32[]{:S(2)}) async-start(f32[8,8,1024]{2,1,0:T(8,128)} %bitcast.40), calls=%async_computation.2 | async-start | bytes 524288 | tf_op jit(solution)/shard_map/all_to_all | solution.py:75
  468.5 9.1 %all-to-all-done.2 = f32[8,8,1024]{2,1,0:T(8,128)S(1)} async-done(((f32[8,8,1024]{2,1,0:T(8,128)}), f32[8,8,1024]{2,1,0:T(8,128)S(1)}, u32[]{:S(2)}, u32[]{:S(2)}) %all-to-all-start.2) | async-done | bytes 262176 | tf_op jit(solution)/shard_map/all_to_all | solution.py:75
  (121 shorter events, 39.4 us)
Async XLA Ops:
  7.2 25.0 %copy-start.2 = (bf16[1,128,1024]{2,1,0:T(8,128)(2,1)S(1)}, bf16[1,128,1024]{2,1,0:T(8,128)(2,1)}, u32[]{:S(2)}) copy-start(bf16[1,128,1024]{2,1,0:T(8,128)(2,1)} %param.9) | copy-start | bytes 786436
  7.2 92.8 %all-gather.6.cloned.1.call-start = ((), (), s32[]{:S(2)}) async-start(), calls=%async_computation.3 | async-start | bytes 8650752 | tf_op jit(solution)/shard_map/all_gather | solution.py:44
  31.1 194.8 %all-gather.8.cloned.1.call-start = ((), (), s32[]{:S(2)}) async-start(), calls=%async_computation.4 | async-start | bytes 4456448 | tf_op jit(solution)/shard_map/all_gather | solution.py:20
  118.7 3.4 copy-start.7
  121.1 9.9 %copy-start.12 = (bf16[128,8,128]{0,2,1:T(8,128)(2,1)}, bf16[128,8,128]{0,2,1:T(8,128)(2,1)S(1)}, u32[]{:S(2)}) copy-start(bf16[128,8,128]{0,2,1:T(8,128)(2,1)S(1)} %copy.108) | copy-start | bytes 786436
  122.1 2.3 collective-permute-start
  126.2 210.4 %all-gather.10.cloned.1.call-start = ((), (), s32[]{:S(2)}) async-start(), calls=%async_computation.5 | async-start | bytes 4456448 | tf_op jit(solution)/shard_map/all_gather | solution.py:20
  225.8 4.3 copy-start.5
  225.8 4.3 copy-start.8
  228.6 2.7 collective-permute-start.1
  235.0 11.8 %copy-start.4 = (bf16[128,8,128]{0,2,1:T(8,128)(2,1)S(1)}, bf16[128,8,128]{0,2,1:T(8,128)(2,1)}, u32[]{:S(2)}) copy-start(bf16[128,8,128]{0,2,1:T(8,128)(2,1)} %copy-done.3) | copy-start | bytes 786436
  235.0 2.0 collective-permute-start.2
  239.4 1.9 collective-permute-start.4
  239.6 9.8 %collective-permute-start.7 = (bf16[128,1024]{1,0:T(8,128)(2,1)}, bf16[128,1024]{1,0:T(8,128)(2,1)}, u32[]{:S(2)}, u32[]{:S(2)}) collective-permute-start(bf16[128,1024]{1,0:T(8,128)(2,1)} %bitcast.12), channel_id=1, source_target_pairs={{0,1},{1,0},{2,3},{3,2},{4,5},{5,4},{6,7},{7,6},{8,9},{9,8},{10,11... | collective-permute-start | bytes 786440 | tf_op jit(solution)/shard_map/ppermute | solution.py:58
  239.9 7.5 %copy-start.11 = (bf16[8,128,128]{2,1,0:T(8,128)(2,1)S(1)}, bf16[8,128,128]{2,1,0:T(8,128)(2,1)}, u32[]{:S(2)}) copy-start(bf16[8,128,128]{2,1,0:T(8,128)(2,1)} %copy-done.10) | copy-start | bytes 786436
  240.8 6.3 %copy-start.13 = (bf16[128,8,128]{0,2,1:T(8,128)(2,1)S(1)}, bf16[128,8,128]{0,2,1:T(8,128)(2,1)}, u32[]{:S(2)}) copy-start(bf16[128,8,128]{0,2,1:T(8,128)(2,1)} %copy-done.12) | copy-start | bytes 786436
  246.6 1.8 copy-start.14
  246.6 1.7 collective-permute-start.6
  247.7 93.4 %copy-start.16 = (bf16[8,128,128]{2,1,0:T(8,128)(2,1)}, bf16[8,128,128]{2,1,0:T(8,128)(2,1)S(1)}, u32[]{:S(2)}) copy-start(bf16[8,128,128]{2,1,0:T(8,128)(2,1)S(1)} %fusion.8) | copy-start | bytes 786436
  247.7 93.4 %collective-permute-start.5 = (bf16[128,1024]{0,1:T(8,128)(2,1)S(1)}, bf16[128,1024]{0,1:T(8,128)(2,1)}, u32[]{:S(2)}, u32[]{:S(2)}) collective-permute-start(bf16[128,1024]{0,1:T(8,128)(2,1)S(1)} %bitcast.152), channel_id=1, source_target_pairs={{0,1},{1,0},{2,3},{3,2},{4,5},{5,4},{6,7},{7,6},{8,9},{9,8},{10,11... | collective-permute-start | bytes 786440 | tf_op jit(solution)/shard_map/ppermute | solution.py:58
  336.6 4.5 copy-start.22
  339.3 15.9 %collective-permute-start.3 = (f32[1,4,128,128]{3,2,1,0:T(8,128)S(1)}, f32[1,4,128,128]{3,2,1,0:T(8,128)}, u32[]{:S(2)}, u32[]{:S(2)}) collective-permute-start(f32[1,4,128,128]{3,2,1,0:T(8,128)S(1)} %bitcast.155), channel_id=1, source_target_pairs={{0,1},{1,0},{2,3},{3,2},{4,5},{5,4},{6,7},{7,6},{8,9},{9,8},{10,11... | collective-permute-start | bytes 786440 | tf_op jit(solution)/shard_map/ppermute | solution.py:24
  352.9 3.3 copy-start.19
  356.3 4.7 copy-start.6
  356.3 101.6 %all-to-all-start.1 = ((f32[16,64,1024]{2,1,0:T(8,128)}), f32[16,64,1024]{2,1,0:T(8,128)}, u32[]{:S(2)}, u32[]{:S(2)}) async-start(f32[16,64,1024]{2,1,0:T(8,128)} %bitcast.141), calls=%async_computation.1 | async-start | bytes 8388608 | tf_op jit(solution)/shard_map/all_to_all | solution.py:72
  361.0 2.6 copy-start.17
  362.2 3.8 copy-start.1
  362.2 3.8 copy-start.15
  362.3 3.8 copy-start.24
  366.1 1.8 copy-start
  369.7 97.9 %copy-start.23 = (bf16[1,128,1024]{2,1,0:T(8,128)(2,1)S(1)}, bf16[1,128,1024]{2,1,0:T(8,128)(2,1)}, u32[]{:S(2)}) copy-start(bf16[1,128,1024]{2,1,0:T(8,128)(2,1)} %param.11) | copy-start | bytes 786436
  461.1 16.6 %all-to-all-start.2 = ((f32[8,8,1024]{2,1,0:T(8,128)}), f32[8,8,1024]{2,1,0:T(8,128)S(1)}, u32[]{:S(2)}, u32[]{:S(2)}) async-start(f32[8,8,1024]{2,1,0:T(8,128)} %bitcast.40), calls=%async_computation.2 | async-start | bytes 524288 | tf_op jit(solution)/shard_map/all_to_all | solution.py:75
  (6 other events, 5.9 us)
Sparse Core Ops, SparseCore 0:
  31.2 68.7 all-gather.5
  126.3 99.4 all-gather.7
  238.7 97.8 all-gather.9

commit v8 on v7

--- a/solution.py
+++ b/solution.py
@@ -70,8 +70,8 @@
     stacked = jnp.transpose(stacked, (1, 0, 2, 3)).reshape(-1, width)
     stacked, _ = lax.optimization_barrier((stacked, wait_for))
     share = lax.all_to_all(
-        stacked.reshape(chips, -1, width), "cy", 0, 0, tiled=False
-    ).sum(0)
+        stacked.reshape(chips, -1, width).astype(jnp.bfloat16), "cy", 0, 0, tiled=False
+    ).astype(jnp.float32).sum(0)
     share = lax.all_to_all(
         share.reshape(outer, -1, width), "dp", 0, 0, tiled=False
     ).sum(0)

time: 487 us -> 438 us (0.90)
  waiting for transfers between devices: 331 us -> 290 us
    all_to_all x1, waiting for transfers between devices: 88.2 us -> 46.1 us  [weight_grads(): lax.all_to_all(stacked.reshape(chips, -1, width).astype(jnp.bfloat16), 'c...]
  transfers between devices with their start and end apart: 13 -> 13, of which waited for: 10 -> 9; matrix products, arithmetic and copies ran while one was open for 13% -> 13% of each run, Pallas kernels for 0% -> 0%
where the time goes in v8:
time: 438 us; the launch traced here: 437 us
  waiting for transfers between devices  290 us (66%)
  local copies, waits for them, and re-layouts  51.9 us (12%)
  matrix products  24.3 us (6%)
  other arithmetic  21.3 us (5%)
  blocking collectives  21.3 us (5%)
  between operations  14.2 us (3%)
  starting transfers between devices  13.8 us (3%)
    all_gather x2, waiting for transfers between devices, state_sum(): gathered = lax.all_gather(mine, 'cy', axis=0, tiled=False)  162 us
    all_gather x1, waiting for transfers between devices, spread_rows(): gathered = lax.all_gather(across, CTX, axis=0, tiled=False)  67.6 us
    all_to_all x1, waiting for transfers between devices, weight_grads(): lax.all_to_all(stacked.reshape(chips, -1, width).astype(jnp.bfloat16), 'c...  46.1 us
    all_to_all x1, blocking collectives, gather_rows(): across = lax.all_to_all(copies, 'dp', 0, 0, tiled=False)  21.3 us
    slice x5, local copies, waits for them, and re-layouts, spread_rows(): return tuple((gathered[index].reshape(-1, width) for index in range(count)))  21.1 us
    another operation x4, local copies, waits for them, and re-layouts, spread_rows(): return tuple((gathered[index].reshape(-1, width) for index in range(count)))  12.7 us
    all_to_all x1, waiting for transfers between devices, weight_grads(): lax.all_to_all(share.reshape(outer, -1, width), 'dp', 0, 0, tiled=False)  9.01 us
  transfers between devices with their start and end apart: 13, of which 9 were waited for; matrix products, arithmetic and copies ran while one was open for 13% of the time, Pallas kernels for 0%

profile of v8, /device:TPU:1, one launch (start us, length us, event | category | flops | bytes accessed | tf_op | source)
XLA Modules:
  0.0 436.6 jit_solution(11384765662511597204)
XLA Ops:
  8.8 21.3 %all_to_all.15 = bf16[8,16,1024]{2,1,0:T(8,128)(2,1)S(1)} all-to-all(bf16[8,16,1024]{2,1,0:T(8,128)(2,1)S(1)} %broadcast_in_dim.56), channel_id=1, replica_groups=mesh['dp'=8,'cy'=16,'core'=2] {'dp'}, dimensions={0} | all-to-all | bytes 524288 | tf_op jit(solution)/shard_map/all_to_all | solution.py:38
  32.3 67.6 %all-gather.6.cloned.1.call-done = bf16[32,8,4,4,1024]{4,1,3,2,0:T(8,128)(2,1)} async-done(((bf16[1,8,4,4,1024]{4,1,3,2,0:T(8,128)(2,1)}), bf16[32,8,4,4,1024]{4,1,3,2,0:T(8,128)(2,1)}) %all-gather.6.cloned.1.call-update) | async-done | bytes 8388624 | tf_op jit(solution)/shard_map/all_gather | solution.py:44
  99.9 5.8 %fusion.55 = (bf16[1,8,32,4,1024]{4,1,3,0,2:T(8,128)(2,1)}, bf16[1,8,32,4,1024]{4,1,3,0,2:T(8,128)(2,1)S(1)}, bf16[1,8,32,4,1024]{4,1,3,0,2:T(8,128)(2,1)}, bf16[1,8,32,4,1024]{4,1,3,0,2:T(8,128)(2,1)}) fusion(bf16[4,8,32,4,1024]{4,1,3,0,2:T(8,128)(2,1)} %bitcast.141), kind=kLoop, calls=%fused_computation.105 | loop fusion | bytes 16777216 | tf_op jit(solution)/shard_map/slice | solution.py:47
  107.3 2.1 reshape_squeeze.14
  109.4 4.6 %copy.102 = bf16[1,8,32,4,1024]{4,3,2,1,0:T(4,128)(2,1)} copy(bf16[1,8,32,4,1024]{4,1,3,0,2:T(8,128)(2,1)} %get-tuple-element.9) | data formatting | bytes 4194304 | tf_op jit(solution)/shard_map/slice | solution.py:47
  114.0 2.5 reshape_squeeze.12
  116.6 2.0 convolution_convert_fusion
  122.3 2.0 collective-permute-done
  126.3 4.5 %copy.103 = bf16[1,8,32,4,1024]{4,3,2,1,0:T(4,128)(2,1)} copy(bf16[1,8,32,4,1024]{4,1,3,0,2:T(8,128)(2,1)} %get-tuple-element.8) | data formatting | bytes 4194304 | tf_op jit(solution)/shard_map/slice | solution.py:47
  130.8 4.0 reshape_squeeze.13
  134.9 2.1 convolution_convert_fusion.1
  137.9 4.6 %copy.112 = bf16[1,8,32,4,1024]{4,3,2,1,0:T(4,128)(2,1)} copy(bf16[1,8,32,4,1024]{4,1,3,0,2:T(8,128)(2,1)} %get-tuple-element.6) | data formatting | bytes 4194304 | tf_op jit(solution)/shard_map/slice | solution.py:47
  142.4 4.1 reshape_squeeze.15
  146.5 2.3 fusion.50
  148.8 76.9 %all-gather.8.cloned.1.call-done = f32[16,4,128,128]{3,2,1,0:T(8,128)} async-done(((f32[1,4,128,128]{3,2,1,0:T(8,128)}), f32[16,4,128,128]{3,2,1,0:T(8,128)}) %all-gather.8.cloned.1.call-update) | async-done | bytes 4194320 | tf_op jit(solution)/shard_map/all_gather | solution.py:20
  225.7 2.7 fusion.1
  235.0 1.9 collective-permute-done.2
  241.2 1.8 copy.124
  243.0 1.8 fusion.31
  248.8 2.4 convolution_multiply_fusion
  251.3 85.2 %all-gather.10.cloned.1.call-done = f32[16,4,128,128]{3,2,1,0:T(8,128)} async-done(((f32[1,4,128,128]{3,2,1,0:T(8,128)}), f32[16,4,128,128]{3,2,1,0:T(8,128)}) %all-gather.10.cloned.1.call-update) | async-done | bytes 4194320 | tf_op jit(solution)/shard_map/all_gather | solution.py:20
  336.5 2.7 fusion
  340.9 2.5 convolution_multiply_fusion.1
  343.4 2.2 reshape.255
  345.7 2.2 reshape.253
  347.9 2.6 pad_maximum_fusion
  353.1 4.6 %all-to-all-start.1 = ((bf16[16,64,1024]{2,1,0:T(8,128)(2,1)}), bf16[16,64,1024]{2,1,0:T(8,128)(2,1)}, u32[]{:S(2)}, u32[]{:S(2)}) async-start(bf16[16,64,1024]{2,1,0:T(8,128)(2,1)} %bitcast.142), calls=%async_computation.1 | async-start | bytes 4194304 | tf_op jit(solution)/shard_map/all_to_all | solution.py:72
  360.2 2.5 fusion.58
  366.4 46.1 %all-to-all-done.1 = bf16[16,64,1024]{2,1,0:T(8,128)(2,1)} async-done(((bf16[16,64,1024]{2,1,0:T(8,128)(2,1)}), bf16[16,64,1024]{2,1,0:T(8,128)(2,1)}, u32[]{:S(2)}, u32[]{:S(2)}) %all-to-all-start.1) | async-done | bytes 2097184 | tf_op jit(solution)/shard_map/all_to_all | solution.py:72
  412.6 2.7 convert_reduce_fusion
  415.3 4.2 all-to-all-start.2
  420.4 9.0 %all-to-all-done.2 = f32[8,8,1024]{2,1,0:T(8,128)S(1)} async-done(((f32[8,8,1024]{2,1,0:T(8,128)}), f32[8,8,1024]{2,1,0:T(8,128)S(1)}, u32[]{:S(2)}, u32[]{:S(2)}) %all-to-all-start.2) | async-done | bytes 262176 | tf_op jit(solution)/shard_map/all_to_all | solution.py:75
  (117 shorter events, 38.7 us)
Async XLA Ops:
  7.2 25.0 %copy-start.2 = (bf16[1,128,1024]{2,1,0:T(8,128)(2,1)S(1)}, bf16[1,128,1024]{2,1,0:T(8,128)(2,1)}, u32[]{:S(2)}) copy-start(bf16[1,128,1024]{2,1,0:T(8,128)(2,1)} %param.9) | copy-start | bytes 786436
  7.2 92.8 %all-gather.6.cloned.1.call-start = ((), (), s32[]{:S(2)}) async-start(), calls=%async_computation.3 | async-start | bytes 8650752 | tf_op jit(solution)/shard_map/all_gather | solution.py:44
  31.1 194.7 %all-gather.8.cloned.1.call-start = ((), (), s32[]{:S(2)}) async-start(), calls=%async_computation.4 | async-start | bytes 4456448 | tf_op jit(solution)/shard_map/all_gather | solution.py:20
  118.6 3.4 copy-start.7
  121.0 9.9 %copy-start.12 = (bf16[128,8,128]{0,2,1:T(8,128)(2,1)}, bf16[128,8,128]{0,2,1:T(8,128)(2,1)S(1)}, u32[]{:S(2)}) copy-start(bf16[128,8,128]{0,2,1:T(8,128)(2,1)S(1)} %copy.108) | copy-start | bytes 786436
  122.0 2.3 collective-permute-start
  126.1 210.4 %all-gather.10.cloned.1.call-start = ((), (), s32[]{:S(2)}) async-start(), calls=%async_computation.5 | async-start | bytes 4456448 | tf_op jit(solution)/shard_map/all_gather | solution.py:20
  225.7 4.3 copy-start.5
  225.7 4.3 copy-start.8
  228.5 2.7 collective-permute-start.1
  234.9 11.7 %copy-start.4 = (bf16[128,8,128]{0,2,1:T(8,128)(2,1)S(1)}, bf16[128,8,128]{0,2,1:T(8,128)(2,1)}, u32[]{:S(2)}) copy-start(bf16[128,8,128]{0,2,1:T(8,128)(2,1)} %copy-done.3) | copy-start | bytes 786436
  234.9 2.0 collective-permute-start.2
  239.3 1.9 collective-permute-start.4
  239.4 9.4 %collective-permute-start.7 = (bf16[128,1024]{1,0:T(8,128)(2,1)}, bf16[128,1024]{1,0:T(8,128)(2,1)}, u32[]{:S(2)}, u32[]{:S(2)}) collective-permute-start(bf16[128,1024]{1,0:T(8,128)(2,1)} %bitcast.12), channel_id=1, source_target_pairs={{0,1},{1,0},{2,3},{3,2},{4,5},{5,4},{6,7},{7,6},{8,9},{9,8},{10,11... | collective-permute-start | bytes 786440 | tf_op jit(solution)/shard_map/ppermute | solution.py:58
  239.8 7.5 %copy-start.11 = (bf16[8,128,128]{2,1,0:T(8,128)(2,1)S(1)}, bf16[8,128,128]{2,1,0:T(8,128)(2,1)}, u32[]{:S(2)}) copy-start(bf16[8,128,128]{2,1,0:T(8,128)(2,1)} %copy-done.10) | copy-start | bytes 786436
  240.7 6.3 %copy-start.13 = (bf16[128,8,128]{0,2,1:T(8,128)(2,1)S(1)}, bf16[128,8,128]{0,2,1:T(8,128)(2,1)}, u32[]{:S(2)}) copy-start(bf16[128,8,128]{0,2,1:T(8,128)(2,1)} %copy-done.12) | copy-start | bytes 786436
  246.5 2.1 copy-start.14
  246.5 2.1 collective-permute-start.6
  247.0 1.6 copy-start.19
  248.2 92.7 %collective-permute-start.5 = (bf16[128,1024]{0,1:T(8,128)(2,1)}, bf16[128,1024]{0,1:T(8,128)(2,1)}, u32[]{:S(2)}, u32[]{:S(2)}) collective-permute-start(bf16[128,1024]{0,1:T(8,128)(2,1)} %bitcast.19), channel_id=1, source_target_pairs={{0,1},{1,0},{2,3},{3,2},{4,5},{5,4},{6,7},{7,6},{8,9},{9,8},{10,11... | collective-permute-start | bytes 786440 | tf_op jit(solution)/shard_map/ppermute | solution.py:58
  251.3 89.7 %copy-start.20 = (bf16[256,512]{0,1:T(8,128)(2,1)S(1)}, bf16[256,512]{0,1:T(8,128)(2,1)}, u32[]{:S(2)}) copy-start(bf16[256,512]{0,1:T(8,128)(2,1)} %reshape.252) | copy-start | bytes 786436
  339.2 12.9 %collective-permute-start.3 = (f32[1,4,128,128]{3,2,1,0:T(8,128)S(1)}, f32[1,4,128,128]{3,2,1,0:T(8,128)}, u32[]{:S(2)}, u32[]{:S(2)}) collective-permute-start(f32[1,4,128,128]{3,2,1,0:T(8,128)S(1)} %bitcast.152), channel_id=1, source_target_pairs={{0,1},{1,0},{2,3},{3,2},{4,5},{5,4},{6,7},{7,6},{8,9},{9,8},{10,11... | collective-permute-start | bytes 786440 | tf_op jit(solution)/shard_map/ppermute | solution.py:24
  350.5 2.5 copy-start.17
  353.1 4.6 %copy-start.6 = (bf16[128,1024]{0,1:T(8,128)(2,1)S(1)}, bf16[128,1024]{0,1:T(8,128)(2,1)}, u32[]{:S(2)}) copy-start(bf16[128,1024]{0,1:T(8,128)(2,1)} %copy.133) | copy-start | bytes 786436
  353.1 59.4 %all-to-all-start.1 = ((bf16[16,64,1024]{2,1,0:T(8,128)(2,1)}), bf16[16,64,1024]{2,1,0:T(8,128)(2,1)}, u32[]{:S(2)}, u32[]{:S(2)}) async-start(bf16[16,64,1024]{2,1,0:T(8,128)(2,1)} %bitcast.142), calls=%async_computation.1 | async-start | bytes 4194304 | tf_op jit(solution)/shard_map/all_to_all | solution.py:72
  358.9 3.9 copy-start.1
  358.9 3.9 copy-start.15
  358.9 3.9 copy-start.22
  362.8 1.5 copy-start.9
  362.8 1.8 copy-start
  366.4 53.1 %copy-start.21 = (bf16[1,128,1024]{2,1,0:T(8,128)(2,1)S(1)}, bf16[1,128,1024]{2,1,0:T(8,128)(2,1)}, u32[]{:S(2)}) copy-start(bf16[1,128,1024]{2,1,0:T(8,128)(2,1)} %param.11) | copy-start | bytes 786436
  415.3 14.2 %all-to-all-start.2 = ((f32[8,8,1024]{2,1,0:T(8,128)}), f32[8,8,1024]{2,1,0:T(8,128)S(1)}, u32[]{:S(2)}, u32[]{:S(2)}) async-start(f32[8,8,1024]{2,1,0:T(8,128)} %bitcast.40), calls=%async_computation.2 | async-start | bytes 524288 | tf_op jit(solution)/shard_map/all_to_all | solution.py:75
  (4 other events, 3.1 us)
Sparse Core Ops, SparseCore 0:
  31.2 68.7 all-gather.5
  126.2 99.4 all-gather.7
  238.6 97.8 all-gather.9

commit v9 on v8

--- a/solution.py
+++ b/solution.py
@@ -32,20 +32,29 @@
 def gather_rows(weights, piece):
     place = lax.axis_index(CTX)
     width = weights[0].shape[1]
+    blocks = lax.axis_size("dp")
     parts = [lax.dynamic_slice_in_dim(weight, place * piece, piece, 0) for weight in weights]
     joined = jnp.concatenate(parts, 0)
-    copies = jnp.broadcast_to(joined[None], (lax.axis_size("dp"),) + joined.shape)
+    copies = jnp.broadcast_to(joined[None], (blocks,) + joined.shape)
     across = lax.all_to_all(copies, "dp", 0, 0, tiled=False)
-    return across.reshape(across.shape[0], len(weights), piece, width)
+    across = across.reshape(blocks, len(weights), piece, width)
+    across = jnp.transpose(across, (1, 0, 2, 3)).reshape(len(weights), blocks * piece, width)
+    gathered = lax.all_gather(across, CTX, axis=1, tiled=False)
+    return tuple(gathered[index].reshape(-1, width) for index in range(len(weights)))
 
 
-def spread_rows(across):
-    blocks, count, piece, width = across.shape
-    gathered = lax.all_gather(across, CTX, axis=0, tiled=False)
-    gathered = jnp.transpose(gathered, (2, 1, 0, 3, 4))
-    return tuple(
-        gathered[index].reshape(-1, width) for index in range(count)
-    )
+def to_gathered(values, blocks, piece):
+    lead = values.shape[:-1]
+    split = values.reshape(lead + (blocks, -1, piece))
+    order = tuple(range(len(lead))) + (len(lead) + 1, len(lead), len(lead) + 2)
+    return jnp.transpose(split, order).reshape(values.shape)
+
+
+def from_gathered(values, blocks, piece):
+    lead = values.shape[:-1]
+    split = values.reshape(lead + (-1, blocks, piece))
+    order = tuple(range(len(lead))) + (len(lead) + 1, len(lead), len(lead) + 2)
+    return jnp.transpose(split, order).reshape(values.shape)
 
 
 def weight_grads(pairs, factor, wait_for):
@@ -83,15 +92,18 @@
     owners = lax.axis_size("dp") * lax.axis_size(CTX)
     factor = float(batch * tokens_here * owners) ** (-0.5)
     piece = w_query.shape[0] // lax.axis_size(CTX)
-    across = gather_rows((w_query, w_key, w_value, w_out), piece)
-    full_query, full_key, full_value, full_out = spread_rows(across)
+    blocks = lax.axis_size("dp")
+    full_query, full_key, full_value, full_out = gather_rows(
+        (w_query, w_key, w_value, w_out), piece
+    )
     second_wide = x_second.astype(jnp.float32)
     inv_rms = lax.rsqrt(jnp.mean(second_wide * second_wide, -1, keepdims=True) + 1e-06)
     normed_wide = second_wide * inv_rms
     normed = normed_wide.astype(jnp.bfloat16)
+    normed_moved = to_gathered(normed, blocks, piece)
 
     def project(weight):
-        made = jnp.einsum("btd,df->btf", normed, weight, preferred_element_type=jnp.float32)
+        made = jnp.einsum("btd,df->btf", normed_moved, weight, preferred_element_type=jnp.float32)
         return made.astype(jnp.bfloat16).reshape(batch, tokens_here, HEADS, HEAD_DIM)
 
     queries = project(full_query)
@@ -111,9 +123,11 @@
     inv_head = lax.rsqrt(jnp.mean(mixed * mixed, -1, keepdims=True) + 1e-06)
     unit = mixed * inv_head
     attn_out = unit.astype(jnp.bfloat16).reshape(batch, tokens_here, width)
-    attended = jnp.einsum("btf,fd->btd", attn_out, full_out, preferred_element_type=jnp.float32)
+    attn_moved = to_gathered(attn_out, blocks, piece)
+    attended = jnp.einsum("btf,fd->btd", attn_moved, full_out, preferred_element_type=jnp.float32)
     x_first = (y_first.astype(jnp.float32) - attended).astype(jnp.bfloat16)
     grad_unit = jnp.einsum("btd,fd->btf", grad_first, full_out, preferred_element_type=jnp.float32)
+    grad_unit = from_gathered(grad_unit, blocks, piece)
     grad_unit = grad_unit.reshape(batch, tokens_here, HEADS, HEAD_DIM)
     grad_mixed = inv_head * (grad_unit - unit * jnp.mean(grad_unit * unit, -1, keepdims=True))
     grad_mixed = grad_mixed.astype(jnp.bfloat16)
@@ -155,6 +169,7 @@
     grad_normed = grad_normed + jnp.einsum(
         "btf,df->btd", value_grad, full_value, preferred_element_type=jnp.float32
     )
+    grad_normed = from_gathered(grad_normed, blocks, piece)
     back = inv_rms * (
         grad_normed - normed_wide * jnp.mean(grad_normed * normed_wide, -1, keepdims=True)
     )

time: 438 us -> 424 us (0.968)
  local copies, waits for them, and re-layouts: 51.9 us -> 29.5 us
  waiting for transfers between devices: 290 us -> 303 us
    slice x5 -> x1, local copies, waits for them, and re-layouts: 21.1 us -> 4.12 us  [gather_rows(): gathered[index].reshape(-1, width)]
    all_gather x2, waiting for transfers between devices: 162 us -> 178 us  [state_sum(): gathered = lax.all_gather(mine, 'cy', axis=0, tiled=False)]
    another operation x6 -> x4, local copies, waits for them, and re-layouts: 14.7 us -> 3.32 us  [the longest x4 12.7 us: spread_rows(): return tuple((gathered[index].reshape(-1, width) for index in range(count)))]
    unnamed x47 -> x43, local copies, waits for them, and re-layouts: 2.68 us -> 11.2 us
  transfers between devices with their start and end apart: 13 -> 13, of which waited for: 9 -> 7; matrix products, arithmetic and copies ran while one was open for 13% -> 11% of each run, Pallas kernels for 0% -> 0%
where the time goes in v9:
time: 424 us; the launch traced here: 423 us
  waiting for transfers between devices  303 us (71%)
  local copies, waits for them, and re-layouts  29.5 us (7%)
  matrix products  22.1 us (5%)
  blocking collectives  21.3 us (5%)
  other arithmetic  20 us (5%)
  between operations  14.2 us (3%)
  starting transfers between devices  13.2 us (3%)
    all_gather x2, waiting for transfers between devices, state_sum(): gathered = lax.all_gather(mine, 'cy', axis=0, tiled=False)  178 us
    all_gather x1, waiting for transfers between devices, gather_rows(): gathered = lax.all_gather(across, CTX, axis=1, tiled=False)  67.7 us
    all_to_all x1, waiting for transfers between devices, weight_grads(): lax.all_to_all(stacked.reshape(chips, -1, width).astype(jnp.bfloat16), 'c...  43.5 us
    all_to_all x1, blocking collectives, gather_rows(): across = lax.all_to_all(copies, 'dp', 0, 0, tiled=False)  21.3 us
    unnamed x43, local copies, waits for them, and re-layouts  11.2 us
    all_to_all x1, waiting for transfers between devices, weight_grads(): lax.all_to_all(share.reshape(outer, -1, width), 'dp', 0, 0, tiled=False)  8.97 us
  transfers between devices with their start and end apart: 13, of which 7 were waited for; matrix products, arithmetic and copies ran while one was open for 11% of the time, Pallas kernels for 0%

profile of v9, /device:TPU:1, one launch (start us, length us, event | category | flops | bytes accessed | tf_op | source)
XLA Modules:
  0.0 422.8 jit_solution(5989927514197400835)
XLA Ops:
  8.8 21.3 %all_to_all.15 = bf16[8,16,1024]{2,1,0:T(8,128)(2,1)S(1)} all-to-all(bf16[8,16,1024]{2,1,0:T(8,128)(2,1)S(1)} %broadcast_in_dim.56), channel_id=1, replica_groups=mesh['dp'=8,'cy'=16,'core'=2] {'dp'}, dimensions={0} | all-to-all | bytes 524288 | tf_op jit(solution)/shard_map/all_to_all | solution.py:39
  32.5 67.7 %all-gather.6.cloned.1.call-done = bf16[4,32,32,1024]{3,2,0,1:T(8,128)(2,1)} async-done(((bf16[4,1,32,1024]{3,2,0,1:T(8,128)(2,1)}), bf16[4,32,32,1024]{3,2,0,1:T(8,128)(2,1)}) %all-gather.6.cloned.1.call-update) | async-done | bytes 8388624 | tf_op jit(solution)/shard_map/all_gather | solution.py:42
  100.2 5.5 %slice_bitcast_fusion = (bf16[1,32,32,1024]{3,2,1,0:T(8,128)(2,1)}, bf16[1,32,32,1024]{3,2,0,1:T(8,128)(2,1)S(1)}, bf16[1,32,32,1024]{3,2,0,1:T(8,128)(2,1)}, bf...) fusion(bf16[4,32,32,1024]{3,2,0,1:T(8,128)(2,1)} %all-gather.6.cloned.1.call-done), kind=kLoop, calls=%fused_computation.101 | loop fusion | bytes 18874368
  105.7 1.3 copy-done
  109.6 2.0 collective-permute-done
  111.6 1.8 dynamic-slice_add_fusion.1
  113.4 2.8 convolution_convert_fusion.1
  117.3 4.1 copy.142
  121.8 91.2 %all-gather.8.cloned.1.call-done = f32[16,4,128,128]{3,2,1,0:T(8,128)} async-done(((f32[1,4,128,128]{3,2,1,0:T(8,128)}), f32[16,4,128,128]{3,2,1,0:T(8,128)}) %all-gather.8.cloned.1.call-update) | async-done | bytes 4194320 | tf_op jit(solution)/shard_map/all_gather | solution.py:20
  213.0 2.8 fusion.1
  215.8 1.6 collective-permute-start.1
  221.6 1.9 collective-permute-done.2
  226.8 1.4 fusion.51
  233.3 2.6 convolution_multiply_fusion.1
  235.8 87.2 %all-gather.10.cloned.1.call-done = f32[16,4,128,128]{3,2,1,0:T(8,128)} async-done(((f32[1,4,128,128]{3,2,1,0:T(8,128)}), f32[16,4,128,128]{3,2,1,0:T(8,128)}) %all-gather.10.cloned.1.call-update) | async-done | bytes 4194320 | tf_op jit(solution)/shard_map/all_gather | solution.py:20
  323.1 2.7 fusion
  325.8 1.6 collective-permute-start.3
  327.4 2.4 convolution_multiply_fusion
  329.8 2.3 reshape.280
  332.1 2.2 reshape.282
  334.3 2.6 pad_maximum_fusion
  336.9 1.5 copy.165
  339.5 4.4 %all-to-all-start.1 = ((bf16[16,64,1024]{2,1,0:T(8,128)(2,1)}), bf16[16,64,1024]{2,1,0:T(8,128)(2,1)}, u32[]{:S(2)}, u32[]{:S(2)}) async-start(bf16[16,64,1024]{2,1,0:T(8,128)(2,1)} %bitcast.178), calls=%async_computation.1 | async-start | bytes 4194304 | tf_op jit(solution)/shard_map/all_to_all | solution.py:81
  344.0 1.8 copy.141
  345.8 1.2 copy.139
  348.2 1.3 fusion.53
  349.5 1.8 fusion.52
  351.3 1.2 fusion.6
  355.3 43.5 %all-to-all-done.1 = bf16[16,64,1024]{2,1,0:T(8,128)(2,1)} async-done(((bf16[16,64,1024]{2,1,0:T(8,128)(2,1)}), bf16[16,64,1024]{2,1,0:T(8,128)(2,1)}, u32[]{:S(2)}, u32[]{:S(2)}) %all-to-all-start.1) | async-done | bytes 2097184 | tf_op jit(solution)/shard_map/all_to_all | solution.py:81
  398.8 2.7 convert_reduce_fusion
  401.5 4.1 all-to-all-start.2
  406.7 9.0 %all-to-all-done.2 = f32[8,8,1024]{2,1,0:T(8,128)S(1)} async-done(((f32[8,8,1024]{2,1,0:T(8,128)}), f32[8,8,1024]{2,1,0:T(8,128)S(1)}, u32[]{:S(2)}, u32[]{:S(2)}) %all-to-all-start.2) | async-done | bytes 262176 | tf_op jit(solution)/shard_map/all_to_all | solution.py:84
  (111 shorter events, 27.2 us)
Async XLA Ops:
  7.2 24.2 %copy-start.14 = (bf16[1,128,1024]{2,1,0:T(8,128)(2,1)S(1)}, bf16[1,128,1024]{2,1,0:T(8,128)(2,1)}, u32[]{:S(2)}) copy-start(bf16[1,128,1024]{2,1,0:T(8,128)(2,1)} %param.9) | copy-start | bytes 786436
  7.2 93.0 %all-gather.6.cloned.1.call-start = ((), (), s32[]{:S(2)}) async-start(), calls=%async_computation.3 | async-start | bytes 8650752 | tf_op jit(solution)/shard_map/all_gather | solution.py:42
  31.3 181.7 %all-gather.8.cloned.1.call-start = ((), (), s32[]{:S(2)}) async-start(), calls=%async_computation.4 | async-start | bytes 4456448 | tf_op jit(solution)/shard_map/all_gather | solution.py:20
  31.8 0.7 copy-start.7
  105.7 1.3 copy-start
  107.5 14.0 %copy-start.5 = (bf16[128,1024]{1,0:T(8,128)(2,1)}, bf16[128,1024]{1,0:T(8,128)(2,1)S(1)}, u32[]{:S(2)}) copy-start(bf16[128,1024]{1,0:T(8,128)(2,1)S(1)} %convolution_convert_fusion) | copy-start | bytes 786436
  107.8 5.5 %copy-start.8 = (bf16[128,8,128]{0,2,1:T(8,128)(2,1)}, bf16[128,8,128]{0,2,1:T(8,128)(2,1)S(1)}, u32[]{:S(2)}) copy-start(bf16[128,8,128]{0,2,1:T(8,128)(2,1)S(1)} %copy.135) | copy-start | bytes 786436
  109.3 2.3 collective-permute-start
  113.3 209.7 %all-gather.10.cloned.1.call-start = ((), (), s32[]{:S(2)}) async-start(), calls=%async_computation.5 | async-start | bytes 4456448 | tf_op jit(solution)/shard_map/all_gather | solution.py:20
  121.8 96.7 %copy-start.12 = (bf16[8,128,128]{2,1,0:T(8,128)(2,1)}, bf16[8,128,128]{2,1,0:T(8,128)(2,1)S(1)}, u32[]{:S(2)}) copy-start(bf16[8,128,128]{2,1,0:T(8,128)(2,1)S(1)} %fusion.4) | copy-start | bytes 786436
  121.8 95.6 %copy-start.16 = (bf16[1,128,1024]{2,1,0:T(8,128)(2,1)S(1)}, bf16[1,128,1024]{2,1,0:T(8,128)(2,1)}, u32[]{:S(2)}) copy-start(bf16[1,128,1024]{2,1,0:T(8,128)(2,1)} %param.10) | copy-start | bytes 786436
  213.0 4.4 %copy-start.4 = (bf16[1,32,32,1024]{3,1,2,0:T(8,128)(2,1)S(1)}, bf16[1,32,32,1024]{3,1,2,0:T(8,128)(2,1)}, u32[]{:S(2)}) copy-start(bf16[1,32,32,1024]{3,1,2,0:T(8,128)(2,1)} %copy.142) | copy-start | bytes 6291460
  215.8 3.0 collective-permute-start.1
  221.5 2.0 collective-permute-start.2
  223.5 0.8 copy-start.9
  225.8 3.6 collective-permute-start.4
  226.0 101.4 %collective-permute-start.7 = (bf16[128,1024]{1,0:T(8,128)(2,1)}, bf16[128,1024]{1,0:T(8,128)(2,1)}, u32[]{:S(2)}, u32[]{:S(2)}) collective-permute-start(bf16[128,1024]{1,0:T(8,128)(2,1)} %bitcast.206), channel_id=1, source_target_pairs={{0,1},{1,0},{2,3},{3,2},{4,5},{5,4},{6,7},{7,6},{8,9},{9,8},{10,11... | collective-permute-start | bytes 786440 | tf_op jit(solution)/shard_map/ppermute | solution.py:67
  226.4 5.1 %collective-permute-start.6 = (bf16[128,1024]{0,1:T(8,128)(2,1)}, bf16[128,1024]{0,1:T(8,128)(2,1)}, u32[]{:S(2)}, u32[]{:S(2)}) collective-permute-start(bf16[128,1024]{0,1:T(8,128)(2,1)} %bitcast.194), channel_id=1, source_target_pairs={{0,1},{1,0},{2,3},{3,2},{4,5},{5,4},{6,7},{7,6},{8,9},{9,8},{10,11... | collective-permute-start | bytes 786440 | tf_op jit(solution)/shard_map/ppermute | solution.py:67
  226.8 2.3 copy-start.13
  229.1 4.2 collective-permute-start.5
  323.1 4.3 %copy-start.15 = (bf16[256,512]{0,1:T(8,128)(2,1)S(1)}, bf16[256,512]{0,1:T(8,128)(2,1)}, u32[]{:S(2)}) copy-start(bf16[256,512]{0,1:T(8,128)(2,1)} %reshape.281) | copy-start | bytes 786436
  323.1 4.3 %copy-start.17 = (bf16[1,128,1024]{2,1,0:T(8,128)(2,1)S(1)}, bf16[1,128,1024]{2,1,0:T(8,128)(2,1)}, u32[]{:S(2)}) copy-start(bf16[1,128,1024]{2,1,0:T(8,128)(2,1)} %param.10) | copy-start | bytes 786436
  325.8 12.6 %collective-permute-start.3 = (f32[1,4,128,128]{3,2,1,0:T(8,128)S(1)}, f32[1,4,128,128]{3,2,1,0:T(8,128)}, u32[]{:S(2)}, u32[]{:S(2)}) collective-permute-start(f32[1,4,128,128]{3,2,1,0:T(8,128)S(1)} %bitcast.198), channel_id=1, source_target_pairs={{0,1},{1,0},{2,3},{3,2},{4,5},{5,4},{6,7},{7,6},{8,9},{9,8},{10,11... | collective-permute-start | bytes 786440 | tf_op jit(solution)/shard_map/ppermute | solution.py:24
  336.9 2.6 copy-start.10
  339.5 59.3 %all-to-all-start.1 = ((bf16[16,64,1024]{2,1,0:T(8,128)(2,1)}), bf16[16,64,1024]{2,1,0:T(8,128)(2,1)}, u32[]{:S(2)}, u32[]{:S(2)}) async-start(bf16[16,64,1024]{2,1,0:T(8,128)(2,1)} %bitcast.178), calls=%async_computation.1 | async-start | bytes 4194304 | tf_op jit(solution)/shard_map/all_to_all | solution.py:81
  345.8 3.7 copy-start.2
  348.1 3.2 copy-start.3
  348.2 3.2 copy-start.18
  351.3 1.2 copy-start.6
  351.3 1.8 copy-start.1
  355.2 50.5 %copy-start.11 = (bf16[1,128,1024]{1,2,0:T(8,128)(2,1)S(1)}, bf16[1,128,1024]{1,2,0:T(8,128)(2,1)}, u32[]{:S(2)}) copy-start(bf16[1,128,1024]{1,2,0:T(8,128)(2,1)} %copy.141) | copy-start | bytes 786436
  401.5 14.1 %all-to-all-start.2 = ((f32[8,8,1024]{2,1,0:T(8,128)}), f32[8,8,1024]{2,1,0:T(8,128)S(1)}, u32[]{:S(2)}, u32[]{:S(2)}) async-start(f32[8,8,1024]{2,1,0:T(8,128)} %bitcast.57), calls=%async_computation.2 | async-start | bytes 524288 | tf_op jit(solution)/shard_map/all_to_all | solution.py:84
Sparse Core Ops, SparseCore 0:
  31.5 68.7 all-gather.5
  113.5 99.4 all-gather.7
  225.2 97.8 all-gather.9

commit v10 on v9

--- a/solution.py
+++ b/solution.py
@@ -17,10 +17,16 @@
     both = shard + partner
     half = shard.shape[1] // 2
     mine = lax.dynamic_slice_in_dim(both, core * half, half, 1)
-    gathered = lax.all_gather(mine, "cy", axis=0, tiled=False)
-    blocks = lax.broadcasted_iota(jnp.int32, (chips,) + (1,) * mine.ndim, 0)
-    chosen = blocks > chip if later else blocks < chip
-    summed = jnp.sum(jnp.where(chosen, gathered, 0.0), axis=0)
+    total = mine
+    step = 1
+    while step < chips:
+        if later:
+            pairs = [(source, source - step) for source in range(step, chips)]
+        else:
+            pairs = [(source, source + step) for source in range(chips - step)]
+        total = total + lax.ppermute(total, "cy", pairs)
+        step *= 2
+    summed = total - mine
     other = lax.ppermute(summed, "core", swap)
     first = jnp.where(core == 0, summed, other)
     second = jnp.where(core == 0, other, summed)

time: 424 us -> 326 us (0.77)
  waiting for transfers between devices: 303 us -> 166 us
  starting transfers between devices: 13.2 us -> 48.8 us
    all_gather x2 -> x0, waiting for transfers between devices: 178 us -> none  [state_sum(): gathered = lax.all_gather(mine, 'cy', axis=0, tiled=False)]
    ppermute x0 -> x8, waiting for transfers between devices: none -> 42 us  [state_sum(): total = total + lax.ppermute(total, 'cy', pairs)]
    ppermute x0 -> x8, starting transfers between devices: none -> 31.9 us  [state_sum(): total = total + lax.ppermute(total, 'cy', pairs)]
    reduce_sum x2 -> x0, other arithmetic: 5.54 us -> none  [state_sum(): summed = jnp.sum(jnp.where(chosen, gathered, 0.0), axis=0)]
    add x0 -> x6, other arithmetic: none -> 5.09 us  [state_sum(): total = total + lax.ppermute(total, 'cy', pairs)]
    unnamed x43 -> x47, local copies, waits for them, and re-layouts: 11.2 us -> 10.3 us
  transfers between devices with their start and end apart: 13 -> 19, of which waited for: 7 -> 12; matrix products, arithmetic and copies ran while one was open for 11% -> 15% of each run, Pallas kernels for 0% -> 0%
where the time goes in v10:
time: 326 us; the launch traced here: 325 us
  waiting for transfers between devices  166 us (51%)
  starting transfers between devices  48.8 us (15%)
  local copies, waits for them, and re-layouts  29.2 us (9%)
  other arithmetic  22.5 us (7%)
  matrix products  22.1 us (7%)
  blocking collectives  21.3 us (7%)
  between operations  14.6 us (4%)
    all_gather x1, waiting for transfers between devices, gather_rows(): gathered = lax.all_gather(across, CTX, axis=1, tiled=False)  67.8 us
    all_to_all x1, waiting for transfers between devices, weight_grads(): lax.all_to_all(stacked.reshape(chips, -1, width).astype(jnp.bfloat16), 'c...  43.7 us
    ppermute x8, waiting for transfers between devices, state_sum(): total = total + lax.ppermute(total, 'cy', pairs)  42 us
    ppermute x8, starting transfers between devices, state_sum(): total = total + lax.ppermute(total, 'cy', pairs)  31.9 us
    all_to_all x1, blocking collectives, gather_rows(): across = lax.all_to_all(copies, 'dp', 0, 0, tiled=False)  21.3 us
    unnamed x47, local copies, waits for them, and re-layouts  10.3 us
    all_to_all x1, waiting for transfers between devices, weight_grads(): lax.all_to_all(share.reshape(outer, -1, width), 'dp', 0, 0, tiled=False)  8.97 us
    all_to_all x1, starting transfers between devices, weight_grads(): lax.all_to_all(share.reshape(outer, -1, width), 'dp', 0, 0, tiled=False)  6.97 us
  transfers between devices with their start and end apart: 19, of which 12 were waited for; matrix products, arithmetic and copies ran while one was open for 15% of the time, Pallas kernels for 0%

profile of v10, /device:TPU:1, one launch (start us, length us, event | category | flops | bytes accessed | tf_op | source)
XLA Modules:
  0.0 324.8 jit_solution(14569708235268522117)
XLA Ops:
  8.8 21.3 %all_to_all.15 = bf16[8,16,1024]{2,1,0:T(8,128)(2,1)S(1)} all-to-all(bf16[8,16,1024]{2,1,0:T(8,128)(2,1)S(1)} %broadcast_in_dim.38), channel_id=1, replica_groups=mesh['dp'=8,'cy'=16,'core'=2] {'dp'}, dimensions={0} | all-to-all | bytes 524288 | tf_op jit(solution)/shard_map/all_to_all | solution.py:45
  32.5 67.8 %all-gather.2.cloned.1.call-done = bf16[4,32,32,1024]{3,2,0,1:T(8,128)(2,1)} async-done(((bf16[4,1,32,1024]{3,2,0,1:T(8,128)(2,1)}), bf16[4,32,32,1024]{3,2,0,1:T(8,128)(2,1)}) %all-gather.2.cloned.1.call-update) | async-done | bytes 8388624 | tf_op jit(solution)/shard_map/all_gather | solution.py:48
  100.2 5.5 %slice_bitcast_fusion = (bf16[1,32,32,1024]{3,2,1,0:T(8,128)(2,1)}, bf16[1,32,32,1024]{3,2,0,1:T(8,128)(2,1)S(1)}, bf16[1,32,32,1024]{3,2,0,1:T(8,128)(2,1)}, bf...) fusion(bf16[4,32,32,1024]{3,2,0,1:T(8,128)(2,1)} %all-gather.2.cloned.1.call-done), kind=kLoop, calls=%fused_computation.97 | loop fusion | bytes 18874368
  109.6 2.0 collective-permute-done
  112.6 2.7 collective-permute-start.1
  115.3 5.3 %collective-permute-done.1 = f32[1,4,128,128]{3,2,1,0:T(8,128)S(1)} collective-permute-done((f32[1,4,128,128]{3,2,1,0:T(8,128)S(1)}, f32[1,4,128,128]{3,2,1,0:T(8,128)S(1)}, u32[]{:S(2)}, u32[]{:S(2)}) %collective-permute-start.1) | collective-permute-done | bytes 262176 | tf_op jit(solution)/shard_map/ppermute | solution.py:27
  120.7 4.5 %collective-permute-start.2 = (f32[1,4,128,128]{3,2,1,0:T(8,128)S(1)}, f32[1,4,128,128]{3,2,1,0:T(8,128)S(1)}, u32[]{:S(2)}, u32[]{:S(2)}) collective-permute-start(f32[1,4,128,128]{3,2,1,0:T(8,128)S(1)} %add.117), channel_id=1, source_target_pairs={{0,4},{2,6},{4,8},{6,10},{8,12},{10,14},{12,16},{14,18},{16,20},{1... | collective-permute-start | bytes 786440 | tf_op jit(solution)/shard_map/ppermute | solution.py:27
  125.3 4.6 %collective-permute-done.2 = f32[1,4,128,128]{3,2,1,0:T(8,128)S(1)} collective-permute-done((f32[1,4,128,128]{3,2,1,0:T(8,128)S(1)}, f32[1,4,128,128]{3,2,1,0:T(8,128)S(1)}, u32[]{:S(2)}, u32[]{:S(2)}) %collective-permute-start.2) | collective-permute-done | bytes 262176 | tf_op jit(solution)/shard_map/ppermute | solution.py:27
  130.6 13.6 %collective-permute-start.3 = (f32[1,4,128,128]{3,2,1,0:T(8,128)}, f32[1,4,128,128]{3,2,1,0:T(8,128)}, u32[]{:S(2)}, u32[]{:S(2)}) collective-permute-start(f32[1,4,128,128]{3,2,1,0:T(8,128)} %add.118), channel_id=1, source_target_pairs={{0,8},{2,10},{4,12},{6,14},{8,16},{10,18},{12,20},{14,22},{16,24},... | collective-permute-start | bytes 786440 | tf_op jit(solution)/shard_map/ppermute | solution.py:27
  144.2 4.7 %collective-permute-done.3 = f32[1,4,128,128]{3,2,1,0:T(8,128)} collective-permute-done((f32[1,4,128,128]{3,2,1,0:T(8,128)}, f32[1,4,128,128]{3,2,1,0:T(8,128)}, u32[]{:S(2)}, u32[]{:S(2)}) %collective-permute-start.3) | collective-permute-done | bytes 262176 | tf_op jit(solution)/shard_map/ppermute | solution.py:27
  150.7 5.8 %collective-permute-start.4 = (f32[1,4,128,128]{3,2,1,0:T(8,128)}, f32[1,4,128,128]{3,2,1,0:T(8,128)}, u32[]{:S(2)}, u32[]{:S(2)}) collective-permute-start(f32[1,4,128,128]{3,2,1,0:T(8,128)} %add.119), channel_id=1, source_target_pairs={{0,16},{2,18},{4,20},{6,22},{8,24},{10,26},{12,28},{14,30},{1,17},... | collective-permute-start | bytes 786440 | tf_op jit(solution)/shard_map/ppermute | solution.py:27
  156.5 2.8 convolution_convert_fusion.1
  160.4 2.8 copy.142
  171.6 1.9 collective-permute-done.6
  175.8 7.4 %collective-permute-done.7 = f32[1,4,128,128]{3,2,1,0:T(8,128)S(1)} collective-permute-done((f32[1,4,128,128]{3,2,1,0:T(8,128)S(1)}, f32[1,4,128,128]{3,2,1,0:T(8,128)S(1)}, u32[]{:S(2)}, u32[]{:S(2)}) %collective-permute-start.7) | collective-permute-done | bytes 262176 | tf_op jit(solution)/shard_map/ppermute | solution.py:27
  185.3 14.3 %collective-permute-done.8 = f32[1,4,128,128]{3,2,1,0:T(8,128)S(1)} collective-permute-done((f32[1,4,128,128]{3,2,1,0:T(8,128)S(1)}, f32[1,4,128,128]{3,2,1,0:T(8,128)S(1)}, u32[]{:S(2)}, u32[]{:S(2)}) %collective-permute-start.8) | collective-permute-done | bytes 262176 | tf_op jit(solution)/shard_map/ppermute | solution.py:27
  207.1 2.9 collective-permute-done.9
  213.0 2.6 convolution_multiply_fusion.1
  215.6 1.8 fusion.27
  219.1 2.8 collective-permute-done.10
  221.9 1.8 add_subtract_fusion
  223.7 2.2 collective-permute-start.11
  225.9 2.5 convolution_multiply_fusion
  228.5 2.3 reshape.264
  230.7 2.2 reshape.266
  233.0 2.6 pad_maximum_fusion
  238.2 4.5 %all-to-all-start.1 = ((bf16[16,64,1024]{2,1,0:T(8,128)(2,1)}), bf16[16,64,1024]{2,1,0:T(8,128)(2,1)}, u32[]{:S(2)}, u32[]{:S(2)}) async-start(bf16[16,64,1024]{2,1,0:T(8,128)(2,1)} %bitcast.164), calls=%async_computation.1 | async-start | bytes 4194304 | tf_op jit(solution)/shard_map/all_to_all | solution.py:87
  248.1 1.8 fusion.50
  254.0 43.7 %all-to-all-done.1 = bf16[16,64,1024]{2,1,0:T(8,128)(2,1)} async-done(((bf16[16,64,1024]{2,1,0:T(8,128)(2,1)}), bf16[16,64,1024]{2,1,0:T(8,128)(2,1)}, u32[]{:S(2)}, u32[]{:S(2)}) %all-to-all-start.1) | async-done | bytes 2097184 | tf_op jit(solution)/shard_map/all_to_all | solution.py:87
  297.6 2.7 convert_reduce_fusion
  300.3 7.0 %all-to-all-start.2 = ((f32[8,8,1024]{2,1,0:T(8,128)}), f32[8,8,1024]{2,1,0:T(8,128)S(1)}, u32[]{:S(2)}, u32[]{:S(2)}) async-start(f32[8,8,1024]{2,1,0:T(8,128)} %bitcast.53), calls=%async_computation.2 | async-start | bytes 524288 | tf_op jit(solution)/shard_map/all_to_all | solution.py:90
  308.3 9.0 %all-to-all-done.2 = f32[8,8,1024]{2,1,0:T(8,128)S(1)} async-done(((f32[8,8,1024]{2,1,0:T(8,128)}), f32[8,8,1024]{2,1,0:T(8,128)S(1)}, u32[]{:S(2)}, u32[]{:S(2)}) %all-to-all-start.2) | async-done | bytes 262176 | tf_op jit(solution)/shard_map/all_to_all | solution.py:90
  (129 shorter events, 51.0 us)
Async XLA Ops:
  7.2 24.2 %copy-start.19 = (bf16[1,128,1024]{2,1,0:T(8,128)(2,1)S(1)}, bf16[1,128,1024]{2,1,0:T(8,128)(2,1)}, u32[]{:S(2)}) copy-start(bf16[1,128,1024]{2,1,0:T(8,128)(2,1)} %param.9) | copy-start | bytes 786436
  7.2 93.0 %all-gather.2.cloned.1.call-start = ((), (), s32[]{:S(2)}) async-start(), calls=%async_computation.3 | async-start | bytes 8650752 | tf_op jit(solution)/shard_map/all_gather | solution.py:48
  107.5 55.7 %copy-start.4 = (bf16[128,1024]{1,0:T(8,128)(2,1)}, bf16[128,1024]{1,0:T(8,128)(2,1)S(1)}, u32[]{:S(2)}) copy-start(bf16[128,1024]{1,0:T(8,128)(2,1)S(1)} %convolution_convert_fusion) | copy-start | bytes 786436
  109.3 2.3 collective-permute-start
  112.6 43.9 %copy-start.10 = (f32[1,4,128,128]{3,2,1,0:T(8,128)}, f32[1,4,128,128]{3,2,1,0:T(8,128)S(1)}, u32[]{:S(2)}) copy-start(f32[1,4,128,128]{3,2,1,0:T(8,128)S(1)} %dynamic-slice_add_fusion.1) | copy-start | bytes 786436
  112.6 8.0 %collective-permute-start.1 = (f32[1,4,128,128]{3,2,1,0:T(8,128)S(1)}, f32[1,4,128,128]{3,2,1,0:T(8,128)S(1)}, u32[]{:S(2)}, u32[]{:S(2)}) collective-permute-start(f32[1,4,128,128]{3,2,1,0:T(8,128)S(1)} %dynamic-slice_add_fusion.1), channel_id=1, source_target_pairs={{0,2},{2,4},{4,6},{6,8},{8,10},{10,12},{12,14},{14,16},{16,18},{18... | collective-permute-start | bytes 786440 | tf_op jit(solution)/shard_map/ppermute | solution.py:27
  120.7 9.1 %collective-permute-start.2 = (f32[1,4,128,128]{3,2,1,0:T(8,128)S(1)}, f32[1,4,128,128]{3,2,1,0:T(8,128)S(1)}, u32[]{:S(2)}, u32[]{:S(2)}) collective-permute-start(f32[1,4,128,128]{3,2,1,0:T(8,128)S(1)} %add.117), channel_id=1, source_target_pairs={{0,4},{2,6},{4,8},{6,10},{8,12},{10,14},{12,16},{14,18},{16,20},{1... | collective-permute-start | bytes 786440 | tf_op jit(solution)/shard_map/ppermute | solution.py:27
  130.6 18.4 %collective-permute-start.3 = (f32[1,4,128,128]{3,2,1,0:T(8,128)}, f32[1,4,128,128]{3,2,1,0:T(8,128)}, u32[]{:S(2)}, u32[]{:S(2)}) collective-permute-start(f32[1,4,128,128]{3,2,1,0:T(8,128)} %add.118), channel_id=1, source_target_pairs={{0,8},{2,10},{4,12},{6,14},{8,16},{10,18},{12,20},{14,22},{16,24},... | collective-permute-start | bytes 786440 | tf_op jit(solution)/shard_map/ppermute | solution.py:27
  150.7 12.9 %collective-permute-start.4 = (f32[1,4,128,128]{3,2,1,0:T(8,128)}, f32[1,4,128,128]{3,2,1,0:T(8,128)}, u32[]{:S(2)}, u32[]{:S(2)}) collective-permute-start(f32[1,4,128,128]{3,2,1,0:T(8,128)} %add.119), channel_id=1, source_target_pairs={{0,16},{2,18},{4,20},{6,22},{8,24},{10,26},{12,28},{14,30},{1,17},... | collective-permute-start | bytes 786440 | tf_op jit(solution)/shard_map/ppermute | solution.py:27
  163.6 4.9 %copy-start.17 = (bf16[8,128,128]{2,1,0:T(8,128)(2,1)}, bf16[8,128,128]{2,1,0:T(8,128)(2,1)S(1)}, u32[]{:S(2)}) copy-start(bf16[8,128,128]{2,1,0:T(8,128)(2,1)S(1)} %fusion.2) | copy-start | bytes 786436
  164.8 4.1 %collective-permute-start.5 = (f32[1,4,128,128]{3,2,1,0:T(8,128)S(1)}, f32[1,4,128,128]{3,2,1,0:T(8,128)S(1)}, u32[]{:S(2)}, u32[]{:S(2)}) collective-permute-start(f32[1,4,128,128]{3,2,1,0:T(8,128)S(1)} %add_subtract_fusion.1), channel_id=1, source_target_pairs={{0,1},{1,0},{2,3},{3,2},{4,5},{5,4},{6,7},{7,6},{8,9},{9,8},{10,11... | collective-permute-start | bytes 786440 | tf_op jit(solution)/shard_map/ppermute | solution.py:30
  171.3 13.8 %copy-start.13 = (bf16[128,8,128]{0,2,1:T(8,128)(2,1)S(1)}, bf16[128,8,128]{0,2,1:T(8,128)(2,1)}, u32[]{:S(2)}) copy-start(bf16[128,8,128]{0,2,1:T(8,128)(2,1)} %copy-done.12) | copy-start | bytes 786436
  171.6 2.0 collective-permute-start.6
  173.5 9.7 %copy-start.14 = (f32[1,8,128,128]{3,2,1,0:T(8,128)}, f32[1,8,128,128]{3,2,1,0:T(8,128)S(1)}, u32[]{:S(2)}) copy-start(f32[1,8,128,128]{3,2,1,0:T(8,128)S(1)} %collective-permute-done.6) | copy-start | bytes 1572868
  173.6 9.6 %copy-start.8 = (f32[1,4,128,128]{3,2,1,0:T(8,128)}, f32[1,4,128,128]{3,2,1,0:T(8,128)S(1)}, u32[]{:S(2)}) copy-start(f32[1,4,128,128]{3,2,1,0:T(8,128)S(1)} %dynamic-slice_add_fusion) | copy-start | bytes 786436
  173.6 9.6 %collective-permute-start.7 = (f32[1,4,128,128]{3,2,1,0:T(8,128)S(1)}, f32[1,4,128,128]{3,2,1,0:T(8,128)S(1)}, u32[]{:S(2)}, u32[]{:S(2)}) collective-permute-start(f32[1,4,128,128]{3,2,1,0:T(8,128)S(1)} %dynamic-slice_add_fusion), channel_id=1, source_target_pairs={{2,0},{4,2},{6,4},{8,6},{10,8},{12,10},{14,12},{16,14},{18,16},{20... | collective-permute-start | bytes 786440 | tf_op jit(solution)/shard_map/ppermute | solution.py:27
  175.7 27.9 %collective-permute-start.12 = (bf16[128,1024]{0,1:T(8,128)(2,1)}, bf16[128,1024]{0,1:T(8,128)(2,1)}, u32[]{:S(2)}, u32[]{:S(2)}) collective-permute-start(bf16[128,1024]{0,1:T(8,128)(2,1)} %fusion.86), channel_id=1, source_target_pairs={{0,1},{1,0},{2,3},{3,2},{4,5},{5,4},{6,7},{7,6},{8,9},{9,8},{10,11... | collective-permute-start | bytes 786440 | tf_op jit(solution)/shard_map/ppermute | solution.py:73
  183.3 20.3 %copy-start.7 = (bf16[1,128,1024]{1,2,0:T(8,128)(2,1)S(1)}, bf16[1,128,1024]{1,2,0:T(8,128)(2,1)}, u32[]{:S(2)}) copy-start(bf16[1,128,1024]{1,2,0:T(8,128)(2,1)} %copy-done.6) | copy-start | bytes 786436
  183.3 16.3 %collective-permute-start.8 = (f32[1,4,128,128]{3,2,1,0:T(8,128)S(1)}, f32[1,4,128,128]{3,2,1,0:T(8,128)S(1)}, u32[]{:S(2)}, u32[]{:S(2)}) collective-permute-start(f32[1,4,128,128]{3,2,1,0:T(8,128)S(1)} %add.129), channel_id=1, source_target_pairs={{4,0},{6,2},{8,4},{10,6},{12,8},{14,10},{16,12},{18,14},{20,16},{2... | collective-permute-start | bytes 786440 | tf_op jit(solution)/shard_map/ppermute | solution.py:27
  185.0 17.5 %copy-start.18 = (bf16[8,128,128]{2,1,0:T(8,128)(2,1)}, bf16[8,128,128]{2,1,0:T(8,128)(2,1)S(1)}, u32[]{:S(2)}) copy-start(bf16[8,128,128]{2,1,0:T(8,128)(2,1)S(1)} %fusion.3) | copy-start | bytes 786436
  200.4 9.6 %collective-permute-start.9 = (f32[1,4,128,128]{3,2,1,0:T(8,128)}, f32[1,4,128,128]{3,2,1,0:T(8,128)}, u32[]{:S(2)}, u32[]{:S(2)}) collective-permute-start(f32[1,4,128,128]{3,2,1,0:T(8,128)} %add.130), channel_id=1, source_target_pairs={{8,0},{10,2},{12,4},{14,6},{16,8},{18,10},{20,12},{22,14},{24,16},... | collective-permute-start | bytes 786440 | tf_op jit(solution)/shard_map/ppermute | solution.py:27
  202.6 10.4 %collective-permute-start.13 = (bf16[128,1024]{0,1:T(8,128)(2,1)}, bf16[128,1024]{0,1:T(8,128)(2,1)}, u32[]{:S(2)}, u32[]{:S(2)}) collective-permute-start(bf16[128,1024]{0,1:T(8,128)(2,1)} %bitcast.30), channel_id=1, source_target_pairs={{0,1},{1,0},{2,3},{3,2},{4,5},{5,4},{6,7},{7,6},{8,9},{9,8},{10,11... | collective-permute-start | bytes 786440 | tf_op jit(solution)/shard_map/ppermute | solution.py:73
  203.1 22.9 %collective-permute-start.15 = (bf16[128,1024]{1,0:T(8,128)(2,1)}, bf16[128,1024]{1,0:T(8,128)(2,1)}, u32[]{:S(2)}, u32[]{:S(2)}) collective-permute-start(bf16[128,1024]{1,0:T(8,128)(2,1)} %bitcast.20), channel_id=1, source_target_pairs={{0,1},{1,0},{2,3},{3,2},{4,5},{5,4},{6,7},{7,6},{8,9},{9,8},{10,11... | collective-permute-start | bytes 786440 | tf_op jit(solution)/shard_map/ppermute | solution.py:73
  203.1 12.5 %collective-permute-start.14 = (bf16[128,1024]{0,1:T(8,128)(2,1)}, bf16[128,1024]{0,1:T(8,128)(2,1)}, u32[]{:S(2)}, u32[]{:S(2)}) collective-permute-start(bf16[128,1024]{0,1:T(8,128)(2,1)} %bitcast.180), channel_id=1, source_target_pairs={{0,1},{1,0},{2,3},{3,2},{4,5},{5,4},{6,7},{7,6},{8,9},{9,8},{10,11... | collective-permute-start | bytes 786440 | tf_op jit(solution)/shard_map/ppermute | solution.py:73
  207.1 14.9 %copy-start.9 = (f32[1,4,128,128]{3,2,1,0:T(8,128)S(1)}, f32[1,4,128,128]{3,2,1,0:T(8,128)}, u32[]{:S(2)}) copy-start(f32[1,4,128,128]{3,2,1,0:T(8,128)} %copy-done.8) | copy-start | bytes 786436
  211.7 10.2 %collective-permute-start.10 = (f32[1,4,128,128]{3,2,1,0:T(8,128)}, f32[1,4,128,128]{3,2,1,0:T(8,128)}, u32[]{:S(2)}, u32[]{:S(2)}) collective-permute-start(f32[1,4,128,128]{3,2,1,0:T(8,128)} %add.131), channel_id=1, source_target_pairs={{16,0},{18,2},{20,4},{22,6},{24,8},{26,10},{28,12},{30,14},{17,1},... | collective-permute-start | bytes 786440 | tf_op jit(solution)/shard_map/ppermute | solution.py:27
  223.7 13.4 %collective-permute-start.11 = (f32[1,4,128,128]{3,2,1,0:T(8,128)}, f32[1,4,128,128]{3,2,1,0:T(8,128)S(1)}, u32[]{:S(2)}, u32[]{:S(2)}) collective-permute-start(f32[1,4,128,128]{3,2,1,0:T(8,128)} %add_subtract_fusion), channel_id=1, source_target_pairs={{0,1},{1,0},{2,3},{3,2},{4,5},{5,4},{6,7},{7,6},{8,9},{9,8},{10,11... | collective-permute-start | bytes 786440 | tf_op jit(solution)/shard_map/ppermute | solution.py:30
  238.2 59.5 %all-to-all-start.1 = ((bf16[16,64,1024]{2,1,0:T(8,128)(2,1)}), bf16[16,64,1024]{2,1,0:T(8,128)(2,1)}, u32[]{:S(2)}, u32[]{:S(2)}) async-start(bf16[16,64,1024]{2,1,0:T(8,128)(2,1)} %bitcast.164), calls=%async_computation.1 | async-start | bytes 4194304 | tf_op jit(solution)/shard_map/all_to_all | solution.py:87
  244.4 3.7 %copy-start.2 = (bf16[1,32,32,1024]{3,2,0,1:T(8,128)(2,1)S(1)}, bf16[1,32,32,1024]{3,2,0,1:T(8,128)(2,1)}, u32[]{:S(2)}) copy-start(bf16[1,32,32,1024]{3,2,0,1:T(8,128)(2,1)} %get-tuple-element.24) | copy-start | bytes 6291460
  246.8 3.2 copy-start.3
  253.8 53.5 %copy-start.16 = (bf16[1,128,1024]{1,2,0:T(8,128)(2,1)S(1)}, bf16[1,128,1024]{1,2,0:T(8,128)(2,1)}, u32[]{:S(2)}) copy-start(bf16[1,128,1024]{1,2,0:T(8,128)(2,1)} %copy.141) | copy-start | bytes 786436
  300.3 17.0 %all-to-all-start.2 = ((f32[8,8,1024]{2,1,0:T(8,128)}), f32[8,8,1024]{2,1,0:T(8,128)S(1)}, u32[]{:S(2)}, u32[]{:S(2)}) async-start(f32[8,8,1024]{2,1,0:T(8,128)} %bitcast.53), calls=%async_computation.2 | async-start | bytes 524288 | tf_op jit(solution)/shard_map/all_to_all | solution.py:90
  (8 other events, 15.7 us)
Sparse Core Ops, SparseCore 0:
  31.5 68.7 all-gather.1

commit v11 on v10

--- a/solution.py
+++ b/solution.py
@@ -63,7 +63,7 @@
     return jnp.transpose(split, order).reshape(values.shape)
 
 
-def weight_grads(pairs, factor, wait_for):
+def weight_grads(pairs, factor):
     width = pairs[0][0].shape[1]
     outer, chips, cores = lax.axis_size("dp"), lax.axis_size("cy"), lax.axis_size("core")
     mine = lax.axis_index("core")
@@ -83,7 +83,6 @@
     rows = blocks[0].shape[2]
     stacked = jnp.concatenate(blocks, 2)
     stacked = jnp.transpose(stacked, (1, 0, 2, 3)).reshape(-1, width)
-    stacked, _ = lax.optimization_barrier((stacked, wait_for))
     share = lax.all_to_all(
         stacked.reshape(chips, -1, width).astype(jnp.bfloat16), "cy", 0, 0, tiled=False
     ).astype(jnp.float32).sum(0)
@@ -184,7 +183,7 @@
         (normed.reshape(-1, width), query_grad.reshape(-1, width)),
         (attn_out.reshape(-1, width), grad_first.reshape(-1, width)),
     )
-    grad_query, grad_out = weight_grads(pairs, factor, after_state)
+    grad_query, grad_out = weight_grads(pairs, factor)
     return (x_first, grad_x_second, grad_query, grad_out)
 
 

time: 326 us -> 328 us (level)
    ppermute x8, waiting for transfers between devices: 42 us -> 89.6 us  [state_sum(): total = total + lax.ppermute(total, 'cy', pairs)]
    all_to_all x1, waiting for transfers between devices: 43.7 us -> 0.01 us  [weight_grads(): lax.all_to_all(stacked.reshape(chips, -1, width).astype(jnp.bfloat16), 'c...]
    convert_element_type x1, other arithmetic: 0.08 us -> 3.86 us  [weight_grads(): stacked.reshape(chips, -1, width).astype(jnp.bfloat16)]
    unnamed x47 -> x39, local copies, waits for them, and re-layouts: 10.3 us -> 11.2 us
  transfers between devices with their start and end apart: 19 -> 19, of which waited for: 12 -> 11; matrix products, arithmetic and copies ran while one was open for 15% -> 16% of each run, Pallas kernels for 0% -> 0%
where the time goes in v11:
time: 328 us; the launch traced here: 327 us
  waiting for transfers between devices  169 us (52%)
  starting transfers between devices  50.4 us (15%)
  local copies, waits for them, and re-layouts  28.4 us (9%)
  other arithmetic  21.5 us (7%)
  matrix products  21.5 us (7%)
  blocking collectives  21.3 us (6%)
  between operations  14.6 us (4%)
    ppermute x8, waiting for transfers between devices, state_sum(): total = total + lax.ppermute(total, 'cy', pairs)  89.6 us
    all_gather x1, waiting for transfers between devices, gather_rows(): gathered = lax.all_gather(across, CTX, axis=1, tiled=False)  67.7 us
    ppermute x8, starting transfers between devices, state_sum(): total = total + lax.ppermute(total, 'cy', pairs)  31.9 us
    all_to_all x1, blocking collectives, gather_rows(): across = lax.all_to_all(copies, 'dp', 0, 0, tiled=False)  21.3 us
    unnamed x39, local copies, waits for them, and re-layouts  11.2 us
    all_to_all x1, waiting for transfers between devices, weight_grads(): lax.all_to_all(share.reshape(outer, -1, width), 'dp', 0, 0, tiled=False)  9.01 us
    all_to_all x1, starting transfers between devices, weight_grads(): lax.all_to_all(share.reshape(outer, -1, width), 'dp', 0, 0, tiled=False)  7.22 us
  transfers between devices with their start and end apart: 19, of which 11 were waited for; matrix products, arithmetic and copies ran while one was open for 16% of the time, Pallas kernels for 0%

profile of v11, /device:TPU:1, one launch (start us, length us, event | category | flops | bytes accessed | tf_op | source)
XLA Modules:
  0.0 326.7 jit_solution(311285129323685309)
XLA Ops:
  8.8 21.3 %all_to_all.15 = bf16[8,16,1024]{2,1,0:T(8,128)(2,1)S(1)} all-to-all(bf16[8,16,1024]{2,1,0:T(8,128)(2,1)S(1)} %broadcast_in_dim.38), channel_id=1, replica_groups=mesh['dp'=8,'cy'=16,'core'=2] {'dp'}, dimensions={0} | all-to-all | bytes 524288 | tf_op jit(solution)/shard_map/all_to_all | solution.py:45
  32.5 67.7 %all-gather.2.cloned.1.call-done = bf16[4,32,32,1024]{3,2,0,1:T(8,128)(2,1)} async-done(((bf16[4,1,32,1024]{3,2,0,1:T(8,128)(2,1)}), bf16[4,32,32,1024]{3,2,0,1:T(8,128)(2,1)}) %all-gather.2.cloned.1.call-update) | async-done | bytes 8388624 | tf_op jit(solution)/shard_map/all_gather | solution.py:48
  100.2 5.5 %slice_bitcast_fusion = (bf16[1,32,32,1024]{3,2,1,0:T(8,128)(2,1)}, bf16[1,32,32,1024]{3,2,0,1:T(8,128)(2,1)S(1)}, bf16[1,32,32,1024]{3,2,0,1:T(8,128)(2,1)}, bf...) fusion(bf16[4,32,32,1024]{3,2,0,1:T(8,128)(2,1)} %all-gather.2.cloned.1.call-done), kind=kLoop, calls=%fused_computation.97 | loop fusion | bytes 18874368
  109.6 2.0 collective-permute-done
  112.6 2.7 collective-permute-start.1
  115.3 5.3 %collective-permute-done.1 = f32[1,4,128,128]{3,2,1,0:T(8,128)S(1)} collective-permute-done((f32[1,4,128,128]{3,2,1,0:T(8,128)S(1)}, f32[1,4,128,128]{3,2,1,0:T(8,128)S(1)}, u32[]{:S(2)}, u32[]{:S(2)}) %collective-permute-start.1) | collective-permute-done | bytes 262176 | tf_op jit(solution)/shard_map/ppermute | solution.py:27
  120.7 4.5 %collective-permute-start.2 = (f32[1,4,128,128]{3,2,1,0:T(8,128)S(1)}, f32[1,4,128,128]{3,2,1,0:T(8,128)S(1)}, u32[]{:S(2)}, u32[]{:S(2)}) collective-permute-start(f32[1,4,128,128]{3,2,1,0:T(8,128)S(1)} %add.117), channel_id=1, source_target_pairs={{0,4},{2,6},{4,8},{6,10},{8,12},{10,14},{12,16},{14,18},{16,20},{1... | collective-permute-start | bytes 786440 | tf_op jit(solution)/shard_map/ppermute | solution.py:27
  125.3 4.6 %collective-permute-done.2 = f32[1,4,128,128]{3,2,1,0:T(8,128)S(1)} collective-permute-done((f32[1,4,128,128]{3,2,1,0:T(8,128)S(1)}, f32[1,4,128,128]{3,2,1,0:T(8,128)S(1)}, u32[]{:S(2)}, u32[]{:S(2)}) %collective-permute-start.2) | collective-permute-done | bytes 262176 | tf_op jit(solution)/shard_map/ppermute | solution.py:27
  130.6 13.6 %collective-permute-start.3 = (f32[1,4,128,128]{3,2,1,0:T(8,128)}, f32[1,4,128,128]{3,2,1,0:T(8,128)}, u32[]{:S(2)}, u32[]{:S(2)}) collective-permute-start(f32[1,4,128,128]{3,2,1,0:T(8,128)} %add.118), channel_id=1, source_target_pairs={{0,8},{2,10},{4,12},{6,14},{8,16},{10,18},{12,20},{14,22},{16,24},... | collective-permute-start | bytes 786440 | tf_op jit(solution)/shard_map/ppermute | solution.py:27
  145.7 3.2 collective-permute-done.3
  148.9 1.8 add.119
  150.7 5.8 %collective-permute-start.4 = (f32[1,4,128,128]{3,2,1,0:T(8,128)}, f32[1,4,128,128]{3,2,1,0:T(8,128)}, u32[]{:S(2)}, u32[]{:S(2)}) collective-permute-start(f32[1,4,128,128]{3,2,1,0:T(8,128)} %add.119), channel_id=1, source_target_pairs={{0,16},{2,18},{4,20},{6,22},{8,24},{10,26},{12,28},{14,30},{1,17},... | collective-permute-start | bytes 786440 | tf_op jit(solution)/shard_map/ppermute | solution.py:27
  156.5 2.8 convolution_convert_fusion.1
  160.4 2.8 copy.142
  173.4 1.8 fusion.28
  178.5 2.6 multiply_convert_fusion.1
  181.1 2.3 reshape.262
  183.3 1.8 fusion.27
  186.9 2.5 multiply_convert_fusion
  189.4 2.3 reshape.264
  191.7 3.9 %copy_bitcast_fusion = bf16[16,64,1024]{2,1,0:T(8,128)(2,1)} fusion(bf16[8,16,4,1024]{3,2,1,0:T(4,128)(2,1)} %reshape.264, bf16[8,16,4,1024]{3,2,1,0:T(4,128)(2,1)} %reshape.262), kind=kLoop, calls=%fused_computation.2 | loop fusion | flops 4194304 | bytes 4194304 | tf_op jit(solution)/shard_map/convert_element_type | solution.py:87
  195.5 4.4 %all-to-all-start.1 = ((bf16[16,64,1024]{2,1,0:T(8,128)(2,1)}), bf16[16,64,1024]{2,1,0:T(8,128)(2,1)}, u32[]{:S(2)}, u32[]{:S(2)}) async-start(bf16[16,64,1024]{2,1,0:T(8,128)(2,1)} %copy_bitcast_fusion), calls=%async_computation.1 | async-start | bytes 4194304 | tf_op jit(solution)/shard_map/all_to_all | solution.py:86
  202.4 36.4 %collective-permute-done.7 = f32[1,4,128,128]{3,2,1,0:T(8,128)S(1)} collective-permute-done((f32[1,4,128,128]{3,2,1,0:T(8,128)S(1)}, f32[1,4,128,128]{3,2,1,0:T(8,128)S(1)}, u32[]{:S(2)}, u32[]{:S(2)}) %collective-permute-start.7) | collective-permute-done | bytes 262176 | tf_op jit(solution)/shard_map/ppermute | solution.py:27
  240.8 1.8 copy.141
  243.7 24.3 %collective-permute-done.8 = f32[1,4,128,128]{3,2,1,0:T(8,128)} collective-permute-done((f32[1,4,128,128]{3,2,1,0:T(8,128)}, f32[1,4,128,128]{3,2,1,0:T(8,128)}, u32[]{:S(2)}, u32[]{:S(2)}) %collective-permute-start.8) | collective-permute-done | bytes 262176 | tf_op jit(solution)/shard_map/ppermute | solution.py:27
  270.3 2.5 fusion.49
  272.9 9.0 %collective-permute-done.9 = f32[1,4,128,128]{3,2,1,0:T(8,128)S(1)} collective-permute-done((f32[1,4,128,128]{3,2,1,0:T(8,128)S(1)}, f32[1,4,128,128]{3,2,1,0:T(8,128)S(1)}, u32[]{:S(2)}, u32[]{:S(2)}) %collective-permute-start.9) | collective-permute-done | bytes 262176 | tf_op jit(solution)/shard_map/ppermute | solution.py:27
  284.6 6.7 %collective-permute-done.10 = f32[1,4,128,128]{3,2,1,0:T(8,128)S(1)} collective-permute-done((f32[1,4,128,128]{3,2,1,0:T(8,128)S(1)}, f32[1,4,128,128]{3,2,1,0:T(8,128)S(1)}, u32[]{:S(2)}, u32[]{:S(2)}) %collective-permute-start.10) | collective-permute-done | bytes 262176 | tf_op jit(solution)/shard_map/ppermute | solution.py:27
  291.4 3.0 collective-permute-start.11
  299.3 2.7 convert_reduce_fusion
  302.0 7.2 %all-to-all-start.2 = ((f32[8,8,1024]{2,1,0:T(8,128)}), f32[8,8,1024]{2,1,0:T(8,128)S(1)}, u32[]{:S(2)}, u32[]{:S(2)}) async-start(f32[8,8,1024]{2,1,0:T(8,128)} %bitcast.52), calls=%async_computation.2 | async-start | bytes 524288 | tf_op jit(solution)/shard_map/all_to_all | solution.py:89
  310.2 9.0 %all-to-all-done.2 = f32[8,8,1024]{2,1,0:T(8,128)S(1)} async-done(((f32[8,8,1024]{2,1,0:T(8,128)}), f32[8,8,1024]{2,1,0:T(8,128)S(1)}, u32[]{:S(2)}, u32[]{:S(2)}) %all-to-all-start.2) | async-done | bytes 262176 | tf_op jit(solution)/shard_map/all_to_all | solution.py:89
  (120 shorter events, 44.3 us)
Async XLA Ops:
  7.2 24.2 %copy-start.15 = (bf16[1,128,1024]{2,1,0:T(8,128)(2,1)S(1)}, bf16[1,128,1024]{2,1,0:T(8,128)(2,1)}, u32[]{:S(2)}) copy-start(bf16[1,128,1024]{2,1,0:T(8,128)(2,1)} %param.9) | copy-start | bytes 786436
  7.2 93.0 %all-gather.2.cloned.1.call-start = ((), (), s32[]{:S(2)}) async-start(), calls=%async_computation.3 | async-start | bytes 8650752 | tf_op jit(solution)/shard_map/all_gather | solution.py:48
  107.8 1.8 copy-start.8
  109.3 2.3 collective-permute-start
  112.6 43.9 %copy-start.4 = (f32[1,4,128,128]{3,2,1,0:T(8,128)}, f32[1,4,128,128]{3,2,1,0:T(8,128)S(1)}, u32[]{:S(2)}) copy-start(f32[1,4,128,128]{3,2,1,0:T(8,128)S(1)} %dynamic-slice_add_fusion.1) | copy-start | bytes 786436
  112.6 8.0 %collective-permute-start.1 = (f32[1,4,128,128]{3,2,1,0:T(8,128)S(1)}, f32[1,4,128,128]{3,2,1,0:T(8,128)S(1)}, u32[]{:S(2)}, u32[]{:S(2)}) collective-permute-start(f32[1,4,128,128]{3,2,1,0:T(8,128)S(1)} %dynamic-slice_add_fusion.1), channel_id=1, source_target_pairs={{0,2},{2,4},{4,6},{6,8},{8,10},{10,12},{12,14},{14,16},{16,18},{18... | collective-permute-start | bytes 786440 | tf_op jit(solution)/shard_map/ppermute | solution.py:27
  120.7 9.1 %collective-permute-start.2 = (f32[1,4,128,128]{3,2,1,0:T(8,128)S(1)}, f32[1,4,128,128]{3,2,1,0:T(8,128)S(1)}, u32[]{:S(2)}, u32[]{:S(2)}) collective-permute-start(f32[1,4,128,128]{3,2,1,0:T(8,128)S(1)} %add.117), channel_id=1, source_target_pairs={{0,4},{2,6},{4,8},{6,10},{8,12},{10,14},{12,16},{14,18},{16,20},{1... | collective-permute-start | bytes 786440 | tf_op jit(solution)/shard_map/ppermute | solution.py:27
  130.6 18.4 %collective-permute-start.3 = (f32[1,4,128,128]{3,2,1,0:T(8,128)}, f32[1,4,128,128]{3,2,1,0:T(8,128)}, u32[]{:S(2)}, u32[]{:S(2)}) collective-permute-start(f32[1,4,128,128]{3,2,1,0:T(8,128)} %add.118), channel_id=1, source_target_pairs={{0,8},{2,10},{4,12},{6,14},{8,16},{10,18},{12,20},{14,22},{16,24},... | collective-permute-start | bytes 786440 | tf_op jit(solution)/shard_map/ppermute | solution.py:27
  144.9 28.4 %collective-permute-start.12 = (bf16[128,1024]{0,1:T(8,128)(2,1)}, bf16[128,1024]{0,1:T(8,128)(2,1)}, u32[]{:S(2)}, u32[]{:S(2)}) collective-permute-start(bf16[128,1024]{0,1:T(8,128)(2,1)} %fusion.87), channel_id=1, source_target_pairs={{0,1},{1,0},{2,3},{3,2},{4,5},{5,4},{6,7},{7,6},{8,9},{9,8},{10,11... | collective-permute-start | bytes 786440 | tf_op jit(solution)/shard_map/ppermute | solution.py:73
  150.7 12.9 %collective-permute-start.4 = (f32[1,4,128,128]{3,2,1,0:T(8,128)}, f32[1,4,128,128]{3,2,1,0:T(8,128)}, u32[]{:S(2)}, u32[]{:S(2)}) collective-permute-start(f32[1,4,128,128]{3,2,1,0:T(8,128)} %add.119), channel_id=1, source_target_pairs={{0,16},{2,18},{4,20},{6,22},{8,24},{10,26},{12,28},{14,30},{1,17},... | collective-permute-start | bytes 786440 | tf_op jit(solution)/shard_map/ppermute | solution.py:27
  160.4 3.1 copy-start.5
  163.6 5.0 %copy-start.11 = (bf16[8,128,128]{2,1,0:T(8,128)(2,1)}, bf16[8,128,128]{2,1,0:T(8,128)(2,1)S(1)}, u32[]{:S(2)}) copy-start(bf16[8,128,128]{2,1,0:T(8,128)(2,1)S(1)} %fusion.2) | copy-start | bytes 786436
  164.8 4.1 %collective-permute-start.5 = (f32[1,4,128,128]{3,2,1,0:T(8,128)S(1)}, f32[1,4,128,128]{3,2,1,0:T(8,128)S(1)}, u32[]{:S(2)}, u32[]{:S(2)}) collective-permute-start(f32[1,4,128,128]{3,2,1,0:T(8,128)S(1)} %add_subtract_fusion.1), channel_id=1, source_target_pairs={{0,1},{1,0},{2,3},{3,2},{4,5},{5,4},{6,7},{7,6},{8,9},{9,8},{10,11... | collective-permute-start | bytes 786440 | tf_op jit(solution)/shard_map/ppermute | solution.py:30
  172.9 5.7 %collective-permute-start.13 = (bf16[128,1024]{0,1:T(8,128)(2,1)}, bf16[128,1024]{0,1:T(8,128)(2,1)}, u32[]{:S(2)}, u32[]{:S(2)}) collective-permute-start(bf16[128,1024]{0,1:T(8,128)(2,1)} %bitcast.30), channel_id=1, source_target_pairs={{0,1},{1,0},{2,3},{3,2},{4,5},{5,4},{6,7},{7,6},{8,9},{9,8},{10,11... | collective-permute-start | bytes 786440 | tf_op jit(solution)/shard_map/ppermute | solution.py:73
  172.9 14.0 %collective-permute-start.15 = (bf16[128,1024]{1,0:T(8,128)(2,1)}, bf16[128,1024]{1,0:T(8,128)(2,1)}, u32[]{:S(2)}, u32[]{:S(2)}) collective-permute-start(bf16[128,1024]{1,0:T(8,128)(2,1)} %bitcast.20), channel_id=1, source_target_pairs={{0,1},{1,0},{2,3},{3,2},{4,5},{5,4},{6,7},{7,6},{8,9},{9,8},{10,11... | collective-permute-start | bytes 786440 | tf_op jit(solution)/shard_map/ppermute | solution.py:73
  176.9 6.4 %collective-permute-start.14 = (bf16[128,1024]{0,1:T(8,128)(2,1)}, bf16[128,1024]{0,1:T(8,128)(2,1)}, u32[]{:S(2)}, u32[]{:S(2)}) collective-permute-start(bf16[128,1024]{0,1:T(8,128)(2,1)} %bitcast.178), channel_id=1, source_target_pairs={{0,1},{1,0},{2,3},{3,2},{4,5},{5,4},{6,7},{7,6},{8,9},{9,8},{10,11... | collective-permute-start | bytes 786440 | tf_op jit(solution)/shard_map/ppermute | solution.py:73
  178.0 22.0 %collective-permute-start.6 = (f32[1,8,128,128]{3,2,1,0:T(8,128)}, f32[1,8,128,128]{3,2,1,0:T(8,128)}, u32[]{:S(2)}, u32[]{:S(2)}) collective-permute-start(f32[1,8,128,128]{3,2,1,0:T(8,128)} %convolution_bitcast_fusion), channel_id=1, source_target_pairs={{0,1},{1,0},{2,3},{3,2},{4,5},{5,4},{6,7},{7,6},{8,9},{9,8},{10,11... | collective-permute-start | bytes 1572872 | tf_op jit(solution)/shard_map/ppermute | solution.py:16
  195.5 103.7 %all-to-all-start.1 = ((bf16[16,64,1024]{2,1,0:T(8,128)(2,1)}), bf16[16,64,1024]{2,1,0:T(8,128)(2,1)}, u32[]{:S(2)}, u32[]{:S(2)}) async-start(bf16[16,64,1024]{2,1,0:T(8,128)(2,1)} %copy_bitcast_fusion), calls=%async_computation.1 | async-start | bytes 4194304 | tf_op jit(solution)/shard_map/all_to_all | solution.py:86
  201.1 37.7 %copy-start.6 = (f32[1,4,128,128]{3,2,1,0:T(8,128)}, f32[1,4,128,128]{3,2,1,0:T(8,128)S(1)}, u32[]{:S(2)}) copy-start(f32[1,4,128,128]{3,2,1,0:T(8,128)S(1)} %dynamic-slice_add_fusion) | copy-start | bytes 786436
  201.1 37.7 %collective-permute-start.7 = (f32[1,4,128,128]{3,2,1,0:T(8,128)S(1)}, f32[1,4,128,128]{3,2,1,0:T(8,128)S(1)}, u32[]{:S(2)}, u32[]{:S(2)}) collective-permute-start(f32[1,4,128,128]{3,2,1,0:T(8,128)S(1)} %dynamic-slice_add_fusion), channel_id=1, source_target_pairs={{2,0},{4,2},{6,4},{8,6},{10,8},{12,10},{14,12},{16,14},{18,16},{20... | collective-permute-start | bytes 786440 | tf_op jit(solution)/shard_map/ppermute | solution.py:27
  239.5 28.5 %collective-permute-start.8 = (f32[1,4,128,128]{3,2,1,0:T(8,128)}, f32[1,4,128,128]{3,2,1,0:T(8,128)}, u32[]{:S(2)}, u32[]{:S(2)}) collective-permute-start(f32[1,4,128,128]{3,2,1,0:T(8,128)} %add.129), channel_id=1, source_target_pairs={{4,0},{6,2},{8,4},{10,6},{12,8},{14,10},{16,12},{18,14},{20,16},{2... | collective-permute-start | bytes 786440 | tf_op jit(solution)/shard_map/ppermute | solution.py:27
  243.7 39.7 %copy-start.2 = (bf16[1,32,32,1024]{3,2,0,1:T(8,128)(2,1)S(1)}, bf16[1,32,32,1024]{3,2,0,1:T(8,128)(2,1)}, u32[]{:S(2)}) copy-start(bf16[1,32,32,1024]{3,2,0,1:T(8,128)(2,1)} %get-tuple-element.24) | copy-start | bytes 6291460
  243.7 39.7 %copy-start.16 = (bf16[1,128,1024]{2,1,0:T(8,128)(2,1)S(1)}, bf16[1,128,1024]{2,1,0:T(8,128)(2,1)}, u32[]{:S(2)}) copy-start(bf16[1,128,1024]{2,1,0:T(8,128)(2,1)} %param.8) | copy-start | bytes 786436
  269.0 12.9 %collective-permute-start.9 = (f32[1,4,128,128]{3,2,1,0:T(8,128)S(1)}, f32[1,4,128,128]{3,2,1,0:T(8,128)S(1)}, u32[]{:S(2)}, u32[]{:S(2)}) collective-permute-start(f32[1,4,128,128]{3,2,1,0:T(8,128)S(1)} %add.130), channel_id=1, source_target_pairs={{8,0},{10,2},{12,4},{14,6},{16,8},{18,10},{20,12},{22,14},{24,16},... | collective-permute-start | bytes 786440 | tf_op jit(solution)/shard_map/ppermute | solution.py:27
  272.9 18.5 %copy-start.7 = (f32[1,4,128,128]{3,2,1,0:T(8,128)S(1)}, f32[1,4,128,128]{3,2,1,0:T(8,128)}, u32[]{:S(2)}) copy-start(f32[1,4,128,128]{3,2,1,0:T(8,128)} %copy-done.6) | copy-start | bytes 786436
  281.9 12.4 %copy-start.12 = (bf16[8,128,128]{2,1,0:T(8,128)(2,1)S(1)}, bf16[8,128,128]{2,1,0:T(8,128)(2,1)}, u32[]{:S(2)}) copy-start(bf16[8,128,128]{2,1,0:T(8,128)(2,1)} %copy-done.11) | copy-start | bytes 786436
  282.0 9.4 %collective-permute-start.10 = (f32[1,4,128,128]{3,2,1,0:T(8,128)S(1)}, f32[1,4,128,128]{3,2,1,0:T(8,128)S(1)}, u32[]{:S(2)}, u32[]{:S(2)}) collective-permute-start(f32[1,4,128,128]{3,2,1,0:T(8,128)S(1)} %add.131), channel_id=1, source_target_pairs={{16,0},{18,2},{20,4},{22,6},{24,8},{26,10},{28,12},{30,14},{17,1},... | collective-permute-start | bytes 786440 | tf_op jit(solution)/shard_map/ppermute | solution.py:27
  283.4 11.2 %copy-start.14 = (bf16[8,128,128]{2,1,0:T(8,128)(2,1)S(1)}, bf16[8,128,128]{2,1,0:T(8,128)(2,1)}, u32[]{:S(2)}) copy-start(bf16[8,128,128]{2,1,0:T(8,128)(2,1)} %copy-done.13) | copy-start | bytes 786436
  291.4 4.1 %collective-permute-start.11 = (f32[1,4,128,128]{3,2,1,0:T(8,128)S(1)}, f32[1,4,128,128]{3,2,1,0:T(8,128)S(1)}, u32[]{:S(2)}, u32[]{:S(2)}) collective-permute-start(f32[1,4,128,128]{3,2,1,0:T(8,128)S(1)} %add_subtract_fusion), channel_id=1, source_target_pairs={{0,1},{1,0},{2,3},{3,2},{4,5},{5,4},{6,7},{7,6},{8,9},{9,8},{10,11... | collective-permute-start | bytes 786440 | tf_op jit(solution)/shard_map/ppermute | solution.py:30
  295.5 1.6 copy-start.1
  299.1 10.1 %copy-start.10 = (bf16[1,128,1024]{1,2,0:T(8,128)(2,1)S(1)}, bf16[1,128,1024]{1,2,0:T(8,128)(2,1)}, u32[]{:S(2)}) copy-start(bf16[1,128,1024]{1,2,0:T(8,128)(2,1)} %copy.141) | copy-start | bytes 786436
  302.0 17.2 %all-to-all-start.2 = ((f32[8,8,1024]{2,1,0:T(8,128)}), f32[8,8,1024]{2,1,0:T(8,128)S(1)}, u32[]{:S(2)}, u32[]{:S(2)}) async-start(f32[8,8,1024]{2,1,0:T(8,128)} %bitcast.52), calls=%async_computation.2 | async-start | bytes 524288 | tf_op jit(solution)/shard_map/all_to_all | solution.py:89
  (4 other events, 4.6 us)
Sparse Core Ops, SparseCore 0:
  31.5 68.7 all-gather.1

commit v12 on v10

--- a/solution.py
+++ b/solution.py
@@ -81,15 +81,11 @@
         )
         blocks.append((factor * made).reshape(outer, chips, -1, width))
     rows = blocks[0].shape[2]
-    stacked = jnp.concatenate(blocks, 2)
-    stacked = jnp.transpose(stacked, (1, 0, 2, 3)).reshape(-1, width)
+    stacked = jnp.concatenate(blocks, 2).reshape(outer * chips, -1, width)
     stacked, _ = lax.optimization_barrier((stacked, wait_for))
     share = lax.all_to_all(
-        stacked.reshape(chips, -1, width).astype(jnp.bfloat16), "cy", 0, 0, tiled=False
+        stacked.astype(jnp.bfloat16), ("dp", "cy"), 0, 0, tiled=False
     ).astype(jnp.float32).sum(0)
-    share = lax.all_to_all(
-        share.reshape(outer, -1, width), "dp", 0, 0, tiled=False
-    ).sum(0)
     return tuple(share[index * rows : (index + 1) * rows] for index in range(len(pairs)))
 
 

time: 326 us -> 312 us (0.957)
  waiting for transfers between devices: 166 us -> 154 us
    all_to_all x2 -> x1, waiting for transfers between devices: 52.6 us -> 40.1 us  [weight_grads(): lax.all_to_all(stacked.astype(jnp.bfloat16), ('dp', 'cy'), 0, 0, tiled=Fa...]
    reshape x2 -> x0, local copies, waits for them, and re-layouts: 4.52 us -> none  [weight_grads(): blocks.append((factor * made).reshape(outer, chips, -1, width))]
    all_to_all x2 -> x1, starting transfers between devices: 11.4 us -> 10.5 us  [weight_grads(): lax.all_to_all(stacked.astype(jnp.bfloat16), ('dp', 'cy'), 0, 0, tiled=Fa...]
  transfers between devices with their start and end apart: 19 -> 18, of which waited for: 12 -> 11; matrix products, arithmetic and copies ran while one was open for 15% -> 16% of each run, Pallas kernels for 0% -> 0%
where the time goes in v12:
time: 312 us; the launch traced here: 311 us
  waiting for transfers between devices  154 us (49%)
  starting transfers between devices  47.9 us (15%)
  local copies, waits for them, and re-layouts  28.1 us (9%)
  other arithmetic  23 us (7%)
  matrix products  22 us (7%)
  blocking collectives  21.3 us (7%)
  between operations  14.6 us (5%)
    all_gather x1, waiting for transfers between devices, gather_rows(): gathered = lax.all_gather(across, CTX, axis=1, tiled=False)  67.8 us
    ppermute x8, waiting for transfers between devices, state_sum(): total = total + lax.ppermute(total, 'cy', pairs)  42 us
    all_to_all x1, waiting for transfers between devices, weight_grads(): lax.all_to_all(stacked.astype(jnp.bfloat16), ('dp', 'cy'), 0, 0, tiled=Fa...  40.1 us
    ppermute x8, starting transfers between devices, state_sum(): total = total + lax.ppermute(total, 'cy', pairs)  32 us
    all_to_all x1, blocking collectives, gather_rows(): across = lax.all_to_all(copies, 'dp', 0, 0, tiled=False)  21.3 us
    unnamed x47, local copies, waits for them, and re-layouts  10.8 us
    all_to_all x1, starting transfers between devices, weight_grads(): lax.all_to_all(stacked.astype(jnp.bfloat16), ('dp', 'cy'), 0, 0, tiled=Fa...  10.5 us
  transfers between devices with their start and end apart: 18, of which 11 were waited for; matrix products, arithmetic and copies ran while one was open for 16% of the time, Pallas kernels for 0%

profile of v12, /device:TPU:1, one launch (start us, length us, event | category | flops | bytes accessed | tf_op | source)
XLA Modules:
  0.0 310.8 jit_solution(15469889981741537728)
XLA Ops:
  8.8 21.3 %all_to_all.10 = bf16[8,16,1024]{2,1,0:T(8,128)(2,1)S(1)} all-to-all(bf16[8,16,1024]{2,1,0:T(8,128)(2,1)S(1)} %broadcast_in_dim.38), channel_id=1, replica_groups=mesh['dp'=8,'cy'=16,'core'=2] {'dp'}, dimensions={0} | all-to-all | bytes 524288 | tf_op jit(solution)/shard_map/all_to_all | solution.py:45
  32.5 67.8 %all-gather.2.cloned.1.call-done = bf16[4,32,32,1024]{3,2,0,1:T(8,128)(2,1)} async-done(((bf16[4,1,32,1024]{3,2,0,1:T(8,128)(2,1)}), bf16[4,32,32,1024]{3,2,0,1:T(8,128)(2,1)}) %all-gather.2.cloned.1.call-update) | async-done | bytes 8388624 | tf_op jit(solution)/shard_map/all_gather | solution.py:48
  100.2 5.4 %slice_bitcast_fusion = (bf16[1,32,32,1024]{3,2,1,0:T(8,128)(2,1)}, bf16[1,32,32,1024]{3,2,0,1:T(8,128)(2,1)S(1)}, bf16[1,32,32,1024]{3,2,0,1:T(8,128)(2,1)}, bf...) fusion(bf16[4,32,32,1024]{3,2,0,1:T(8,128)(2,1)} %all-gather.2.cloned.1.call-done), kind=kLoop, calls=%fused_computation.97 | loop fusion | bytes 18874368
  109.6 2.0 collective-permute-done
  112.6 2.7 collective-permute-start.1
  115.3 5.3 %collective-permute-done.1 = f32[1,4,128,128]{3,2,1,0:T(8,128)S(1)} collective-permute-done((f32[1,4,128,128]{3,2,1,0:T(8,128)S(1)}, f32[1,4,128,128]{3,2,1,0:T(8,128)S(1)}, u32[]{:S(2)}, u32[]{:S(2)}) %collective-permute-start.1) | collective-permute-done | bytes 262176 | tf_op jit(solution)/shard_map/ppermute | solution.py:27
  120.7 4.5 %collective-permute-start.2 = (f32[1,4,128,128]{3,2,1,0:T(8,128)S(1)}, f32[1,4,128,128]{3,2,1,0:T(8,128)S(1)}, u32[]{:S(2)}, u32[]{:S(2)}) collective-permute-start(f32[1,4,128,128]{3,2,1,0:T(8,128)S(1)} %add.117), channel_id=1, source_target_pairs={{0,4},{2,6},{4,8},{6,10},{8,12},{10,14},{12,16},{14,18},{16,20},{1... | collective-permute-start | bytes 786440 | tf_op jit(solution)/shard_map/ppermute | solution.py:27
  125.2 4.6 %collective-permute-done.2 = f32[1,4,128,128]{3,2,1,0:T(8,128)S(1)} collective-permute-done((f32[1,4,128,128]{3,2,1,0:T(8,128)S(1)}, f32[1,4,128,128]{3,2,1,0:T(8,128)S(1)}, u32[]{:S(2)}, u32[]{:S(2)}) %collective-permute-start.2) | collective-permute-done | bytes 262176 | tf_op jit(solution)/shard_map/ppermute | solution.py:27
  130.5 13.7 %collective-permute-start.3 = (f32[1,4,128,128]{3,2,1,0:T(8,128)}, f32[1,4,128,128]{3,2,1,0:T(8,128)}, u32[]{:S(2)}, u32[]{:S(2)}) collective-permute-start(f32[1,4,128,128]{3,2,1,0:T(8,128)} %add.118), channel_id=1, source_target_pairs={{0,8},{2,10},{4,12},{6,14},{8,16},{10,18},{12,20},{14,22},{16,24},... | collective-permute-start | bytes 786440 | tf_op jit(solution)/shard_map/ppermute | solution.py:27
  144.2 4.8 %collective-permute-done.3 = f32[1,4,128,128]{3,2,1,0:T(8,128)} collective-permute-done((f32[1,4,128,128]{3,2,1,0:T(8,128)}, f32[1,4,128,128]{3,2,1,0:T(8,128)}, u32[]{:S(2)}, u32[]{:S(2)}) %collective-permute-start.3) | collective-permute-done | bytes 262176 | tf_op jit(solution)/shard_map/ppermute | solution.py:27
  148.9 1.8 add.119
  150.8 5.8 %collective-permute-start.4 = (f32[1,4,128,128]{3,2,1,0:T(8,128)}, f32[1,4,128,128]{3,2,1,0:T(8,128)}, u32[]{:S(2)}, u32[]{:S(2)}) collective-permute-start(f32[1,4,128,128]{3,2,1,0:T(8,128)} %add.119), channel_id=1, source_target_pairs={{0,16},{2,18},{4,20},{6,22},{8,24},{10,26},{12,28},{14,30},{1,17},... | collective-permute-start | bytes 786440 | tf_op jit(solution)/shard_map/ppermute | solution.py:27
  156.6 2.8 convolution_convert_fusion.1
  160.5 2.8 copy.103
  171.7 1.9 collective-permute-done.6
  175.8 7.4 %collective-permute-done.7 = f32[1,4,128,128]{3,2,1,0:T(8,128)S(1)} collective-permute-done((f32[1,4,128,128]{3,2,1,0:T(8,128)S(1)}, f32[1,4,128,128]{3,2,1,0:T(8,128)S(1)}, u32[]{:S(2)}, u32[]{:S(2)}) %collective-permute-start.7) | collective-permute-done | bytes 262176 | tf_op jit(solution)/shard_map/ppermute | solution.py:27
  185.4 14.2 %collective-permute-done.8 = f32[1,4,128,128]{3,2,1,0:T(8,128)S(1)} collective-permute-done((f32[1,4,128,128]{3,2,1,0:T(8,128)S(1)}, f32[1,4,128,128]{3,2,1,0:T(8,128)S(1)}, u32[]{:S(2)}, u32[]{:S(2)}) %collective-permute-start.8) | collective-permute-done | bytes 262176 | tf_op jit(solution)/shard_map/ppermute | solution.py:27
  207.0 2.9 collective-permute-done.9
  213.0 2.6 convolution_multiply_fusion.1
  215.5 1.8 fusion.27
  219.1 2.8 collective-permute-done.10
  221.9 1.8 add_subtract_fusion
  223.7 2.2 collective-permute-start.11
  225.9 2.5 convolution_multiply_fusion
  228.4 2.3 concatenate.46
  230.7 2.2 concatenate.51
  232.9 3.9 %pad_maximum_fusion = bf16[128,8,1024]{2,1,0:T(8,128)(2,1)} fusion(bf16[128,4,1024]{2,1,0:T(4,128)(2,1)} %concatenate.51, bf16[128,4,1024]{2,1,0:T(4,128)(2,1)} %concatenate.46), kind=kLoop, calls=%fused_computation | loop fusion | flops 4194304 | bytes 4194304 | tf_op jit(solution)/shard_map/concatenate | solution.py:84
  238.0 10.5 %all-to-all-start.1 = ((bf16[128,8,1024]{2,1,0:T(8,128)(2,1)}), bf16[128,8,1024]{2,1,0:T(8,128)(2,1)}, u32[]{:S(2)}, u32[]{:S(2)}) async-start(bf16[128,8,1024]{2,1,0:T(8,128)(2,1)} %pad_maximum_fusion), calls=%async_computation.1 | async-start | bytes 4194304 | tf_op jit(solution)/shard_map/all_to_all | solution.py:86
  248.4 1.8 copy.102
  253.9 1.8 fusion.50
  261.3 40.1 %all-to-all-done.1 = bf16[128,8,1024]{2,1,0:T(8,128)(2,1)} async-done(((bf16[128,8,1024]{2,1,0:T(8,128)(2,1)}), bf16[128,8,1024]{2,1,0:T(8,128)(2,1)}, u32[]{:S(2)}, u32[]{:S(2)}) %all-to-all-start.1) | async-done | bytes 2097184 | tf_op jit(solution)/shard_map/all_to_all | solution.py:86
  301.4 2.0 convert_reduce_fusion
  (125 shorter events, 46.3 us)
Async XLA Ops:
  7.2 24.2 %copy-start.19 = (bf16[1,128,1024]{2,1,0:T(8,128)(2,1)S(1)}, bf16[1,128,1024]{2,1,0:T(8,128)(2,1)}, u32[]{:S(2)}) copy-start(bf16[1,128,1024]{2,1,0:T(8,128)(2,1)} %param.9) | copy-start | bytes 786436
  7.2 93.0 %all-gather.2.cloned.1.call-start = ((), (), s32[]{:S(2)}) async-start(), calls=%async_computation.2 | async-start | bytes 8650752 | tf_op jit(solution)/shard_map/all_gather | solution.py:48
  107.5 55.8 %copy-start.4 = (bf16[128,1024]{1,0:T(8,128)(2,1)}, bf16[128,1024]{1,0:T(8,128)(2,1)S(1)}, u32[]{:S(2)}) copy-start(bf16[128,1024]{1,0:T(8,128)(2,1)S(1)} %convolution_convert_fusion) | copy-start | bytes 786436
  109.3 2.3 collective-permute-start
  112.6 44.0 %copy-start.10 = (f32[1,4,128,128]{3,2,1,0:T(8,128)}, f32[1,4,128,128]{3,2,1,0:T(8,128)S(1)}, u32[]{:S(2)}) copy-start(f32[1,4,128,128]{3,2,1,0:T(8,128)S(1)} %dynamic-slice_add_fusion.1) | copy-start | bytes 786436
  112.6 8.0 %collective-permute-start.1 = (f32[1,4,128,128]{3,2,1,0:T(8,128)S(1)}, f32[1,4,128,128]{3,2,1,0:T(8,128)S(1)}, u32[]{:S(2)}, u32[]{:S(2)}) collective-permute-start(f32[1,4,128,128]{3,2,1,0:T(8,128)S(1)} %dynamic-slice_add_fusion.1), channel_id=1, source_target_pairs={{0,2},{2,4},{4,6},{6,8},{8,10},{10,12},{12,14},{14,16},{16,18},{18... | collective-permute-start | bytes 786440 | tf_op jit(solution)/shard_map/ppermute | solution.py:27
  120.7 9.1 %collective-permute-start.2 = (f32[1,4,128,128]{3,2,1,0:T(8,128)S(1)}, f32[1,4,128,128]{3,2,1,0:T(8,128)S(1)}, u32[]{:S(2)}, u32[]{:S(2)}) collective-permute-start(f32[1,4,128,128]{3,2,1,0:T(8,128)S(1)} %add.117), channel_id=1, source_target_pairs={{0,4},{2,6},{4,8},{6,10},{8,12},{10,14},{12,16},{14,18},{16,20},{1... | collective-permute-start | bytes 786440 | tf_op jit(solution)/shard_map/ppermute | solution.py:27
  130.5 18.4 %collective-permute-start.3 = (f32[1,4,128,128]{3,2,1,0:T(8,128)}, f32[1,4,128,128]{3,2,1,0:T(8,128)}, u32[]{:S(2)}, u32[]{:S(2)}) collective-permute-start(f32[1,4,128,128]{3,2,1,0:T(8,128)} %add.118), channel_id=1, source_target_pairs={{0,8},{2,10},{4,12},{6,14},{8,16},{10,18},{12,20},{14,22},{16,24},... | collective-permute-start | bytes 786440 | tf_op jit(solution)/shard_map/ppermute | solution.py:27
  150.8 12.9 %collective-permute-start.4 = (f32[1,4,128,128]{3,2,1,0:T(8,128)}, f32[1,4,128,128]{3,2,1,0:T(8,128)}, u32[]{:S(2)}, u32[]{:S(2)}) collective-permute-start(f32[1,4,128,128]{3,2,1,0:T(8,128)} %add.119), channel_id=1, source_target_pairs={{0,16},{2,18},{4,20},{6,22},{8,24},{10,26},{12,28},{14,30},{1,17},... | collective-permute-start | bytes 786440 | tf_op jit(solution)/shard_map/ppermute | solution.py:27
  163.6 4.9 %copy-start.17 = (bf16[8,128,128]{2,1,0:T(8,128)(2,1)}, bf16[8,128,128]{2,1,0:T(8,128)(2,1)S(1)}, u32[]{:S(2)}) copy-start(bf16[8,128,128]{2,1,0:T(8,128)(2,1)S(1)} %fusion.2) | copy-start | bytes 786436
  164.8 4.1 %collective-permute-start.5 = (f32[1,4,128,128]{3,2,1,0:T(8,128)S(1)}, f32[1,4,128,128]{3,2,1,0:T(8,128)S(1)}, u32[]{:S(2)}, u32[]{:S(2)}) collective-permute-start(f32[1,4,128,128]{3,2,1,0:T(8,128)S(1)} %add_subtract_fusion.1), channel_id=1, source_target_pairs={{0,1},{1,0},{2,3},{3,2},{4,5},{5,4},{6,7},{7,6},{8,9},{9,8},{10,11... | collective-permute-start | bytes 786440 | tf_op jit(solution)/shard_map/ppermute | solution.py:30
  171.3 13.8 %copy-start.13 = (bf16[128,8,128]{0,2,1:T(8,128)(2,1)S(1)}, bf16[128,8,128]{0,2,1:T(8,128)(2,1)}, u32[]{:S(2)}) copy-start(bf16[128,8,128]{0,2,1:T(8,128)(2,1)} %copy-done.12) | copy-start | bytes 786436
  171.6 2.0 collective-permute-start.6
  173.6 9.7 %copy-start.14 = (f32[1,8,128,128]{3,2,1,0:T(8,128)}, f32[1,8,128,128]{3,2,1,0:T(8,128)S(1)}, u32[]{:S(2)}) copy-start(f32[1,8,128,128]{3,2,1,0:T(8,128)S(1)} %collective-permute-done.6) | copy-start | bytes 1572868
  173.6 9.6 %copy-start.8 = (f32[1,4,128,128]{3,2,1,0:T(8,128)}, f32[1,4,128,128]{3,2,1,0:T(8,128)S(1)}, u32[]{:S(2)}) copy-start(f32[1,4,128,128]{3,2,1,0:T(8,128)S(1)} %dynamic-slice_add_fusion) | copy-start | bytes 786436
  173.6 9.6 %collective-permute-start.7 = (f32[1,4,128,128]{3,2,1,0:T(8,128)S(1)}, f32[1,4,128,128]{3,2,1,0:T(8,128)S(1)}, u32[]{:S(2)}, u32[]{:S(2)}) collective-permute-start(f32[1,4,128,128]{3,2,1,0:T(8,128)S(1)} %dynamic-slice_add_fusion), channel_id=1, source_target_pairs={{2,0},{4,2},{6,4},{8,6},{10,8},{12,10},{14,12},{16,14},{18,16},{20... | collective-permute-start | bytes 786440 | tf_op jit(solution)/shard_map/ppermute | solution.py:27
  175.7 27.9 %collective-permute-start.12 = (bf16[128,1024]{0,1:T(8,128)(2,1)}, bf16[128,1024]{0,1:T(8,128)(2,1)}, u32[]{:S(2)}, u32[]{:S(2)}) collective-permute-start(bf16[128,1024]{0,1:T(8,128)(2,1)} %fusion.86), channel_id=1, source_target_pairs={{0,1},{1,0},{2,3},{3,2},{4,5},{5,4},{6,7},{7,6},{8,9},{9,8},{10,11... | collective-permute-start | bytes 786440 | tf_op jit(solution)/shard_map/ppermute | solution.py:73
  183.3 20.3 %copy-start.7 = (bf16[1,128,1024]{1,2,0:T(8,128)(2,1)S(1)}, bf16[1,128,1024]{1,2,0:T(8,128)(2,1)}, u32[]{:S(2)}) copy-start(bf16[1,128,1024]{1,2,0:T(8,128)(2,1)} %copy-done.6) | copy-start | bytes 786436
  183.3 16.3 %collective-permute-start.8 = (f32[1,4,128,128]{3,2,1,0:T(8,128)S(1)}, f32[1,4,128,128]{3,2,1,0:T(8,128)S(1)}, u32[]{:S(2)}, u32[]{:S(2)}) collective-permute-start(f32[1,4,128,128]{3,2,1,0:T(8,128)S(1)} %add.129), channel_id=1, source_target_pairs={{4,0},{6,2},{8,4},{10,6},{12,8},{14,10},{16,12},{18,14},{20,16},{2... | collective-permute-start | bytes 786440 | tf_op jit(solution)/shard_map/ppermute | solution.py:27
  185.1 17.5 %copy-start.18 = (bf16[8,128,128]{2,1,0:T(8,128)(2,1)}, bf16[8,128,128]{2,1,0:T(8,128)(2,1)S(1)}, u32[]{:S(2)}) copy-start(bf16[8,128,128]{2,1,0:T(8,128)(2,1)S(1)} %fusion.3) | copy-start | bytes 786436
  200.3 9.6 %collective-permute-start.9 = (f32[1,4,128,128]{3,2,1,0:T(8,128)}, f32[1,4,128,128]{3,2,1,0:T(8,128)}, u32[]{:S(2)}, u32[]{:S(2)}) collective-permute-start(f32[1,4,128,128]{3,2,1,0:T(8,128)} %add.130), channel_id=1, source_target_pairs={{8,0},{10,2},{12,4},{14,6},{16,8},{18,10},{20,12},{22,14},{24,16},... | collective-permute-start | bytes 786440 | tf_op jit(solution)/shard_map/ppermute | solution.py:27
  202.6 10.4 %collective-permute-start.13 = (bf16[128,1024]{0,1:T(8,128)(2,1)}, bf16[128,1024]{0,1:T(8,128)(2,1)}, u32[]{:S(2)}, u32[]{:S(2)}) collective-permute-start(bf16[128,1024]{0,1:T(8,128)(2,1)} %bitcast.30), channel_id=1, source_target_pairs={{0,1},{1,0},{2,3},{3,2},{4,5},{5,4},{6,7},{7,6},{8,9},{9,8},{10,11... | collective-permute-start | bytes 786440 | tf_op jit(solution)/shard_map/ppermute | solution.py:73
  203.1 22.8 %collective-permute-start.15 = (bf16[128,1024]{1,0:T(8,128)(2,1)}, bf16[128,1024]{1,0:T(8,128)(2,1)}, u32[]{:S(2)}, u32[]{:S(2)}) collective-permute-start(bf16[128,1024]{1,0:T(8,128)(2,1)} %bitcast.20), channel_id=1, source_target_pairs={{0,1},{1,0},{2,3},{3,2},{4,5},{5,4},{6,7},{7,6},{8,9},{9,8},{10,11... | collective-permute-start | bytes 786440 | tf_op jit(solution)/shard_map/ppermute | solution.py:73
  203.1 12.5 %collective-permute-start.14 = (bf16[128,1024]{0,1:T(8,128)(2,1)}, bf16[128,1024]{0,1:T(8,128)(2,1)}, u32[]{:S(2)}, u32[]{:S(2)}) collective-permute-start(bf16[128,1024]{0,1:T(8,128)(2,1)} %bitcast.174), channel_id=1, source_target_pairs={{0,1},{1,0},{2,3},{3,2},{4,5},{5,4},{6,7},{7,6},{8,9},{9,8},{10,11... | collective-permute-start | bytes 786440 | tf_op jit(solution)/shard_map/ppermute | solution.py:73
  207.0 14.9 %copy-start.9 = (f32[1,4,128,128]{3,2,1,0:T(8,128)S(1)}, f32[1,4,128,128]{3,2,1,0:T(8,128)}, u32[]{:S(2)}) copy-start(f32[1,4,128,128]{3,2,1,0:T(8,128)} %copy-done.8) | copy-start | bytes 786436
  211.7 10.2 %collective-permute-start.10 = (f32[1,4,128,128]{3,2,1,0:T(8,128)}, f32[1,4,128,128]{3,2,1,0:T(8,128)}, u32[]{:S(2)}, u32[]{:S(2)}) collective-permute-start(f32[1,4,128,128]{3,2,1,0:T(8,128)} %add.131), channel_id=1, source_target_pairs={{16,0},{18,2},{20,4},{22,6},{24,8},{26,10},{28,12},{30,14},{17,1},... | collective-permute-start | bytes 786440 | tf_op jit(solution)/shard_map/ppermute | solution.py:27
  223.7 13.2 %collective-permute-start.11 = (f32[1,4,128,128]{3,2,1,0:T(8,128)}, f32[1,4,128,128]{3,2,1,0:T(8,128)S(1)}, u32[]{:S(2)}, u32[]{:S(2)}) collective-permute-start(f32[1,4,128,128]{3,2,1,0:T(8,128)} %add_subtract_fusion), channel_id=1, source_target_pairs={{0,1},{1,0},{2,3},{3,2},{4,5},{5,4},{6,7},{7,6},{8,9},{9,8},{10,11... | collective-permute-start | bytes 786440 | tf_op jit(solution)/shard_map/ppermute | solution.py:30
  232.9 5.0 %copy-start.15 = (f32[1,8,128,128]{3,2,1,0:T(8,128)S(1)}, f32[1,8,128,128]{3,2,1,0:T(8,128)}, u32[]{:S(2)}) copy-start(f32[1,8,128,128]{3,2,1,0:T(8,128)} %copy-done.14) | copy-start | bytes 1572868
  238.0 63.4 %all-to-all-start.1 = ((bf16[128,8,1024]{2,1,0:T(8,128)(2,1)}), bf16[128,8,1024]{2,1,0:T(8,128)(2,1)}, u32[]{:S(2)}, u32[]{:S(2)}) async-start(bf16[128,8,1024]{2,1,0:T(8,128)(2,1)} %pad_maximum_fusion), calls=%async_computation.1 | async-start | bytes 4194304 | tf_op jit(solution)/shard_map/all_to_all | solution.py:86
  250.2 3.7 %copy-start.2 = (bf16[1,32,32,1024]{3,2,0,1:T(8,128)(2,1)S(1)}, bf16[1,32,32,1024]{3,2,0,1:T(8,128)(2,1)}, u32[]{:S(2)}) copy-start(bf16[1,32,32,1024]{3,2,0,1:T(8,128)(2,1)} %get-tuple-element.20) | copy-start | bytes 6291460
  252.6 3.2 %copy-start.3 = (bf16[1,32,32,1024]{3,2,0,1:T(8,128)(2,1)S(1)}, bf16[1,32,32,1024]{3,2,0,1:T(8,128)(2,1)}, u32[]{:S(2)}) copy-start(bf16[1,32,32,1024]{3,2,0,1:T(8,128)(2,1)} %get-tuple-element.22) | copy-start | bytes 6291460
  252.6 3.2 %copy-start.20 = (bf16[1,128,1024]{2,1,0:T(8,128)(2,1)S(1)}, bf16[1,128,1024]{2,1,0:T(8,128)(2,1)}, u32[]{:S(2)}) copy-start(bf16[1,128,1024]{2,1,0:T(8,128)(2,1)} %param.8) | copy-start | bytes 786436
  (7 other events, 11.0 us)
Sparse Core Ops, SparseCore 0:
  31.5 68.7 all-gather.1
